TPU v7x, 512 devices: a whole 4x8x8 slice. The times are simulated.
512 devices in a mesh: rows: 64 (over y, z), cols: 8 (over x, core).
Axes of the slice: x: 4, y: 8, z: 8, core: 2. Of those that a mesh axis runs over, the one named last changes fastest.
Arguments:
- queries: bfloat16 [32768, 128], P('rows'), may hold values from -1 to 1
- prototypes: bfloat16 [16384, 128], P('cols'), may hold values from -1 to 1
- potential: float32 [16384], P('cols'), may hold values from -0.15 to 0.15
- weights: int32 [32768], P('rows'), may hold values from 1 to 10, as said below
- capacity: int32 [16384], P('cols'), may hold values from 1 to 7, as said below
- cotangent: bfloat16 [32768, 128], P('rows'), may hold values from -16 to 16
Outputs:
- grad_queries: float32 [32768, 128], P(('rows', 'cols'))
- grad_protos: float32 [16384, 128], P('cols')
Inputs may be any that keep to these rules, and one draw needn't show every extreme that they name: weights rise along the queries: the first quarter are all 1, the k-th quarter (k = 0..3) lies in 1 + k to 1 + 3 k. `capacity`: capacities rise along the slots: the k-th quarter (k = 0..3) lies in 1 + k to 1 + 2 k.
All inputs are finite; a program needn't handle non-finite values.
Results may differ from a plain program's by a relative error of at most 0.0019.
The roundings to bfloat16 on the way count: a program that leaves them out, or rounds other values in their place, can miss the bound.
Values sent between devices are 32-bit elements; how exact they have to be, the bound alone decides.
No kernel may reach another device: no remote copies, remote signals or barrier semaphores. Data moves between devices by JAX's collectives and lax.ppermute only.
A program may use at most 64 MiB of HBM per device.

v0:
```python
import math

import jax
import jax.numpy as jnp
from jax import lax
from jax.sharding import PartitionSpec as P

TEMPER = 0.05


def unit_rows(matrix):
    wide = matrix.astype(jnp.float32)
    length = jnp.sqrt(jnp.sum(wide * wide, axis=1) + 1e-06)
    return ((wide / length[:, None]).astype(jnp.bfloat16), length)


def unit_back(grad, unit, length):
    wide = unit.astype(jnp.float32)
    along = jnp.sum(wide * grad, axis=1, keepdims=True)
    return (grad - wide * along) / length[:, None]


def pair_dot(left, right):
    return lax.dot_general(
        left, right, (((1,), (1,)), ((), ())), preferred_element_type=jnp.float32
    )


def across_slots(stack):
    return lax.psum(stack, "cols")


def across_queries(stack):
    return lax.psum(stack, "rows")


def local(queries, prototypes, potential, weights, capacity, cotangent):
    qhat, qlen = unit_rows(queries)
    phat, plen = unit_rows(prototypes)
    wgt = weights.astype(jnp.float32)
    scaled = (cotangent.astype(jnp.float32) / wgt[:, None]).astype(jnp.bfloat16)
    local_rows = qhat.shape[0]
    slots = phat.shape[0]
    width = math.gcd(slots, 512)
    starts = list(range(0, slots, width))

    def kernel_tile(start):
        scores = pair_dot(qhat, phat[start : start + width])
        weight_cols = capacity[start : start + width].astype(jnp.float32)
        return weight_cols[None, :] * jnp.exp(
            (scores - potential[start : start + width][None, :]) / TEMPER
        )

    def coupling_tile(start):
        return pair_dot(scaled, phat[start : start + width])

    ztot = jnp.zeros((local_rows,), jnp.float32)
    kgsum = jnp.zeros((local_rows,), jnp.float32)
    for start in starts:
        kern = kernel_tile(start)
        ztot = ztot + jnp.sum(kern, axis=1)
        kgsum = kgsum + jnp.sum(kern * coupling_tile(start), axis=1)
    totals = across_slots(jnp.stack([ztot, kgsum]))
    share = wgt / totals[0]
    pvec = share * totals[1]
    alpha_one = pvec / wgt
    col_parts, q_parts, t_parts = ([], [], [])
    for start in starts:
        plan = share[:, None] * kernel_tile(start)
        col_parts.append(jnp.sum(plan, axis=0))
        q_parts.append(jnp.sum(plan * coupling_tile(start), axis=0))
    summed = across_queries(jnp.stack([jnp.concatenate(col_parts), jnp.concatenate(q_parts)]))
    colsum, qvec = (summed[0], summed[1])
    for start in starts:
        plan = share[:, None] * kernel_tile(start)
        t_parts.append(jnp.sum(alpha_one[:, None] * plan, axis=0))
    t_one = across_queries(jnp.concatenate(t_parts)[None, :])[0]
    beta_one = (qvec - t_one) / colsum
    rowprod = jnp.zeros((local_rows,), jnp.float32)
    for start in starts:
        plan = share[:, None] * kernel_tile(start)
        rowprod = rowprod + jnp.sum(plan * beta_one[start : start + width][None, :], axis=1)
    rowprod = across_slots(rowprod[None, :])[0]
    alpha_two = (pvec - rowprod) / wgt
    t_parts = []
    for start in starts:
        plan = share[:, None] * kernel_tile(start)
        t_parts.append(jnp.sum(alpha_two[:, None] * plan, axis=0))
    t_two = across_queries(jnp.concatenate(t_parts)[None, :])[0]
    beta_two = (qvec - t_two) / colsum
    dqhat = jnp.zeros(qhat.shape, jnp.float32)
    dp_parts = []
    for start in starts:
        plan = share[:, None] * kernel_tile(start)
        coupling = coupling_tile(start)
        shift_cols = beta_two[start : start + width][None, :]
        dscore = (plan * (coupling - alpha_two[:, None] - shift_cols) / TEMPER).astype(jnp.bfloat16)
        planb = plan.astype(jnp.bfloat16)
        dqhat = dqhat + jnp.dot(
            dscore, phat[start : start + width], preferred_element_type=jnp.float32
        )
        part = lax.dot_general(
            dscore, qhat, (((0,), (0,)), ((), ())), preferred_element_type=jnp.float32
        )
        part = part + lax.dot_general(
            planb, scaled, (((0,), (0,)), ((), ())), preferred_element_type=jnp.float32
        )
        dp_parts.append(part)
    dphat = jnp.concatenate(dp_parts, axis=0)
    query_part = lax.psum_scatter(dqhat, "cols", scatter_dimension=0, tiled=True)
    piece = query_part.shape[0]
    begin = lax.axis_index("cols") * piece
    grad_queries = unit_back(
        query_part,
        lax.dynamic_slice_in_dim(qhat, begin, piece, 0),
        lax.dynamic_slice_in_dim(qlen, begin, piece, 0),
    )
    whole = lax.psum(dphat, "rows")
    grad_protos = unit_back(whole, phat, plen)
    return (grad_queries, grad_protos)


def solution(mesh):
    in_specs = (P("rows", None), P("cols", None), P("cols"), P("rows"), P("cols"), P("rows", None))
    out_specs = (P(("rows", "cols"), None), P("cols", None))
    return jax.shard_map(local, mesh=mesh, in_specs=in_specs, out_specs=out_specs, check_vma=False)
```

profile of v0, /device:TPU:6, one launch (start us, length us, event | category | flops | bytes accessed | tf_op | source)
XLA Modules:
  0.0 655.7 jit_solution(12685750839305819001)
XLA Ops:
  8.1 0.7 convert_element_type.83
  8.8 1.4 fusion.12
  12.6 0.7 copy-done.18
  14.0 0.7 copy-done.22
  16.5 1.4 fusion.43
  17.9 14.3 %psum.42 = f32[2,512]{1,0:T(2,128)S(1)} all-reduce(f32[2,512]{1,0:T(2,128)S(1)} %pad_maximum_fusion.6), channel_id=1, replica_groups=mesh['rows'=64,'cols'=8] {'cols'}, use_global_device_ids=true, to_apply=%region_10.0 | all-reduce | flops 1024 | bytes 8192 | tf_op jit(solution)/shard_map/psum | solution.py:30
  33.0 3.5 multiply_reduce_fusion.20
  36.6 282.1 %all-reduce = (f32[1,2048]{1,0:T(1,128)S(1)}, f32[2,2048]{1,0:T(2,128)S(1)}) all-reduce(f32[1,2048]{1,0:T(1,128)S(1)} %bitcast.32, f32[2,2048]{1,0:T(2,128)S(1)} %pad_maximum_fusion.1), channel_id=1, replica_groups=mesh['rows'=64,'cols'=8] {'rows'}, use_global_device_ids=true, to_apply=%region_24.0 | all-reduce | flops 6144 | bytes 49152 | tf_op jit(solution)/shard_map/psum | solution.py:34
  318.7 1.8 multiply_reduce_fusion.6
  320.5 13.0 %psum.45 = f32[512]{0:T(512)S(1)} all-reduce(f32[512]{0:T(512)S(1)} %add_add_fusion), channel_id=1, replica_groups=mesh['rows'=64,'cols'=8] {'cols'}, use_global_device_ids=true, to_apply=%region_29.0 | all-reduce | flops 512 | bytes 4096 | tf_op jit(solution)/shard_map/psum | solution.py:30
  333.6 1.7 multiply_reduce_fusion.3
  335.3 140.0 %psum.46 = f32[1,2048]{1,0:T(1,128)S(1)} all-reduce(f32[1,2048]{1,0:T(1,128)S(1)} %bitcast.33), channel_id=1, replica_groups=mesh['rows'=64,'cols'=8] {'rows'}, use_global_device_ids=true, to_apply=%region_34.0 | all-reduce | flops 2048 | bytes 16384 | tf_op jit(solution)/shard_map/psum | solution.py:34
  475.4 3.4 multiply_convert_fusion
  480.3 1.0 convolution_add_fusion.4
  481.6 1.4 fusion.54
  483.4 0.7 copy-done.13
  484.9 0.7 copy-done
  488.0 1.0 pad_maximum_fusion
  489.1 21.4 %reduce-scatter.2.cloned.1.call-done = f32[64,128]{1,0:T(8,128)} async-done(((f32[512,128]{1,0:T(8,128)}), f32[64,128]{1,0:T(8,128)}) %reduce-scatter.2.cloned.1.call-update) | async-done | bytes 32784 | tf_op jit(solution)/shard_map/reduce_scatter | solution.py:110
  510.6 0.9 fusion.40
  511.5 0.7 fusion.42
  512.2 132.5 %all-reduce.3.cloned.1.call-done = f32[2048,128]{1,0:T(8,128)} async-done(((f32[2048,128]{1,0:T(8,128)}), f32[2048,128]{1,0:T(8,128)}) %all-reduce.3.cloned.1.call-update) | async-done | bytes 1048592 | tf_op jit(solution)/shard_map/psum | solution.py:118
  644.8 1.9 fusion.14
  646.7 1.5 fusion.16
  (86 shorter events, 10.9 us)
Async XLA Ops:
  8.0 2.2 copy-start.7
  8.0 502.6 %reduce-scatter.2.cloned.1.call-start = ((), (), s32[]{:S(2)}) async-start(), calls=%async_computation.1 | async-start | bytes 294912 | tf_op jit(solution)/shard_map/reduce_scatter | solution.py:110
  10.2 0.9 copy-start.9
  11.1 5.3 copy-start.5
  11.5 5.0 copy-start.1
  11.8 4.1 copy-start.2
  12.2 3.2 copy-start.3
  12.2 1.0 copy-start.18
  13.3 2.1 copy-start.4
  13.3 0.7 copy-start.21
  14.0 0.7 copy-start.22
  475.4 3.5 copy-start.6
  478.8 0.8 copy-start.10
  478.8 1.0 copy-start.14
  478.8 1.2 copy-start.12
  478.8 1.5 copy-start.16
  481.3 163.4 %all-reduce.3.cloned.1.call-start = ((), (), s32[]{:S(2)}) async-start(), calls=%async_computation.2 | async-start | bytes 2097152 | tf_op jit(solution)/shard_map/psum | solution.py:118
  481.6 1.4 copy-start.15
  483.0 1.0 copy-start.13
  484.4 1.2 copy-start
  486.1 1.0 copy-start.11
  489.0 155.7 %copy-start.8 = (bf16[2048,128]{1,0:T(8,128)(2,1)S(1)}, bf16[2048,128]{1,0:T(8,128)(2,1)}, u32[]{:S(2)}) copy-start(bf16[2048,128]{1,0:T(8,128)(2,1)} %param.7) | copy-start | bytes 1572868
  510.6 0.9 copy-start.19
  644.8 2.0 copy-start.17
  (1 other events, 0.7 us)
Sparse Core Ops, SparseCore 0:
  481.4 29.0 reduce-scatter.1
Sparse Core Ops, SparseCore 1:
  489.1 155.6 all-reduce.2
where the time goes:
time: 656 us
  blocking collectives  449 us (68%)
  waiting for transfers between devices  154 us (23%)
  other arithmetic  19.5 us (3%)
  between operations  15.9 us (2%)
  matrix products  10.7 us (2%)
    psum x2, blocking collectives, across_queries(): return lax.psum(stack, 'rows')  422 us
    psum x1, waiting for transfers between devices, local(): whole = lax.psum(dphat, 'rows')  133 us
    psum x2, blocking collectives, across_slots(): return lax.psum(stack, 'cols')  27.4 us
    reduce_scatter x1, waiting for transfers between devices, local(): lax.psum_scatter(dqhat, 'cols', scatter_dimension=0, tiled=True)  21.4 us
  transfers between devices with their start and end apart: 2, of which 2 were waited for; matrix products, arithmetic and copies ran while one was open for 1% of the time, Pallas kernels for 0%

commit v1 on v0

--- a/solution.py
+++ b/solution.py
@@ -1,3 +1,4 @@
+import functools
 import math
 
 import jax
@@ -30,11 +31,18 @@
     return lax.psum(stack, "cols")
 
 
-def across_queries(stack):
-    return lax.psum(stack, "rows")
+def across_queries(stack, count):
+    if count & (count - 1):
+        return lax.psum(stack, "rows")
+    step = 1
+    while step < count:
+        pairs = [(i, i ^ step) for i in range(count)]
+        stack = stack + lax.ppermute(stack, "rows", pairs)
+        step *= 2
+    return stack
 
 
-def local(queries, prototypes, potential, weights, capacity, cotangent):
+def local(count, queries, prototypes, potential, weights, capacity, cotangent):
     qhat, qlen = unit_rows(queries)
     phat, plen = unit_rows(prototypes)
     wgt = weights.astype(jnp.float32)
@@ -69,12 +77,14 @@
         plan = share[:, None] * kernel_tile(start)
         col_parts.append(jnp.sum(plan, axis=0))
         q_parts.append(jnp.sum(plan * coupling_tile(start), axis=0))
-    summed = across_queries(jnp.stack([jnp.concatenate(col_parts), jnp.concatenate(q_parts)]))
-    colsum, qvec = (summed[0], summed[1])
     for start in starts:
         plan = share[:, None] * kernel_tile(start)
         t_parts.append(jnp.sum(alpha_one[:, None] * plan, axis=0))
-    t_one = across_queries(jnp.concatenate(t_parts)[None, :])[0]
+    summed = across_queries(
+        jnp.stack([jnp.concatenate(col_parts), jnp.concatenate(q_parts), jnp.concatenate(t_parts)]),
+        count,
+    )
+    colsum, qvec, t_one = (summed[0], summed[1], summed[2])
     beta_one = (qvec - t_one) / colsum
     rowprod = jnp.zeros((local_rows,), jnp.float32)
     for start in starts:
@@ -86,7 +96,7 @@
     for start in starts:
         plan = share[:, None] * kernel_tile(start)
         t_parts.append(jnp.sum(alpha_two[:, None] * plan, axis=0))
-    t_two = across_queries(jnp.concatenate(t_parts)[None, :])[0]
+    t_two = across_queries(jnp.concatenate(t_parts)[None, :], count)[0]
     beta_two = (qvec - t_two) / colsum
     dqhat = jnp.zeros(qhat.shape, jnp.float32)
     dp_parts = []
@@ -123,4 +133,5 @@
 def solution(mesh):
     in_specs = (P("rows", None), P("cols", None), P("cols"), P("rows"), P("cols"), P("rows", None))
     out_specs = (P(("rows", "cols"), None), P("cols", None))
-    return jax.shard_map(local, mesh=mesh, in_specs=in_specs, out_specs=out_specs, check_vma=False)
+    body = functools.partial(local, mesh.shape["rows"])
+    return jax.shard_map(body, mesh=mesh, in_specs=in_specs, out_specs=out_specs, check_vma=False)

time: 656 us -> 328 us (0.50)
  blocking collectives: 449 us -> 27.2 us
  starting transfers between devices: 0.26 us -> 57.5 us
  waiting for transfers between devices: 154 us -> 193 us
    psum x2 -> x0, blocking collectives: 422 us -> none  [across_queries(): return lax.psum(stack, 'rows')]
    ppermute x0 -> x12, starting transfers between devices: none -> 57.4 us  [across_queries(): stack = stack + lax.ppermute(stack, 'rows', pairs)]
    ppermute x0 -> x12, waiting for transfers between devices: none -> 30.1 us  [across_queries(): stack = stack + lax.ppermute(stack, 'rows', pairs)]
    reduce_scatter x1, waiting for transfers between devices: 21.4 us -> 33.3 us  [local(): lax.psum_scatter(dqhat, 'cols', scatter_dimension=0, tiled=True)]
  transfers between devices with their start and end apart: 2 -> 14, of which waited for: 2 -> 14; matrix products, arithmetic and copies ran while one was open for 1% -> 1% of each run, Pallas kernels for 0% -> 0%
where the time goes in v1:
time: 328 us; the launch traced here: 327 us
  waiting for transfers between devices  193 us (59%)
  starting transfers between devices  57.5 us (18%)
  blocking collectives  27.2 us (8%)
  other arithmetic  17.4 us (5%)
  between operations  16 us (5%)
  matrix products  11.7 us (4%)
  local copies, waits for them, and re-layouts  3.92 us (1%)
    psum x1, waiting for transfers between devices, local(): whole = lax.psum(dphat, 'rows')  130 us
    ppermute x12, starting transfers between devices, across_queries(): stack = stack + lax.ppermute(stack, 'rows', pairs)  57.4 us
    reduce_scatter x1, waiting for transfers between devices, local(): lax.psum_scatter(dqhat, 'cols', scatter_dimension=0, tiled=True)  33.3 us
    ppermute x12, waiting for transfers between devices, across_queries(): stack = stack + lax.ppermute(stack, 'rows', pairs)  30.1 us
    psum x2, blocking collectives, across_slots(): return lax.psum(stack, 'cols')  27.2 us
  transfers between devices with their start and end apart: 14, of which 14 were waited for; matrix products, arithmetic and copies ran while one was open for 1% of the time, Pallas kernels for 0%

profile of v1, /device:TPU:6, one launch (start us, length us, event | category | flops | bytes accessed | tf_op | source)
XLA Modules:
  0.0 326.8 jit_solution(14025920765103015439)
XLA Ops:
  17.9 14.3 %psum.21 = f32[2,512]{1,0:T(2,128)S(1)} all-reduce(f32[2,512]{1,0:T(2,128)S(1)} %pad_maximum_fusion.6), channel_id=1, replica_groups=mesh['rows'=64,'cols'=8] {'cols'}, use_global_device_ids=true, to_apply=%region_10.0 | all-reduce | flops 1024 | bytes 8192 | tf_op jit(solution)/shard_map/psum | solution.py:31
  33.0 3.6 %multiply_reduce_fusion.20 = (f32[512]{0:T(512)S(1)}, f32[512]{0:T(512)S(1)}, f32[512]{0:T(512)S(1)}, f32[512]{0:T(512)S(1)}, f32[512]{0:T(512)S(1)}, /*index=5*...) fusion(f32[512,512]{1,0:T(8,128)S(1)} %get-tuple-element.64, ...), kind=kLoop, calls=%fused_computation.58 | loop fusion | flops 6285312 | bytes 8417280 | tf_op jit(solution)/shard_map/reduce_sum | solution.py:78
  38.6 3.9 %collective-permute-done = f32[3,2048]{1,0:T(4,128)S(1)} collective-permute-done((f32[3,2048]{1,0:T(4,128)S(1)}, f32[3,2048]{1,0:T(4,128)S(1)}, u32[]{:S(2)}, u32[]{:S(2)}) %collective-permute-start) | collective-permute-done | bytes 24608 | tf_op jit(solution)/shard_map/ppermute | solution.py:40
  42.5 2.7 collective-permute-start.1
  45.2 4.1 %collective-permute-done.1 = f32[3,2048]{1,0:T(4,128)S(1)} collective-permute-done((f32[3,2048]{1,0:T(4,128)S(1)}, f32[3,2048]{1,0:T(4,128)S(1)}, u32[]{:S(2)}, u32[]{:S(2)}) %collective-permute-start.1) | collective-permute-done | bytes 24608 | tf_op jit(solution)/shard_map/ppermute | solution.py:40
  49.3 7.6 %collective-permute-start.2 = (f32[3,2048]{1,0:T(4,128)S(1)}, f32[3,2048]{1,0:T(4,128)S(1)}, u32[]{:S(2)}, u32[]{:S(2)}) collective-permute-start(f32[3,2048]{1,0:T(4,128)S(1)} %fusion.73), channel_id=1, source_target_pairs={{0,32},{8,40},{16,48},{24,56},{32,0},{40,8},{48,16},{56,24},{64,96... | collective-permute-start | bytes 73736 | tf_op jit(solution)/shard_map/ppermute | solution.py:40
  56.9 2.1 collective-permute-done.2
  59.0 3.3 %collective-permute-start.3 = (f32[3,2048]{1,0:T(4,128)S(1)}, f32[3,2048]{1,0:T(4,128)S(1)}, u32[]{:S(2)}, u32[]{:S(2)}) collective-permute-start(f32[3,2048]{1,0:T(4,128)S(1)} %add.208), channel_id=1, source_target_pairs={{0,64},{8,72},{16,80},{24,88},{32,96},{40,104},{48,112},{56,120},{... | collective-permute-start | bytes 73736 | tf_op jit(solution)/shard_map/ppermute | solution.py:40
  62.3 2.5 collective-permute-done.3
  64.8 4.3 %collective-permute-start.4 = (f32[3,2048]{1,0:T(4,128)S(1)}, f32[3,2048]{1,0:T(4,128)S(1)}, u32[]{:S(2)}, u32[]{:S(2)}) collective-permute-start(f32[3,2048]{1,0:T(4,128)S(1)} %add.209), channel_id=1, source_target_pairs={{0,128},{8,136},{16,144},{24,152},{32,160},{40,168},{48,176},{56,1... | collective-permute-start | bytes 73736 | tf_op jit(solution)/shard_map/ppermute | solution.py:40
  69.1 2.4 collective-permute-done.4
  71.6 7.9 %collective-permute-start.5 = (f32[3,2048]{1,0:T(4,128)S(1)}, f32[3,2048]{1,0:T(4,128)S(1)}, u32[]{:S(2)}, u32[]{:S(2)}) collective-permute-start(f32[3,2048]{1,0:T(4,128)S(1)} %add.210), channel_id=1, source_target_pairs={{0,256},{8,264},{16,272},{24,280},{32,288},{40,296},{48,304},{56,3... | collective-permute-start | bytes 73736 | tf_op jit(solution)/shard_map/ppermute | solution.py:40
  82.1 12.9 %psum.22 = f32[512]{0:T(512)S(1)} all-reduce(f32[512]{0:T(512)S(1)} %add_add_fusion), channel_id=1, replica_groups=mesh['rows'=64,'cols'=8] {'cols'}, use_global_device_ids=true, to_apply=%region_27.0 | all-reduce | flops 512 | bytes 4096 | tf_op jit(solution)/shard_map/psum | solution.py:31
  96.9 3.1 collective-permute-start.6
  100.0 2.5 collective-permute-done.6
  102.5 3.8 %collective-permute-start.7 = (f32[1,2048]{1,0:T(1,128)S(1)}, f32[1,2048]{1,0:T(1,128)S(1)}, u32[]{:S(2)}, u32[]{:S(2)}) collective-permute-start(f32[1,2048]{1,0:T(1,128)S(1)} %add.216), channel_id=1, source_target_pairs={{0,16},{8,24},{16,0},{24,8},{32,48},{40,56},{48,32},{56,40},{64,80... | collective-permute-start | bytes 24584 | tf_op jit(solution)/shard_map/ppermute | solution.py:40
  106.3 2.7 collective-permute-done.7
  108.9 7.6 %collective-permute-start.8 = (f32[1,2048]{1,0:T(1,128)S(1)}, f32[1,2048]{1,0:T(1,128)S(1)}, u32[]{:S(2)}, u32[]{:S(2)}) collective-permute-start(f32[1,2048]{1,0:T(1,128)S(1)} %add.217), channel_id=1, source_target_pairs={{0,32},{8,40},{16,48},{24,56},{32,0},{40,8},{48,16},{56,24},{64,96... | collective-permute-start | bytes 24584 | tf_op jit(solution)/shard_map/ppermute | solution.py:40
  118.4 3.2 collective-permute-start.9
  121.6 2.4 collective-permute-done.9
  123.9 4.4 %collective-permute-start.10 = (f32[1,2048]{1,0:T(1,128)S(1)}, f32[1,2048]{1,0:T(1,128)S(1)}, u32[]{:S(2)}, u32[]{:S(2)}) collective-permute-start(f32[1,2048]{1,0:T(1,128)S(1)} %add.219), channel_id=1, source_target_pairs={{0,128},{8,136},{16,144},{24,152},{32,160},{40,168},{48,176},{56,1... | collective-permute-start | bytes 24584 | tf_op jit(solution)/shard_map/ppermute | solution.py:40
  130.4 7.7 %collective-permute-start.11 = (f32[1,2048]{1,0:T(1,128)S(1)}, f32[1,2048]{1,0:T(1,128)S(1)}, u32[]{:S(2)}, u32[]{:S(2)}) collective-permute-start(f32[1,2048]{1,0:T(1,128)S(1)} %add.220), channel_id=1, source_target_pairs={{0,256},{8,264},{16,272},{24,280},{32,288},{40,296},{48,304},{56,3... | collective-permute-start | bytes 24584 | tf_op jit(solution)/shard_map/ppermute | solution.py:40
  151.3 33.3 %reduce-scatter.2.cloned.1.call-done = f32[64,128]{1,0:T(8,128)} async-done(((f32[512,128]{1,0:T(8,128)}), f32[64,128]{1,0:T(8,128)}) %reduce-scatter.2.cloned.1.call-update) | async-done | bytes 32784 | tf_op jit(solution)/shard_map/reduce_scatter | solution.py:120
  186.2 129.7 %all-reduce.2.cloned.1.call-done = f32[2048,128]{1,0:T(8,128)} async-done(((f32[2048,128]{1,0:T(8,128)}), f32[2048,128]{1,0:T(8,128)}) %all-reduce.2.cloned.1.call-update) | async-done | bytes 1048592 | tf_op jit(solution)/shard_map/psum | solution.py:128
  (123 shorter events, 39.0 us)
Async XLA Ops:
  8.0 176.5 %reduce-scatter.2.cloned.1.call-start = ((), (), s32[]{:S(2)}) async-start(), calls=%async_computation.1 | async-start | bytes 294912 | tf_op jit(solution)/shard_map/reduce_scatter | solution.py:120
  11.1 5.3 %copy-start.9 = (bf16[2048,128]{1,0:T(8,128)(2,1)}, bf16[2048,128]{1,0:T(8,128)(2,1)S(1)}, u32[]{:S(2)}) copy-start(bf16[2048,128]{1,0:T(8,128)(2,1)S(1)} %fusion.13) | copy-start | bytes 1572868
  11.5 5.0 %copy-start.2 = (f32[512,512]{1,0:T(8,128)}, f32[512,512]{1,0:T(8,128)S(1)}, u32[]{:S(2)}) copy-start(f32[512,512]{1,0:T(8,128)S(1)} %fusion.32) | copy-start | bytes 3145732
  11.8 4.1 %copy-start.4 = (f32[512,512]{1,0:T(8,128)}, f32[512,512]{1,0:T(8,128)S(1)}, u32[]{:S(2)}) copy-start(f32[512,512]{1,0:T(8,128)S(1)} %fusion.28) | copy-start | bytes 3145732
  33.0 48.6 %copy-start = (f32[512,512]{1,0:T(8,128)S(1)}, f32[512,512]{1,0:T(8,128)}, u32[]{:S(2)}) copy-start(f32[512,512]{1,0:T(8,128)} %get-tuple-element.67) | copy-start | bytes 3145732
  36.7 5.8 %collective-permute-start = (f32[3,2048]{1,0:T(4,128)S(1)}, f32[3,2048]{1,0:T(4,128)S(1)}, u32[]{:S(2)}, u32[]{:S(2)}) collective-permute-start(f32[3,2048]{1,0:T(4,128)S(1)} %pad_maximum_fusion.1), channel_id=1, source_target_pairs={{0,8},{8,0},{16,24},{24,16},{32,40},{40,32},{48,56},{56,48},{64,72... | collective-permute-start | bytes 73736 | tf_op jit(solution)/shard_map/ppermute | solution.py:40
  42.5 6.7 %collective-permute-start.1 = (f32[3,2048]{1,0:T(4,128)S(1)}, f32[3,2048]{1,0:T(4,128)S(1)}, u32[]{:S(2)}, u32[]{:S(2)}) collective-permute-start(f32[3,2048]{1,0:T(4,128)S(1)} %fusion.44), channel_id=1, source_target_pairs={{0,16},{8,24},{16,0},{24,8},{32,48},{40,56},{48,32},{56,40},{64,80... | collective-permute-start | bytes 73736 | tf_op jit(solution)/shard_map/ppermute | solution.py:40
  49.3 9.7 %collective-permute-start.2 = (f32[3,2048]{1,0:T(4,128)S(1)}, f32[3,2048]{1,0:T(4,128)S(1)}, u32[]{:S(2)}, u32[]{:S(2)}) collective-permute-start(f32[3,2048]{1,0:T(4,128)S(1)} %fusion.73), channel_id=1, source_target_pairs={{0,32},{8,40},{16,48},{24,56},{32,0},{40,8},{48,16},{56,24},{64,96... | collective-permute-start | bytes 73736 | tf_op jit(solution)/shard_map/ppermute | solution.py:40
  59.0 5.8 %collective-permute-start.3 = (f32[3,2048]{1,0:T(4,128)S(1)}, f32[3,2048]{1,0:T(4,128)S(1)}, u32[]{:S(2)}, u32[]{:S(2)}) collective-permute-start(f32[3,2048]{1,0:T(4,128)S(1)} %add.208), channel_id=1, source_target_pairs={{0,64},{8,72},{16,80},{24,88},{32,96},{40,104},{48,112},{56,120},{... | collective-permute-start | bytes 73736 | tf_op jit(solution)/shard_map/ppermute | solution.py:40
  64.8 6.7 %collective-permute-start.4 = (f32[3,2048]{1,0:T(4,128)S(1)}, f32[3,2048]{1,0:T(4,128)S(1)}, u32[]{:S(2)}, u32[]{:S(2)}) collective-permute-start(f32[3,2048]{1,0:T(4,128)S(1)} %add.209), channel_id=1, source_target_pairs={{0,128},{8,136},{16,144},{24,152},{32,160},{40,168},{48,176},{56,1... | collective-permute-start | bytes 73736 | tf_op jit(solution)/shard_map/ppermute | solution.py:40
  71.6 9.9 %collective-permute-start.5 = (f32[3,2048]{1,0:T(4,128)S(1)}, f32[3,2048]{1,0:T(4,128)S(1)}, u32[]{:S(2)}, u32[]{:S(2)}) collective-permute-start(f32[3,2048]{1,0:T(4,128)S(1)} %add.210), channel_id=1, source_target_pairs={{0,256},{8,264},{16,272},{24,280},{32,288},{40,296},{48,304},{56,3... | collective-permute-start | bytes 73736 | tf_op jit(solution)/shard_map/ppermute | solution.py:40
  95.0 44.9 %copy-start.1 = (f32[512,512]{1,0:T(8,128)S(1)}, f32[512,512]{1,0:T(8,128)}, u32[]{:S(2)}) copy-start(f32[512,512]{1,0:T(8,128)} %get-tuple-element.67) | copy-start | bytes 3145732
  95.0 44.9 %copy-start.3 = (f32[512,512]{1,0:T(8,128)S(1)}, f32[512,512]{1,0:T(8,128)}, u32[]{:S(2)}) copy-start(f32[512,512]{1,0:T(8,128)} %copy-done.2) | copy-start | bytes 3145732
  95.0 44.9 %copy-start.5 = (f32[512,512]{1,0:T(8,128)S(1)}, f32[512,512]{1,0:T(8,128)}, u32[]{:S(2)}) copy-start(f32[512,512]{1,0:T(8,128)} %copy-done.4) | copy-start | bytes 3145732
  95.0 44.9 %copy-start.7 = (f32[512,512]{1,0:T(8,128)S(1)}, f32[512,512]{1,0:T(8,128)}, u32[]{:S(2)}) copy-start(f32[512,512]{1,0:T(8,128)} %copy-done.6) | copy-start | bytes 3145732
  96.9 5.5 %collective-permute-start.6 = (f32[1,2048]{1,0:T(1,128)S(1)}, f32[1,2048]{1,0:T(1,128)S(1)}, u32[]{:S(2)}, u32[]{:S(2)}) collective-permute-start(f32[1,2048]{1,0:T(1,128)S(1)} %bitcast.41), channel_id=1, source_target_pairs={{0,8},{8,0},{16,24},{24,16},{32,40},{40,32},{48,56},{56,48},{64,72... | collective-permute-start | bytes 24584 | tf_op jit(solution)/shard_map/ppermute | solution.py:40
  102.5 6.4 %collective-permute-start.7 = (f32[1,2048]{1,0:T(1,128)S(1)}, f32[1,2048]{1,0:T(1,128)S(1)}, u32[]{:S(2)}, u32[]{:S(2)}) collective-permute-start(f32[1,2048]{1,0:T(1,128)S(1)} %add.216), channel_id=1, source_target_pairs={{0,16},{8,24},{16,0},{24,8},{32,48},{40,56},{48,32},{56,40},{64,80... | collective-permute-start | bytes 24584 | tf_op jit(solution)/shard_map/ppermute | solution.py:40
  108.9 9.5 %collective-permute-start.8 = (f32[1,2048]{1,0:T(1,128)S(1)}, f32[1,2048]{1,0:T(1,128)S(1)}, u32[]{:S(2)}, u32[]{:S(2)}) collective-permute-start(f32[1,2048]{1,0:T(1,128)S(1)} %add.217), channel_id=1, source_target_pairs={{0,32},{8,40},{16,48},{24,56},{32,0},{40,8},{48,16},{56,24},{64,96... | collective-permute-start | bytes 24584 | tf_op jit(solution)/shard_map/ppermute | solution.py:40
  118.4 5.5 %collective-permute-start.9 = (f32[1,2048]{1,0:T(1,128)S(1)}, f32[1,2048]{1,0:T(1,128)S(1)}, u32[]{:S(2)}, u32[]{:S(2)}) collective-permute-start(f32[1,2048]{1,0:T(1,128)S(1)} %add.218), channel_id=1, source_target_pairs={{0,64},{8,72},{16,80},{24,88},{32,96},{40,104},{48,112},{56,120},{... | collective-permute-start | bytes 24584 | tf_op jit(solution)/shard_map/ppermute | solution.py:40
  123.9 6.4 %collective-permute-start.10 = (f32[1,2048]{1,0:T(1,128)S(1)}, f32[1,2048]{1,0:T(1,128)S(1)}, u32[]{:S(2)}, u32[]{:S(2)}) collective-permute-start(f32[1,2048]{1,0:T(1,128)S(1)} %add.219), channel_id=1, source_target_pairs={{0,128},{8,136},{16,144},{24,152},{32,160},{40,168},{48,176},{56,1... | collective-permute-start | bytes 24584 | tf_op jit(solution)/shard_map/ppermute | solution.py:40
  130.4 9.5 %collective-permute-start.11 = (f32[1,2048]{1,0:T(1,128)S(1)}, f32[1,2048]{1,0:T(1,128)S(1)}, u32[]{:S(2)}, u32[]{:S(2)}) collective-permute-start(f32[1,2048]{1,0:T(1,128)S(1)} %add.220), channel_id=1, source_target_pairs={{0,256},{8,264},{16,272},{24,280},{32,288},{40,296},{48,304},{56,3... | collective-permute-start | bytes 24584 | tf_op jit(solution)/shard_map/ppermute | solution.py:40
  142.1 4.6 %copy-start.14 = (bf16[512,512]{1,0:T(8,128)(2,1)}, bf16[512,512]{1,0:T(8,128)(2,1)S(1)}, u32[]{:S(2)}) copy-start(bf16[512,512]{1,0:T(8,128)(2,1)S(1)} %get-tuple-element.61) | copy-start | bytes 1572868
  148.6 167.3 %all-reduce.2.cloned.1.call-start = ((), (), s32[]{:S(2)}) async-start(), calls=%async_computation.2 | async-start | bytes 2097152 | tf_op jit(solution)/shard_map/psum | solution.py:128
  151.2 164.7 %copy-start.12 = (bf16[2048,128]{1,0:T(8,128)(2,1)S(1)}, bf16[2048,128]{1,0:T(8,128)(2,1)}, u32[]{:S(2)}) copy-start(bf16[2048,128]{1,0:T(8,128)(2,1)} %param.7) | copy-start | bytes 1572868
  (15 other events, 19.7 us)
Sparse Core Ops, SparseCore 0:
  148.7 35.7 reduce-scatter.1
Sparse Core Ops, SparseCore 1:
  153.2 162.6 all-reduce.1

commit v2 on v1

--- a/solution.py
+++ b/solution.py
@@ -42,7 +42,21 @@
     return stack
 
 
-def local(count, queries, prototypes, potential, weights, capacity, cotangent):
+def halving_scatter(block, axis, count):
+    where = lax.axis_index(axis)
+    step = count // 2
+    while step >= 1:
+        half = block.shape[0] // 2
+        bit = (where // step) % 2
+        keep = lax.dynamic_slice_in_dim(block, bit * half, half, 0)
+        send = lax.dynamic_slice_in_dim(block, (1 - bit) * half, half, 0)
+        pairs = [(i, i ^ step) for i in range(count)]
+        block = keep + lax.ppermute(send, axis, pairs)
+        step //= 2
+    return block
+
+
+def local(count, width_cols, queries, prototypes, potential, weights, capacity, cotangent):
     qhat, qlen = unit_rows(queries)
     phat, plen = unit_rows(prototypes)
     wgt = weights.astype(jnp.float32)
@@ -117,7 +131,10 @@
         )
         dp_parts.append(part)
     dphat = jnp.concatenate(dp_parts, axis=0)
-    query_part = lax.psum_scatter(dqhat, "cols", scatter_dimension=0, tiled=True)
+    if width_cols & (width_cols - 1) or local_rows % width_cols:
+        query_part = lax.psum_scatter(dqhat, "cols", scatter_dimension=0, tiled=True)
+    else:
+        query_part = halving_scatter(dqhat, "cols", width_cols)
     piece = query_part.shape[0]
     begin = lax.axis_index("cols") * piece
     grad_queries = unit_back(
@@ -133,5 +150,5 @@
 def solution(mesh):
     in_specs = (P("rows", None), P("cols", None), P("cols"), P("rows"), P("cols"), P("rows", None))
     out_specs = (P(("rows", "cols"), None), P("cols", None))
-    body = functools.partial(local, mesh.shape["rows"])
+    body = functools.partial(local, mesh.shape["rows"], mesh.shape["cols"])
     return jax.shard_map(body, mesh=mesh, in_specs=in_specs, out_specs=out_specs, check_vma=False)

time: 328 us -> 328 us (level)
  starting transfers between devices: 57.5 us -> 69.1 us
  waiting for transfers between devices: 193 us -> 184 us
    reduce_scatter x1 -> x0, waiting for transfers between devices: 33.3 us -> none  [local(): lax.psum_scatter(dqhat, 'cols', scatter_dimension=0, tiled=True)]
    psum x1, waiting for transfers between devices: 130 us -> 151 us  [local(): whole = lax.psum(dphat, 'rows')]
    ppermute x0 -> x3, starting transfers between devices: none -> 10.7 us  [halving_scatter(): block = keep + lax.ppermute(send, axis, pairs)]
    ppermute x0 -> x3, waiting for transfers between devices: none -> 4.19 us  [halving_scatter(): block = keep + lax.ppermute(send, axis, pairs)]
  transfers between devices with their start and end apart: 14 -> 16, of which waited for: 14 -> 16; matrix products, arithmetic and copies ran while one was open for 1% -> 1% of each run, Pallas kernels for 0% -> 0%
where the time goes in v2:
time: 328 us; the launch traced here: 327 us
  waiting for transfers between devices  184 us (56%)
  starting transfers between devices  69.1 us (21%)
  blocking collectives  27.2 us (8%)
  other arithmetic  18 us (5%)
  between operations  14.7 us (4%)
  matrix products  8.91 us (3%)
  local copies, waits for them, and re-layouts  4.79 us (1%)
    psum x1, waiting for transfers between devices, local(): whole = lax.psum(dphat, 'rows')  151 us
    ppermute x12, starting transfers between devices, across_queries(): stack = stack + lax.ppermute(stack, 'rows', pairs)  58.4 us
    ppermute x12, waiting for transfers between devices, across_queries(): stack = stack + lax.ppermute(stack, 'rows', pairs)  29.1 us
    psum x2, blocking collectives, across_slots(): return lax.psum(stack, 'cols')  27.2 us
    ppermute x3, starting transfers between devices, halving_scatter(): block = keep + lax.ppermute(send, axis, pairs)  10.7 us
  transfers between devices with their start and end apart: 16, of which 16 were waited for; matrix products, arithmetic and copies ran while one was open for 1% of the time, Pallas kernels for 0%

profile of v2, /device:TPU:6, one launch (start us, length us, event | category | flops | bytes accessed | tf_op | source)
XLA Modules:
  0.0 327.0 jit_solution(6576879975461872445)
XLA Ops:
  16.5 14.3 %psum.21 = f32[2,512]{1,0:T(2,128)S(1)} all-reduce(f32[2,512]{1,0:T(2,128)S(1)} %pad_maximum_fusion.6), channel_id=1, replica_groups=mesh['rows'=64,'cols'=8] {'cols'}, use_global_device_ids=true, to_apply=%region_10.0 | all-reduce | flops 1024 | bytes 8192 | tf_op jit(solution)/shard_map/psum | solution.py:31
  30.8 3.6 %multiply_reduce_fusion.20 = (f32[512]{0:T(512)S(1)}, f32[512]{0:T(512)S(1)}, f32[512]{0:T(512)S(1)}, f32[512]{0:T(512)S(1)}, f32[512]{0:T(512)S(1)}, /*index=5*...) fusion(f32[512,512]{1,0:T(8,128)S(1)} %get-tuple-element.64, ...), kind=kLoop, calls=%fused_computation.58 | loop fusion | flops 6285312 | bytes 8417280 | tf_op jit(solution)/shard_map/reduce_sum | solution.py:92
  36.5 3.9 %collective-permute-done = f32[3,2048]{1,0:T(4,128)S(1)} collective-permute-done((f32[3,2048]{1,0:T(4,128)S(1)}, f32[3,2048]{1,0:T(4,128)S(1)}, u32[]{:S(2)}, u32[]{:S(2)}) %collective-permute-start) | collective-permute-done | bytes 24608 | tf_op jit(solution)/shard_map/ppermute | solution.py:40
  40.4 2.7 collective-permute-start.1
  43.0 4.1 %collective-permute-done.1 = f32[3,2048]{1,0:T(4,128)S(1)} collective-permute-done((f32[3,2048]{1,0:T(4,128)S(1)}, f32[3,2048]{1,0:T(4,128)S(1)}, u32[]{:S(2)}, u32[]{:S(2)}) %collective-permute-start.1) | collective-permute-done | bytes 24608 | tf_op jit(solution)/shard_map/ppermute | solution.py:40
  47.2 7.6 %collective-permute-start.2 = (f32[3,2048]{1,0:T(4,128)S(1)}, f32[3,2048]{1,0:T(4,128)S(1)}, u32[]{:S(2)}, u32[]{:S(2)}) collective-permute-start(f32[3,2048]{1,0:T(4,128)S(1)} %fusion.73), channel_id=1, source_target_pairs={{0,32},{8,40},{16,48},{24,56},{32,0},{40,8},{48,16},{56,24},{64,96... | collective-permute-start | bytes 73736 | tf_op jit(solution)/shard_map/ppermute | solution.py:40
  56.9 3.3 %collective-permute-start.3 = (f32[3,2048]{1,0:T(4,128)S(1)}, f32[3,2048]{1,0:T(4,128)S(1)}, u32[]{:S(2)}, u32[]{:S(2)}) collective-permute-start(f32[3,2048]{1,0:T(4,128)S(1)} %add.246), channel_id=1, source_target_pairs={{0,64},{8,72},{16,80},{24,88},{32,96},{40,104},{48,112},{56,120},{... | collective-permute-start | bytes 73736 | tf_op jit(solution)/shard_map/ppermute | solution.py:40
  60.2 2.5 collective-permute-done.3
  62.7 4.3 %collective-permute-start.4 = (f32[3,2048]{1,0:T(4,128)S(1)}, f32[3,2048]{1,0:T(4,128)S(1)}, u32[]{:S(2)}, u32[]{:S(2)}) collective-permute-start(f32[3,2048]{1,0:T(4,128)S(1)} %add.247), channel_id=1, source_target_pairs={{0,128},{8,136},{16,144},{24,152},{32,160},{40,168},{48,176},{56,1... | collective-permute-start | bytes 73736 | tf_op jit(solution)/shard_map/ppermute | solution.py:40
  67.0 2.4 collective-permute-done.4
  69.4 7.9 %collective-permute-start.5 = (f32[3,2048]{1,0:T(4,128)S(1)}, f32[3,2048]{1,0:T(4,128)S(1)}, u32[]{:S(2)}, u32[]{:S(2)}) collective-permute-start(f32[3,2048]{1,0:T(4,128)S(1)} %add.248), channel_id=1, source_target_pairs={{0,256},{8,264},{16,272},{24,280},{32,288},{40,296},{48,304},{56,3... | collective-permute-start | bytes 73736 | tf_op jit(solution)/shard_map/ppermute | solution.py:40
  80.0 12.9 %psum.22 = f32[512]{0:T(512)S(1)} all-reduce(f32[512]{0:T(512)S(1)} %add_add_fusion), channel_id=1, replica_groups=mesh['rows'=64,'cols'=8] {'cols'}, use_global_device_ids=true, to_apply=%region_27.0 | all-reduce | flops 512 | bytes 4096 | tf_op jit(solution)/shard_map/psum | solution.py:31
  94.6 3.1 collective-permute-start.6
  97.7 2.5 collective-permute-done.6
  100.2 4.4 %collective-permute-start.7 = (f32[1,2048]{1,0:T(1,128)S(1)}, f32[1,2048]{1,0:T(1,128)S(1)}, u32[]{:S(2)}, u32[]{:S(2)}) collective-permute-start(f32[1,2048]{1,0:T(1,128)S(1)} %add.254), channel_id=1, source_target_pairs={{0,16},{8,24},{16,0},{24,8},{32,48},{40,56},{48,32},{56,40},{64,80... | collective-permute-start | bytes 24584 | tf_op jit(solution)/shard_map/ppermute | solution.py:40
  106.6 7.6 %collective-permute-start.8 = (f32[1,2048]{1,0:T(1,128)S(1)}, f32[1,2048]{1,0:T(1,128)S(1)}, u32[]{:S(2)}, u32[]{:S(2)}) collective-permute-start(f32[1,2048]{1,0:T(1,128)S(1)} %add.255), channel_id=1, source_target_pairs={{0,32},{8,40},{16,48},{24,56},{32,0},{40,8},{48,16},{56,24},{64,96... | collective-permute-start | bytes 24584 | tf_op jit(solution)/shard_map/ppermute | solution.py:40
  116.1 3.1 collective-permute-start.9
  119.2 2.4 collective-permute-done.9
  121.6 4.5 %collective-permute-start.10 = (f32[1,2048]{1,0:T(1,128)S(1)}, f32[1,2048]{1,0:T(1,128)S(1)}, u32[]{:S(2)}, u32[]{:S(2)}) collective-permute-start(f32[1,2048]{1,0:T(1,128)S(1)} %add.257), channel_id=1, source_target_pairs={{0,128},{8,136},{16,144},{24,152},{32,160},{40,168},{48,176},{56,1... | collective-permute-start | bytes 24584 | tf_op jit(solution)/shard_map/ppermute | solution.py:40
  128.1 7.9 %collective-permute-start.11 = (f32[1,2048]{1,0:T(1,128)S(1)}, f32[1,2048]{1,0:T(1,128)S(1)}, u32[]{:S(2)}, u32[]{:S(2)}) collective-permute-start(f32[1,2048]{1,0:T(1,128)S(1)} %add.258), channel_id=1, source_target_pairs={{0,256},{8,264},{16,272},{24,280},{32,288},{40,296},{48,304},{56,3... | collective-permute-start | bytes 24584 | tf_op jit(solution)/shard_map/ppermute | solution.py:40
  137.6 3.4 %multiply_convert_fusion = (bf16[512,512]{1,0:T(8,128)(2,1)S(1)}, bf16[512,512]{1,0:T(8,128)(2,1)S(1)}, bf16[512,512]{1,0:T(8,128)(2,1)S(1)}, bf16[512,512]{1,0:T(8,128)(2,1)S(1)}) fusion(f32[512,512]{1,0:T(8,128)} %copy-done.2, f32[512,512]{1,0:T(8,128)S(1)} %get-tuple-element.64, f32[512]{0:T(512)S(1)} %bitcast.51, f32[512]{0:T(512)S(1)} %subtract_divide_fusion.1, ...), kind=kLoop, calls=%fused_computation.33 | loop fusion | flops 6291456 | bytes 10498048 | tf_op jit(solution)/shard_map/convert_element_type | solution.py:121
  145.0 4.0 %collective-permute-start.12 = (f32[256,128]{1,0:T(8,128)}, f32[256,128]{1,0:T(8,128)}, u32[]{:S(2)}, u32[]{:S(2)}) collective-permute-start(f32[256,128]{1,0:T(8,128)} %constant_dynamic-slice_fusion.2), channel_id=1, source_target_pairs={{0,4},{1,5},{2,6},{3,7},{4,0},{5,1},{6,2},{7,3},{8,12},{9,13},{10,... | collective-permute-start | bytes 393224 | tf_op jit(solution)/shard_map/ppermute | solution.py:54
  154.6 4.8 %collective-permute-start.13 = (f32[128,128]{1,0:T(8,128)S(1)}, f32[128,128]{1,0:T(8,128)S(1)}, u32[]{:S(2)}, u32[]{:S(2)}) collective-permute-start(f32[128,128]{1,0:T(8,128)S(1)} %constant_dynamic-slice_fusion.1), channel_id=1, source_target_pairs={{0,2},{1,3},{2,0},{3,1},{4,6},{5,7},{6,4},{7,5},{8,10},{9,11},{10,... | collective-permute-start | bytes 196616 | tf_op jit(solution)/shard_map/ppermute | solution.py:54
  165.6 151.1 %all-reduce.2.cloned.1.call-done = f32[2048,128]{1,0:T(8,128)} async-done(((f32[2048,128]{1,0:T(8,128)}), f32[2048,128]{1,0:T(8,128)}) %all-reduce.2.cloned.1.call-update) | async-done | bytes 1048592 | tf_op jit(solution)/shard_map/psum | solution.py:145
  (117 shorter events, 44.1 us)
Async XLA Ops:
  7.2 309.5 %all-reduce.2.cloned.1.call-start = ((), (), s32[]{:S(2)}) async-start(), calls=%async_computation | async-start | bytes 2097152 | tf_op jit(solution)/shard_map/psum | solution.py:145
  9.4 5.6 %copy-start.6 = (bf16[2048,128]{1,0:T(8,128)(2,1)}, bf16[2048,128]{1,0:T(8,128)(2,1)S(1)}, u32[]{:S(2)}) copy-start(bf16[2048,128]{1,0:T(8,128)(2,1)S(1)} %fusion.13) | copy-start | bytes 1572868
  10.0 3.4 %copy-start.2 = (f32[512,512]{1,0:T(8,128)}, f32[512,512]{1,0:T(8,128)S(1)}, u32[]{:S(2)}) copy-start(f32[512,512]{1,0:T(8,128)S(1)} %fusion.24) | copy-start | bytes 3145732
  10.3 3.6 %copy-start.3 = (f32[512,512]{1,0:T(8,128)}, f32[512,512]{1,0:T(8,128)S(1)}, u32[]{:S(2)}) copy-start(f32[512,512]{1,0:T(8,128)S(1)} %fusion.37) | copy-start | bytes 3145732
  10.7 3.7 %copy-start.4 = (f32[512,512]{1,0:T(8,128)}, f32[512,512]{1,0:T(8,128)S(1)}, u32[]{:S(2)}) copy-start(f32[512,512]{1,0:T(8,128)S(1)} %fusion.28) | copy-start | bytes 3145732
  11.8 3.2 copy-start.5
  30.8 48.6 %copy-start = (f32[512,512]{1,0:T(8,128)S(1)}, f32[512,512]{1,0:T(8,128)}, u32[]{:S(2)}) copy-start(f32[512,512]{1,0:T(8,128)} %get-tuple-element.67) | copy-start | bytes 3145732
  34.5 5.8 %collective-permute-start = (f32[3,2048]{1,0:T(4,128)S(1)}, f32[3,2048]{1,0:T(4,128)S(1)}, u32[]{:S(2)}, u32[]{:S(2)}) collective-permute-start(f32[3,2048]{1,0:T(4,128)S(1)} %pad_maximum_fusion.1), channel_id=1, source_target_pairs={{0,8},{8,0},{16,24},{24,16},{32,40},{40,32},{48,56},{56,48},{64,72... | collective-permute-start | bytes 73736 | tf_op jit(solution)/shard_map/ppermute | solution.py:40
  40.4 6.7 %collective-permute-start.1 = (f32[3,2048]{1,0:T(4,128)S(1)}, f32[3,2048]{1,0:T(4,128)S(1)}, u32[]{:S(2)}, u32[]{:S(2)}) collective-permute-start(f32[3,2048]{1,0:T(4,128)S(1)} %fusion.44), channel_id=1, source_target_pairs={{0,16},{8,24},{16,0},{24,8},{32,48},{40,56},{48,32},{56,40},{64,80... | collective-permute-start | bytes 73736 | tf_op jit(solution)/shard_map/ppermute | solution.py:40
  47.2 9.7 %collective-permute-start.2 = (f32[3,2048]{1,0:T(4,128)S(1)}, f32[3,2048]{1,0:T(4,128)S(1)}, u32[]{:S(2)}, u32[]{:S(2)}) collective-permute-start(f32[3,2048]{1,0:T(4,128)S(1)} %fusion.73), channel_id=1, source_target_pairs={{0,32},{8,40},{16,48},{24,56},{32,0},{40,8},{48,16},{56,24},{64,96... | collective-permute-start | bytes 73736 | tf_op jit(solution)/shard_map/ppermute | solution.py:40
  56.9 5.8 %collective-permute-start.3 = (f32[3,2048]{1,0:T(4,128)S(1)}, f32[3,2048]{1,0:T(4,128)S(1)}, u32[]{:S(2)}, u32[]{:S(2)}) collective-permute-start(f32[3,2048]{1,0:T(4,128)S(1)} %add.246), channel_id=1, source_target_pairs={{0,64},{8,72},{16,80},{24,88},{32,96},{40,104},{48,112},{56,120},{... | collective-permute-start | bytes 73736 | tf_op jit(solution)/shard_map/ppermute | solution.py:40
  62.7 6.7 %collective-permute-start.4 = (f32[3,2048]{1,0:T(4,128)S(1)}, f32[3,2048]{1,0:T(4,128)S(1)}, u32[]{:S(2)}, u32[]{:S(2)}) collective-permute-start(f32[3,2048]{1,0:T(4,128)S(1)} %add.247), channel_id=1, source_target_pairs={{0,128},{8,136},{16,144},{24,152},{32,160},{40,168},{48,176},{56,1... | collective-permute-start | bytes 73736 | tf_op jit(solution)/shard_map/ppermute | solution.py:40
  69.4 9.9 %collective-permute-start.5 = (f32[3,2048]{1,0:T(4,128)S(1)}, f32[3,2048]{1,0:T(4,128)S(1)}, u32[]{:S(2)}, u32[]{:S(2)}) collective-permute-start(f32[3,2048]{1,0:T(4,128)S(1)} %add.248), channel_id=1, source_target_pairs={{0,256},{8,264},{16,272},{24,280},{32,288},{40,296},{48,304},{56,3... | collective-permute-start | bytes 73736 | tf_op jit(solution)/shard_map/ppermute | solution.py:40
  94.6 5.5 %collective-permute-start.6 = (f32[1,2048]{1,0:T(1,128)S(1)}, f32[1,2048]{1,0:T(1,128)S(1)}, u32[]{:S(2)}, u32[]{:S(2)}) collective-permute-start(f32[1,2048]{1,0:T(1,128)S(1)} %bitcast.41), channel_id=1, source_target_pairs={{0,8},{8,0},{16,24},{24,16},{32,40},{40,32},{48,56},{56,48},{64,72... | collective-permute-start | bytes 24584 | tf_op jit(solution)/shard_map/ppermute | solution.py:40
  100.2 6.4 %collective-permute-start.7 = (f32[1,2048]{1,0:T(1,128)S(1)}, f32[1,2048]{1,0:T(1,128)S(1)}, u32[]{:S(2)}, u32[]{:S(2)}) collective-permute-start(f32[1,2048]{1,0:T(1,128)S(1)} %add.254), channel_id=1, source_target_pairs={{0,16},{8,24},{16,0},{24,8},{32,48},{40,56},{48,32},{56,40},{64,80... | collective-permute-start | bytes 24584 | tf_op jit(solution)/shard_map/ppermute | solution.py:40
  106.6 9.5 %collective-permute-start.8 = (f32[1,2048]{1,0:T(1,128)S(1)}, f32[1,2048]{1,0:T(1,128)S(1)}, u32[]{:S(2)}, u32[]{:S(2)}) collective-permute-start(f32[1,2048]{1,0:T(1,128)S(1)} %add.255), channel_id=1, source_target_pairs={{0,32},{8,40},{16,48},{24,56},{32,0},{40,8},{48,16},{56,24},{64,96... | collective-permute-start | bytes 24584 | tf_op jit(solution)/shard_map/ppermute | solution.py:40
  116.1 5.5 %collective-permute-start.9 = (f32[1,2048]{1,0:T(1,128)S(1)}, f32[1,2048]{1,0:T(1,128)S(1)}, u32[]{:S(2)}, u32[]{:S(2)}) collective-permute-start(f32[1,2048]{1,0:T(1,128)S(1)} %add.256), channel_id=1, source_target_pairs={{0,64},{8,72},{16,80},{24,88},{32,96},{40,104},{48,112},{56,120},{... | collective-permute-start | bytes 24584 | tf_op jit(solution)/shard_map/ppermute | solution.py:40
  121.6 6.4 %collective-permute-start.10 = (f32[1,2048]{1,0:T(1,128)S(1)}, f32[1,2048]{1,0:T(1,128)S(1)}, u32[]{:S(2)}, u32[]{:S(2)}) collective-permute-start(f32[1,2048]{1,0:T(1,128)S(1)} %add.257), channel_id=1, source_target_pairs={{0,128},{8,136},{16,144},{24,152},{32,160},{40,168},{48,176},{56,1... | collective-permute-start | bytes 24584 | tf_op jit(solution)/shard_map/ppermute | solution.py:40
  128.1 9.5 %collective-permute-start.11 = (f32[1,2048]{1,0:T(1,128)S(1)}, f32[1,2048]{1,0:T(1,128)S(1)}, u32[]{:S(2)}, u32[]{:S(2)}) collective-permute-start(f32[1,2048]{1,0:T(1,128)S(1)} %add.258), channel_id=1, source_target_pairs={{0,256},{8,264},{16,272},{24,280},{32,288},{40,296},{48,304},{56,3... | collective-permute-start | bytes 24584 | tf_op jit(solution)/shard_map/ppermute | solution.py:40
  137.6 3.4 %copy-start.7 = (bf16[2048,128]{1,0:T(8,128)(2,1)S(1)}, bf16[2048,128]{1,0:T(8,128)(2,1)}, u32[]{:S(2)}) copy-start(bf16[2048,128]{1,0:T(8,128)(2,1)} %copy-done.6) | copy-start | bytes 1572868
  145.0 8.7 %collective-permute-start.12 = (f32[256,128]{1,0:T(8,128)}, f32[256,128]{1,0:T(8,128)}, u32[]{:S(2)}, u32[]{:S(2)}) collective-permute-start(f32[256,128]{1,0:T(8,128)} %constant_dynamic-slice_fusion.2), channel_id=1, source_target_pairs={{0,4},{1,5},{2,6},{3,7},{4,0},{5,1},{6,2},{7,3},{8,12},{9,13},{10,... | collective-permute-start | bytes 393224 | tf_op jit(solution)/shard_map/ppermute | solution.py:54
  152.8 163.9 %copy-start.9 = (bf16[2048,128]{1,0:T(8,128)(2,1)S(1)}, bf16[2048,128]{1,0:T(8,128)(2,1)}, u32[]{:S(2)}) copy-start(bf16[2048,128]{1,0:T(8,128)(2,1)} %param.7) | copy-start | bytes 1572868
  154.6 7.0 %collective-permute-start.13 = (f32[128,128]{1,0:T(8,128)S(1)}, f32[128,128]{1,0:T(8,128)S(1)}, u32[]{:S(2)}, u32[]{:S(2)}) collective-permute-start(f32[128,128]{1,0:T(8,128)S(1)} %constant_dynamic-slice_fusion.1), channel_id=1, source_target_pairs={{0,2},{1,3},{2,0},{3,1},{4,6},{5,7},{6,4},{7,5},{8,10},{9,11},{10,... | collective-permute-start | bytes 196616 | tf_op jit(solution)/shard_map/ppermute | solution.py:54
  161.7 3.1 collective-permute-start.14
  (10 other events, 10.4 us)
Sparse Core Ops, SparseCore 0:
  152.9 163.7 all-reduce.1

commit v3 on v2

--- a/solution.py
+++ b/solution.py
@@ -1,4 +1,5 @@
 import functools
+import itertools
 import math
 
 import jax
@@ -56,7 +57,36 @@
     return block
 
 
-def local(count, width_cols, queries, prototypes, potential, weights, capacity, cotangent):
+def butterfly(block, axis, count, order):
+    where = lax.axis_index(axis)
+    for step in order:
+        half = block.shape[0] // 2
+        bit = (where // step) % 2
+        keep = lax.dynamic_slice_in_dim(block, bit * half, half, 0)
+        send = lax.dynamic_slice_in_dim(block, (1 - bit) * half, half, 0)
+        pairs = [(i, i ^ step) for i in range(count)]
+        block = keep + lax.ppermute(send, axis, pairs)
+    for step in reversed(order):
+        bit = (where // step) % 2
+        pairs = [(i, i ^ step) for i in range(count)]
+        other = lax.ppermute(block, axis, pairs)
+        block = jnp.where(bit == 0, jnp.concatenate([block, other]), jnp.concatenate([other, block]))
+    return block
+
+
+def whole_sum(block, count, inner):
+    bits = [1 << k for k in range(count.bit_length() - 1)]
+    if count & (count - 1) or inner >= count or block.shape[0] % (2 * count):
+        return lax.psum(block, "rows")
+    low = [b for b in bits if b < inner]
+    high = [b for b in bits if b >= inner]
+    half = block.shape[0] // 2
+    first = butterfly(block[:half], "rows", count, low + high)
+    second = butterfly(block[half:], "rows", count, high + low)
+    return jnp.concatenate([first, second])
+
+
+def local(count, inner, width_cols, queries, prototypes, potential, weights, capacity, cotangent):
     qhat, qlen = unit_rows(queries)
     phat, plen = unit_rows(prototypes)
     wgt = weights.astype(jnp.float32)
@@ -142,13 +172,22 @@
         lax.dynamic_slice_in_dim(qhat, begin, piece, 0),
         lax.dynamic_slice_in_dim(qlen, begin, piece, 0),
     )
-    whole = lax.psum(dphat, "rows")
+    whole = whole_sum(dphat, count, inner)
     grad_protos = unit_back(whole, phat, plen)
     return (grad_queries, grad_protos)
+
+
+def inner_of(mesh):
+    column = list(mesh.devices[:, 0])
+    try:
+        lead = column[0].coords[1]
+        return sum(1 for _ in itertools.takewhile(lambda d: d.coords[1] == lead, column))
+    except (AttributeError, IndexError):
+        return len(column)
 
 
 def solution(mesh):
     in_specs = (P("rows", None), P("cols", None), P("cols"), P("rows"), P("cols"), P("rows", None))
     out_specs = (P(("rows", "cols"), None), P("cols", None))
-    body = functools.partial(local, mesh.shape["rows"], mesh.shape["cols"])
+    body = functools.partial(local, mesh.shape["rows"], inner_of(mesh), mesh.shape["cols"])
     return jax.shard_map(body, mesh=mesh, in_specs=in_specs, out_specs=out_specs, check_vma=False)

time: 328 us -> 276 us (0.84); the launches traced: 327 us -> 271 us
  waiting for transfers between devices: 184 us -> 45.9 us
  starting transfers between devices: 69.1 us -> 167 us
  between operations: 14.7 us -> 2.16 us
    psum x1 -> x0, waiting for transfers between devices: 151 us -> none  [local(): whole = lax.psum(dphat, 'rows')]
    ppermute x0 -> x24, starting transfers between devices: none -> 99.5 us  [the longest x12 53 us: butterfly(): block = keep + lax.ppermute(send, axis, pairs)]
    ppermute x0 -> x24, waiting for transfers between devices: none -> 12.8 us  [the longest x12 8.86 us: butterfly(): other = lax.ppermute(block, axis, pairs)]
  transfers between devices with their start and end apart: 16 -> 39, of which waited for: 16 -> 24; matrix products, arithmetic and copies ran while one was open for 1% -> 2% of each run, Pallas kernels for 0% -> 0%
where the time goes in v3:
time: 276 us; the launch traced here: 271 us
  starting transfers between devices  167 us (61%)
  waiting for transfers between devices  45.9 us (17%)
  blocking collectives  27.1 us (10%)
  other arithmetic  16 us (6%)
  matrix products  8.92 us (3%)
  local copies, waits for them, and re-layouts  3.5 us (1%)
    ppermute x12, starting transfers between devices, across_queries(): stack = stack + lax.ppermute(stack, 'rows', pairs)  58.1 us
    ppermute x12, starting transfers between devices, butterfly(): block = keep + lax.ppermute(send, axis, pairs)  53 us
    ppermute x12, starting transfers between devices, butterfly(): other = lax.ppermute(block, axis, pairs)  46.6 us
    ppermute x12, waiting for transfers between devices, across_queries(): stack = stack + lax.ppermute(stack, 'rows', pairs)  28.9 us
    psum x2, blocking collectives, across_slots(): return lax.psum(stack, 'cols')  27.1 us
    ppermute x3, starting transfers between devices, halving_scatter(): block = keep + lax.ppermute(send, axis, pairs)  9.48 us
    ppermute x12, waiting for transfers between devices, butterfly(): other = lax.ppermute(block, axis, pairs)  8.86 us
  transfers between devices with their start and end apart: 39, of which 24 were waited for; matrix products, arithmetic and copies ran while one was open for 2% of the time, Pallas kernels for 0%

profile of v3, /device:TPU:6, one launch (start us, length us, event | category | flops | bytes accessed | tf_op | source)
XLA Modules:
  0.0 270.7 jit_solution(2745926670243902038)
XLA Ops:
  9.9 14.3 %psum.14 = f32[2,512]{1,0:T(2,128)S(1)} all-reduce(f32[2,512]{1,0:T(2,128)S(1)} %pad_maximum_fusion.6), channel_id=1, replica_groups=mesh['rows'=64,'cols'=8] {'cols'}, use_global_device_ids=true, to_apply=%region_10.0 | all-reduce | flops 1024 | bytes 8192 | tf_op jit(solution)/shard_map/psum | solution.py:32
  29.9 3.9 %collective-permute-done = f32[3,2048]{1,0:T(4,128)S(1)} collective-permute-done((f32[3,2048]{1,0:T(4,128)S(1)}, f32[3,2048]{1,0:T(4,128)S(1)}, u32[]{:S(2)}, u32[]{:S(2)}) %collective-permute-start) | collective-permute-done | bytes 24608 | tf_op jit(solution)/shard_map/ppermute | solution.py:41
  36.5 4.1 %collective-permute-done.1 = f32[3,2048]{1,0:T(4,128)S(1)} collective-permute-done((f32[3,2048]{1,0:T(4,128)S(1)}, f32[3,2048]{1,0:T(4,128)S(1)}, u32[]{:S(2)}, u32[]{:S(2)}) %collective-permute-start.1) | collective-permute-done | bytes 24608 | tf_op jit(solution)/shard_map/ppermute | solution.py:41
  40.6 7.6 %collective-permute-start.2 = (f32[3,2048]{1,0:T(4,128)S(1)}, f32[3,2048]{1,0:T(4,128)S(1)}, u32[]{:S(2)}, u32[]{:S(2)}) collective-permute-start(f32[3,2048]{1,0:T(4,128)S(1)} %fusion.81), channel_id=1, source_target_pairs={{0,32},{8,40},{16,48},{24,56},{32,0},{40,8},{48,16},{56,24},{64,96... | collective-permute-start | bytes 73736 | tf_op jit(solution)/shard_map/ppermute | solution.py:41
  56.1 4.3 %collective-permute-start.4 = (f32[3,2048]{1,0:T(4,128)S(1)}, f32[3,2048]{1,0:T(4,128)S(1)}, u32[]{:S(2)}, u32[]{:S(2)}) collective-permute-start(f32[3,2048]{1,0:T(4,128)S(1)} %add.395), channel_id=1, source_target_pairs={{0,128},{8,136},{16,144},{24,152},{32,160},{40,168},{48,176},{56,1... | collective-permute-start | bytes 73736 | tf_op jit(solution)/shard_map/ppermute | solution.py:41
  62.9 7.9 %collective-permute-start.5 = (f32[3,2048]{1,0:T(4,128)S(1)}, f32[3,2048]{1,0:T(4,128)S(1)}, u32[]{:S(2)}, u32[]{:S(2)}) collective-permute-start(f32[3,2048]{1,0:T(4,128)S(1)} %add.396), channel_id=1, source_target_pairs={{0,256},{8,264},{16,272},{24,280},{32,288},{40,296},{48,304},{56,3... | collective-permute-start | bytes 73736 | tf_op jit(solution)/shard_map/ppermute | solution.py:41
  73.4 12.8 %psum.15 = f32[512]{0:T(512)S(1)} all-reduce(f32[512]{0:T(512)S(1)} %add_add_fusion), channel_id=1, replica_groups=mesh['rows'=64,'cols'=8] {'cols'}, use_global_device_ids=true, to_apply=%region_27.0 | all-reduce | flops 512 | bytes 4096 | tf_op jit(solution)/shard_map/psum | solution.py:32
  93.5 3.9 %collective-permute-start.7 = (f32[1,2048]{1,0:T(1,128)S(1)}, f32[1,2048]{1,0:T(1,128)S(1)}, u32[]{:S(2)}, u32[]{:S(2)}) collective-permute-start(f32[1,2048]{1,0:T(1,128)S(1)} %add.402), channel_id=1, source_target_pairs={{0,16},{8,24},{16,0},{24,8},{32,48},{40,56},{48,32},{56,40},{64,80... | collective-permute-start | bytes 24584 | tf_op jit(solution)/shard_map/ppermute | solution.py:41
  100.0 7.6 %collective-permute-start.8 = (f32[1,2048]{1,0:T(1,128)S(1)}, f32[1,2048]{1,0:T(1,128)S(1)}, u32[]{:S(2)}, u32[]{:S(2)}) collective-permute-start(f32[1,2048]{1,0:T(1,128)S(1)} %add.403), channel_id=1, source_target_pairs={{0,32},{8,40},{16,48},{24,56},{32,0},{40,8},{48,16},{56,24},{64,96... | collective-permute-start | bytes 24584 | tf_op jit(solution)/shard_map/ppermute | solution.py:41
  115.0 4.6 %collective-permute-start.10 = (f32[1,2048]{1,0:T(1,128)S(1)}, f32[1,2048]{1,0:T(1,128)S(1)}, u32[]{:S(2)}, u32[]{:S(2)}) collective-permute-start(f32[1,2048]{1,0:T(1,128)S(1)} %add.405), channel_id=1, source_target_pairs={{0,128},{8,136},{16,144},{24,152},{32,160},{40,168},{48,176},{56,1... | collective-permute-start | bytes 24584 | tf_op jit(solution)/shard_map/ppermute | solution.py:41
  121.5 7.9 %collective-permute-start.11 = (f32[1,2048]{1,0:T(1,128)S(1)}, f32[1,2048]{1,0:T(1,128)S(1)}, u32[]{:S(2)}, u32[]{:S(2)}) collective-permute-start(f32[1,2048]{1,0:T(1,128)S(1)} %add.406), channel_id=1, source_target_pairs={{0,256},{8,264},{16,272},{24,280},{32,288},{40,296},{48,304},{56,3... | collective-permute-start | bytes 24584 | tf_op jit(solution)/shard_map/ppermute | solution.py:41
  147.1 4.1 %collective-permute-done.12 = f32[256,128]{1,0:T(8,128)S(1)} collective-permute-done((f32[256,128]{1,0:T(8,128)S(1)}, f32[256,128]{1,0:T(8,128)S(1)}, u32[]{:S(2)}, u32[]{:S(2)}) %collective-permute-start.12) | collective-permute-done | bytes 131104 | tf_op jit(solution)/shard_map/ppermute | solution.py:55
  160.3 4.5 %collective-permute-start.16 = (f32[256,128]{1,0:T(8,128)S(1)}, f32[256,128]{1,0:T(8,128)S(1)}, u32[]{:S(2)}, u32[]{:S(2)}) collective-permute-start(f32[256,128]{1,0:T(8,128)S(1)} %constant_dynamic-slice_fusion.11), channel_id=1, source_target_pairs={{0,16},{8,24},{16,0},{24,8},{32,48},{40,56},{48,32},{56,40},{64,80... | collective-permute-start | bytes 393224 | tf_op jit(solution)/shard_map/ppermute | solution.py:68
  165.1 4.5 %collective-permute-start.28 = (f32[256,128]{1,0:T(8,128)S(1)}, f32[256,128]{1,0:T(8,128)S(1)}, u32[]{:S(2)}, u32[]{:S(2)}) collective-permute-start(f32[256,128]{1,0:T(8,128)S(1)} %constant_dynamic-slice_fusion.5), channel_id=1, source_target_pairs={{0,128},{8,136},{16,144},{24,152},{32,160},{40,168},{48,176},{56,1... | collective-permute-start | bytes 393224 | tf_op jit(solution)/shard_map/ppermute | solution.py:68
  171.9 7.6 %collective-permute-start.17 = (f32[128,128]{1,0:T(8,128)S(1)}, f32[128,128]{1,0:T(8,128)S(1)}, u32[]{:S(2)}, u32[]{:S(2)}) collective-permute-start(f32[128,128]{1,0:T(8,128)S(1)} %constant_dynamic-slice_fusion.10), channel_id=1, source_target_pairs={{0,32},{8,40},{16,48},{24,56},{32,0},{40,8},{48,16},{56,24},{64,96... | collective-permute-start | bytes 196616 | tf_op jit(solution)/shard_map/ppermute | solution.py:68
  179.5 7.9 %collective-permute-start.29 = (f32[128,128]{1,0:T(8,128)S(1)}, f32[128,128]{1,0:T(8,128)S(1)}, u32[]{:S(2)}, u32[]{:S(2)}) collective-permute-start(f32[128,128]{1,0:T(8,128)S(1)} %constant_dynamic-slice_fusion.4), channel_id=1, source_target_pairs={{0,256},{8,264},{16,272},{24,280},{32,288},{40,296},{48,304},{56,3... | collective-permute-start | bytes 196616 | tf_op jit(solution)/shard_map/ppermute | solution.py:68
  197.0 5.0 %collective-permute-start.31 = (f32[32,128]{1,0:T(8,128)S(1)}, f32[32,128]{1,0:T(8,128)S(1)}, u32[]{:S(2)}, u32[]{:S(2)}) collective-permute-start(f32[32,128]{1,0:T(8,128)S(1)} %constant_dynamic-slice_fusion.2), channel_id=1, source_target_pairs={{0,16},{8,24},{16,0},{24,8},{32,48},{40,56},{48,32},{56,40},{64,80... | collective-permute-start | bytes 49160 | tf_op jit(solution)/shard_map/ppermute | solution.py:68
  202.1 5.6 %collective-permute-start.20 = (f32[16,128]{1,0:T(8,128)S(1)}, f32[16,128]{1,0:T(8,128)S(1)}, u32[]{:S(2)}, u32[]{:S(2)}) collective-permute-start(f32[16,128]{1,0:T(8,128)S(1)} %constant_dynamic-slice_fusion.6), channel_id=1, source_target_pairs={{0,256},{8,264},{16,272},{24,280},{32,288},{40,296},{48,304},{56,3... | collective-permute-start | bytes 24584 | tf_op jit(solution)/shard_map/ppermute | solution.py:68
  211.5 5.7 %collective-permute-start.21 = (f32[16,128]{1,0:T(8,128)S(1)}, f32[16,128]{1,0:T(8,128)S(1)}, u32[]{:S(2)}, u32[]{:S(2)}) collective-permute-start(f32[16,128]{1,0:T(8,128)S(1)} %fusion.49), channel_id=1, source_target_pairs={{0,256},{8,264},{16,272},{24,280},{32,288},{40,296},{48,304},{56,3... | collective-permute-start | bytes 24584 | tf_op jit(solution)/shard_map/ppermute | solution.py:72
  217.3 4.4 %collective-permute-start.33 = (f32[16,128]{1,0:T(8,128)S(1)}, f32[16,128]{1,0:T(8,128)S(1)}, u32[]{:S(2)}, u32[]{:S(2)}) collective-permute-start(f32[16,128]{1,0:T(8,128)S(1)} %fusion.50), channel_id=1, source_target_pairs={{0,32},{8,40},{16,48},{24,56},{32,0},{40,8},{48,16},{56,24},{64,96... | collective-permute-start | bytes 24584 | tf_op jit(solution)/shard_map/ppermute | solution.py:72
  226.7 4.4 %collective-permute-start.34 = (f32[32,128]{1,0:T(8,128)S(1)}, f32[32,128]{1,0:T(8,128)S(1)}, u32[]{:S(2)}, u32[]{:S(2)}) collective-permute-start(f32[32,128]{1,0:T(8,128)S(1)} %maximum_select_fusion.11), channel_id=1, source_target_pairs={{0,16},{8,24},{16,0},{24,8},{32,48},{40,56},{48,32},{56,40},{64,80... | collective-permute-start | bytes 49160 | tf_op jit(solution)/shard_map/ppermute | solution.py:72
  240.4 6.8 %collective-permute-start.36 = (f32[128,128]{1,0:T(8,128)S(1)}, f32[128,128]{1,0:T(8,128)S(1)}, u32[]{:S(2)}, u32[]{:S(2)}) collective-permute-start(f32[128,128]{1,0:T(8,128)S(1)} %maximum_select_fusion.7), channel_id=1, source_target_pairs={{0,256},{8,264},{16,272},{24,280},{32,288},{40,296},{48,304},{56,3... | collective-permute-start | bytes 196616 | tf_op jit(solution)/shard_map/ppermute | solution.py:72
  250.6 4.6 %collective-permute-start.37 = (f32[256,128]{1,0:T(8,128)S(1)}, f32[256,128]{1,0:T(8,128)S(1)}, u32[]{:S(2)}, u32[]{:S(2)}) collective-permute-start(f32[256,128]{1,0:T(8,128)S(1)} %maximum_select_fusion.5), channel_id=1, source_target_pairs={{0,128},{8,136},{16,144},{24,152},{32,160},{40,168},{48,176},{56,1... | collective-permute-start | bytes 393224 | tf_op jit(solution)/shard_map/ppermute | solution.py:72
  259.0 4.9 %collective-permute-start.38 = (f32[512,128]{1,0:T(8,128)S(1)}, f32[512,128]{1,0:T(8,128)S(1)}, u32[]{:S(2)}, u32[]{:S(2)}) collective-permute-start(f32[512,128]{1,0:T(8,128)S(1)} %maximum_select_fusion.3), channel_id=1, source_target_pairs={{0,64},{8,72},{16,80},{24,88},{32,96},{40,104},{48,112},{56,120},{... | collective-permute-start | bytes 786440 | tf_op jit(solution)/shard_map/ppermute | solution.py:72
  (191 shorter events, 119.7 us)
Async XLA Ops:
  40.6 9.7 %collective-permute-start.2 = (f32[3,2048]{1,0:T(4,128)S(1)}, f32[3,2048]{1,0:T(4,128)S(1)}, u32[]{:S(2)}, u32[]{:S(2)}) collective-permute-start(f32[3,2048]{1,0:T(4,128)S(1)} %fusion.81), channel_id=1, source_target_pairs={{0,32},{8,40},{16,48},{24,56},{32,0},{40,8},{48,16},{56,24},{64,96... | collective-permute-start | bytes 73736 | tf_op jit(solution)/shard_map/ppermute | solution.py:41
  62.9 9.9 %collective-permute-start.5 = (f32[3,2048]{1,0:T(4,128)S(1)}, f32[3,2048]{1,0:T(4,128)S(1)}, u32[]{:S(2)}, u32[]{:S(2)}) collective-permute-start(f32[3,2048]{1,0:T(4,128)S(1)} %add.396), channel_id=1, source_target_pairs={{0,256},{8,264},{16,272},{24,280},{32,288},{40,296},{48,304},{56,3... | collective-permute-start | bytes 73736 | tf_op jit(solution)/shard_map/ppermute | solution.py:41
  100.0 9.5 %collective-permute-start.8 = (f32[1,2048]{1,0:T(1,128)S(1)}, f32[1,2048]{1,0:T(1,128)S(1)}, u32[]{:S(2)}, u32[]{:S(2)}) collective-permute-start(f32[1,2048]{1,0:T(1,128)S(1)} %add.403), channel_id=1, source_target_pairs={{0,32},{8,40},{16,48},{24,56},{32,0},{40,8},{48,16},{56,24},{64,96... | collective-permute-start | bytes 24584 | tf_op jit(solution)/shard_map/ppermute | solution.py:41
  121.5 9.6 %collective-permute-start.11 = (f32[1,2048]{1,0:T(1,128)S(1)}, f32[1,2048]{1,0:T(1,128)S(1)}, u32[]{:S(2)}, u32[]{:S(2)}) collective-permute-start(f32[1,2048]{1,0:T(1,128)S(1)} %add.406), channel_id=1, source_target_pairs={{0,256},{8,264},{16,272},{24,280},{32,288},{40,296},{48,304},{56,3... | collective-permute-start | bytes 24584 | tf_op jit(solution)/shard_map/ppermute | solution.py:41
  137.3 22.8 %collective-permute-start.15 = (f32[512,128]{1,0:T(8,128)S(1)}, f32[512,128]{1,0:T(8,128)S(1)}, u32[]{:S(2)}, u32[]{:S(2)}) collective-permute-start(f32[512,128]{1,0:T(8,128)S(1)} %fusion.26), channel_id=1, source_target_pairs={{0,8},{8,0},{16,24},{24,16},{32,40},{40,32},{48,56},{56,48},{64,72... | collective-permute-start | bytes 786440 | tf_op jit(solution)/shard_map/ppermute | solution.py:68
  142.8 8.4 %collective-permute-start.12 = (f32[256,128]{1,0:T(8,128)S(1)}, f32[256,128]{1,0:T(8,128)S(1)}, u32[]{:S(2)}, u32[]{:S(2)}) collective-permute-start(f32[256,128]{1,0:T(8,128)S(1)} %constant_dynamic-slice_fusion.14), channel_id=1, source_target_pairs={{0,4},{1,5},{2,6},{3,7},{4,0},{5,1},{6,2},{7,3},{8,12},{9,13},{10,... | collective-permute-start | bytes 393224 | tf_op jit(solution)/shard_map/ppermute | solution.py:55
  155.2 9.7 %collective-permute-start.27 = (f32[512,128]{1,0:T(8,128)S(1)}, f32[512,128]{1,0:T(8,128)S(1)}, u32[]{:S(2)}, u32[]{:S(2)}) collective-permute-start(f32[512,128]{1,0:T(8,128)S(1)} %fusion.23), channel_id=1, source_target_pairs={{0,64},{8,72},{16,80},{24,88},{32,96},{40,104},{48,112},{56,120},{... | collective-permute-start | bytes 786440 | tf_op jit(solution)/shard_map/ppermute | solution.py:68
  158.2 97.0 %collective-permute-start.14 = (f32[64,128]{1,0:T(8,128)S(1)}, f32[64,128]{1,0:T(8,128)S(1)}, u32[]{:S(2)}, u32[]{:S(2)}) collective-permute-start(f32[64,128]{1,0:T(8,128)S(1)} %constant_dynamic-slice_fusion.12), channel_id=1, source_target_pairs={{0,1},{1,0},{2,3},{3,2},{4,5},{5,4},{6,7},{7,6},{8,9},{9,8},{10,11... | collective-permute-start | bytes 98312 | tf_op jit(solution)/shard_map/ppermute | solution.py:55
  160.3 11.5 %collective-permute-start.16 = (f32[256,128]{1,0:T(8,128)S(1)}, f32[256,128]{1,0:T(8,128)S(1)}, u32[]{:S(2)}, u32[]{:S(2)}) collective-permute-start(f32[256,128]{1,0:T(8,128)S(1)} %constant_dynamic-slice_fusion.11), channel_id=1, source_target_pairs={{0,16},{8,24},{16,0},{24,8},{32,48},{40,56},{48,32},{56,40},{64,80... | collective-permute-start | bytes 393224 | tf_op jit(solution)/shard_map/ppermute | solution.py:68
  165.1 14.3 %collective-permute-start.28 = (f32[256,128]{1,0:T(8,128)S(1)}, f32[256,128]{1,0:T(8,128)S(1)}, u32[]{:S(2)}, u32[]{:S(2)}) collective-permute-start(f32[256,128]{1,0:T(8,128)S(1)} %constant_dynamic-slice_fusion.5), channel_id=1, source_target_pairs={{0,128},{8,136},{16,144},{24,152},{32,160},{40,168},{48,176},{56,1... | collective-permute-start | bytes 393224 | tf_op jit(solution)/shard_map/ppermute | solution.py:68
  171.9 15.5 %collective-permute-start.17 = (f32[128,128]{1,0:T(8,128)S(1)}, f32[128,128]{1,0:T(8,128)S(1)}, u32[]{:S(2)}, u32[]{:S(2)}) collective-permute-start(f32[128,128]{1,0:T(8,128)S(1)} %constant_dynamic-slice_fusion.10), channel_id=1, source_target_pairs={{0,32},{8,40},{16,48},{24,56},{32,0},{40,8},{48,16},{56,24},{64,96... | collective-permute-start | bytes 196616 | tf_op jit(solution)/shard_map/ppermute | solution.py:68
  179.5 11.0 %collective-permute-start.29 = (f32[128,128]{1,0:T(8,128)S(1)}, f32[128,128]{1,0:T(8,128)S(1)}, u32[]{:S(2)}, u32[]{:S(2)}) collective-permute-start(f32[128,128]{1,0:T(8,128)S(1)} %constant_dynamic-slice_fusion.4), channel_id=1, source_target_pairs={{0,256},{8,264},{16,272},{24,280},{32,288},{40,296},{48,304},{56,3... | collective-permute-start | bytes 196616 | tf_op jit(solution)/shard_map/ppermute | solution.py:68
  193.2 8.8 %collective-permute-start.19 = (f32[32,128]{1,0:T(8,128)S(1)}, f32[32,128]{1,0:T(8,128)S(1)}, u32[]{:S(2)}, u32[]{:S(2)}) collective-permute-start(f32[32,128]{1,0:T(8,128)S(1)} %constant_dynamic-slice_fusion.8), channel_id=1, source_target_pairs={{0,128},{8,136},{16,144},{24,152},{32,160},{40,168},{48,176},{56,1... | collective-permute-start | bytes 49160 | tf_op jit(solution)/shard_map/ppermute | solution.py:68
  197.0 10.7 %collective-permute-start.31 = (f32[32,128]{1,0:T(8,128)S(1)}, f32[32,128]{1,0:T(8,128)S(1)}, u32[]{:S(2)}, u32[]{:S(2)}) collective-permute-start(f32[32,128]{1,0:T(8,128)S(1)} %constant_dynamic-slice_fusion.2), channel_id=1, source_target_pairs={{0,16},{8,24},{16,0},{24,8},{32,48},{40,56},{48,32},{56,40},{64,80... | collective-permute-start | bytes 49160 | tf_op jit(solution)/shard_map/ppermute | solution.py:68
  202.1 9.5 %collective-permute-start.20 = (f32[16,128]{1,0:T(8,128)S(1)}, f32[16,128]{1,0:T(8,128)S(1)}, u32[]{:S(2)}, u32[]{:S(2)}) collective-permute-start(f32[16,128]{1,0:T(8,128)S(1)} %constant_dynamic-slice_fusion.6), channel_id=1, source_target_pairs={{0,256},{8,264},{16,272},{24,280},{32,288},{40,296},{48,304},{56,3... | collective-permute-start | bytes 24584 | tf_op jit(solution)/shard_map/ppermute | solution.py:68
  207.8 9.5 %collective-permute-start.32 = (f32[16,128]{1,0:T(8,128)S(1)}, f32[16,128]{1,0:T(8,128)S(1)}, u32[]{:S(2)}, u32[]{:S(2)}) collective-permute-start(f32[16,128]{1,0:T(8,128)S(1)} %constant_dynamic-slice_fusion), channel_id=1, source_target_pairs={{0,32},{8,40},{16,48},{24,56},{32,0},{40,8},{48,16},{56,24},{64,96... | collective-permute-start | bytes 24584 | tf_op jit(solution)/shard_map/ppermute | solution.py:68
  211.5 10.2 %collective-permute-start.21 = (f32[16,128]{1,0:T(8,128)S(1)}, f32[16,128]{1,0:T(8,128)S(1)}, u32[]{:S(2)}, u32[]{:S(2)}) collective-permute-start(f32[16,128]{1,0:T(8,128)S(1)} %fusion.49), channel_id=1, source_target_pairs={{0,256},{8,264},{16,272},{24,280},{32,288},{40,296},{48,304},{56,3... | collective-permute-start | bytes 24584 | tf_op jit(solution)/shard_map/ppermute | solution.py:72
  217.3 9.5 %collective-permute-start.33 = (f32[16,128]{1,0:T(8,128)S(1)}, f32[16,128]{1,0:T(8,128)S(1)}, u32[]{:S(2)}, u32[]{:S(2)}) collective-permute-start(f32[16,128]{1,0:T(8,128)S(1)} %fusion.50), channel_id=1, source_target_pairs={{0,32},{8,40},{16,48},{24,56},{32,0},{40,8},{48,16},{56,24},{64,96... | collective-permute-start | bytes 24584 | tf_op jit(solution)/shard_map/ppermute | solution.py:72
  221.7 9.4 %collective-permute-start.22 = (f32[32,128]{1,0:T(8,128)S(1)}, f32[32,128]{1,0:T(8,128)S(1)}, u32[]{:S(2)}, u32[]{:S(2)}) collective-permute-start(f32[32,128]{1,0:T(8,128)S(1)} %maximum_select_fusion.10), channel_id=1, source_target_pairs={{0,128},{8,136},{16,144},{24,152},{32,160},{40,168},{48,176},{56,1... | collective-permute-start | bytes 49160 | tf_op jit(solution)/shard_map/ppermute | solution.py:72
  237.0 10.8 %collective-permute-start.24 = (f32[128,128]{1,0:T(8,128)S(1)}, f32[128,128]{1,0:T(8,128)S(1)}, u32[]{:S(2)}, u32[]{:S(2)}) collective-permute-start(f32[128,128]{1,0:T(8,128)S(1)} %maximum_select_fusion.6), channel_id=1, source_target_pairs={{0,32},{8,40},{16,48},{24,56},{32,0},{40,8},{48,16},{56,24},{64,96... | collective-permute-start | bytes 196616 | tf_op jit(solution)/shard_map/ppermute | solution.py:72
  240.4 10.2 %collective-permute-start.36 = (f32[128,128]{1,0:T(8,128)S(1)}, f32[128,128]{1,0:T(8,128)S(1)}, u32[]{:S(2)}, u32[]{:S(2)}) collective-permute-start(f32[128,128]{1,0:T(8,128)S(1)} %maximum_select_fusion.7), channel_id=1, source_target_pairs={{0,256},{8,264},{16,272},{24,280},{32,288},{40,296},{48,304},{56,3... | collective-permute-start | bytes 196616 | tf_op jit(solution)/shard_map/ppermute | solution.py:72
  247.8 8.8 %collective-permute-start.25 = (f32[256,128]{1,0:T(8,128)S(1)}, f32[256,128]{1,0:T(8,128)S(1)}, u32[]{:S(2)}, u32[]{:S(2)}) collective-permute-start(f32[256,128]{1,0:T(8,128)S(1)} %maximum_select_fusion.4), channel_id=1, source_target_pairs={{0,16},{8,24},{16,0},{24,8},{32,48},{40,56},{48,32},{56,40},{64,80... | collective-permute-start | bytes 393224 | tf_op jit(solution)/shard_map/ppermute | solution.py:72
  250.6 8.4 %collective-permute-start.37 = (f32[256,128]{1,0:T(8,128)S(1)}, f32[256,128]{1,0:T(8,128)S(1)}, u32[]{:S(2)}, u32[]{:S(2)}) collective-permute-start(f32[256,128]{1,0:T(8,128)S(1)} %maximum_select_fusion.5), channel_id=1, source_target_pairs={{0,128},{8,136},{16,144},{24,152},{32,160},{40,168},{48,176},{56,1... | collective-permute-start | bytes 393224 | tf_op jit(solution)/shard_map/ppermute | solution.py:72
  259.0 9.2 %collective-permute-start.38 = (f32[512,128]{1,0:T(8,128)S(1)}, f32[512,128]{1,0:T(8,128)S(1)}, u32[]{:S(2)}, u32[]{:S(2)}) collective-permute-start(f32[512,128]{1,0:T(8,128)S(1)} %maximum_select_fusion.3), channel_id=1, source_target_pairs={{0,64},{8,72},{16,80},{24,88},{32,96},{40,104},{48,112},{56,120},{... | collective-permute-start | bytes 786440 | tf_op jit(solution)/shard_map/ppermute | solution.py:72
  (30 other events, 177.8 us)

commit v4 on v3

--- a/solution.py
+++ b/solution.py
@@ -32,7 +32,19 @@
     return lax.psum(stack, "cols")
 
 
+def exchange_sum(stack, axis, count):
+    pieces = lax.all_to_all(stack.reshape(count, -1), axis, 0, 0)
+    return jnp.sum(pieces, axis=0)
+
+
+def exchange_gather(piece, axis, count, shape):
+    copies = jnp.broadcast_to(piece.reshape(1, -1), (count, piece.size))
+    return lax.all_to_all(copies, axis, 0, 0).reshape(shape)
+
+
 def across_queries(stack, count):
+    if stack.size % count == 0:
+        return exchange_gather(exchange_sum(stack, "rows", count), "rows", count, stack.shape)
     if count & (count - 1):
         return lax.psum(stack, "rows")
     step = 1
@@ -161,10 +173,10 @@
         )
         dp_parts.append(part)
     dphat = jnp.concatenate(dp_parts, axis=0)
-    if width_cols & (width_cols - 1) or local_rows % width_cols:
+    if local_rows % width_cols:
         query_part = lax.psum_scatter(dqhat, "cols", scatter_dimension=0, tiled=True)
     else:
-        query_part = halving_scatter(dqhat, "cols", width_cols)
+        query_part = exchange_sum(dqhat, "cols", width_cols).reshape(-1, dqhat.shape[1])
     piece = query_part.shape[0]
     begin = lax.axis_index("cols") * piece
     grad_queries = unit_back(
@@ -172,8 +184,18 @@
         lax.dynamic_slice_in_dim(qhat, begin, piece, 0),
         lax.dynamic_slice_in_dim(qlen, begin, piece, 0),
     )
-    whole = whole_sum(dphat, count, inner)
-    grad_protos = unit_back(whole, phat, plen)
+    if slots % count:
+        grad_protos = unit_back(whole_sum(dphat, count, inner), phat, plen)
+    else:
+        own = slots // count
+        first = lax.axis_index("rows") * own
+        summed = exchange_sum(dphat, "rows", count).reshape(own, dphat.shape[1])
+        piece = unit_back(
+            summed,
+            lax.dynamic_slice_in_dim(phat, first, own, 0),
+            lax.dynamic_slice_in_dim(plen, first, own, 0),
+        )
+        grad_protos = exchange_gather(piece, "rows", count, dphat.shape)
     return (grad_queries, grad_protos)
 
 

time: 276 us -> 216 us (0.78)
  starting transfers between devices: 167 us -> 17.7 us
  blocking collectives: 27.1 us -> 99.3 us
  waiting for transfers between devices: 45.9 us -> 56.9 us
  local copies, waits for them, and re-layouts: 3.5 us -> 10.4 us
    ppermute x39 -> x0, starting transfers between devices: 167 us -> none  [the longest x12 58.1 us: across_queries(): stack = stack + lax.ppermute(stack, 'rows', pairs)]
    all_to_all x0 -> x4, blocking collectives: none -> 72.2 us  [the longest x2 40.7 us: exchange_sum(): pieces = lax.all_to_all(stack.reshape(count, -1), axis, 0, 0)]
    all_to_all x0 -> x3, waiting for transfers between devices: none -> 56.9 us  [the longest x2 28.7 us: exchange_sum(): pieces = lax.all_to_all(stack.reshape(count, -1), axis, 0, 0)]
    ppermute x39 -> x0, waiting for transfers between devices: 45.9 us -> none  [the longest x12 28.9 us: across_queries(): stack = stack + lax.ppermute(stack, 'rows', pairs)]
    all_to_all x0 -> x3, starting transfers between devices: none -> 17.7 us  [the longest x2 11.2 us: exchange_sum(): pieces = lax.all_to_all(stack.reshape(count, -1), axis, 0, 0)]
    unnamed x30 -> x43, local copies, waits for them, and re-layouts: 3.24 us -> 7.05 us
  transfers between devices with their start and end apart: 39 -> 3, of which waited for: 24 -> 3; matrix products, arithmetic and copies ran while one was open for 2% -> 2% of each run, Pallas kernels for 0% -> 0%
where the time goes in v4:
time: 216 us; the launch traced here: 213 us
  blocking collectives  99.3 us (46%)
  waiting for transfers between devices  56.9 us (26%)
  other arithmetic  18 us (8%)
  starting transfers between devices  17.7 us (8%)
  local copies, waits for them, and re-layouts  10.4 us (5%)
  matrix products  9.59 us (4%)
    all_to_all x2, blocking collectives, exchange_sum(): pieces = lax.all_to_all(stack.reshape(count, -1), axis, 0, 0)  40.7 us
    all_to_all x2, blocking collectives, exchange_gather(): return lax.all_to_all(copies, axis, 0, 0).reshape(shape)  31.5 us
    all_to_all x2, waiting for transfers between devices, exchange_sum(): pieces = lax.all_to_all(stack.reshape(count, -1), axis, 0, 0)  28.7 us
    all_to_all x1, waiting for transfers between devices, exchange_gather(): return lax.all_to_all(copies, axis, 0, 0).reshape(shape)  28.2 us
    psum x2, blocking collectives, across_slots(): return lax.psum(stack, 'cols')  27.1 us
    all_to_all x2, starting transfers between devices, exchange_sum(): pieces = lax.all_to_all(stack.reshape(count, -1), axis, 0, 0)  11.2 us
    unnamed x43, local copies, waits for them, and re-layouts  7.05 us
    all_to_all x1, starting transfers between devices, exchange_gather(): return lax.all_to_all(copies, axis, 0, 0).reshape(shape)  6.48 us
  transfers between devices with their start and end apart: 3, of which 3 were waited for; matrix products, arithmetic and copies ran while one was open for 2% of the time, Pallas kernels for 0%

profile of v4, /device:TPU:6, one launch (start us, length us, event | category | flops | bytes accessed | tf_op | source)
XLA Modules:
  0.0 212.9 jit_solution(14117261469635978862)
XLA Ops:
  1.4 1.4 fusion.12
  8.5 1.4 fusion.44
  10.5 14.3 %psum.14 = f32[2,512]{1,0:T(2,128)S(1)} all-reduce(f32[2,512]{1,0:T(2,128)S(1)} %pad_maximum_fusion.6), channel_id=1, replica_groups=mesh['rows'=64,'cols'=8] {'cols'}, use_global_device_ids=true, to_apply=%region_10.0 | all-reduce | flops 1024 | bytes 8192 | tf_op jit(solution)/shard_map/psum | solution.py:32
  25.5 3.5 %multiply_reduce_fusion.20 = (f32[512]{0:T(512)S(1)}, f32[512]{0:T(512)S(1)}, f32[512]{0:T(512)S(1)}, f32[512]{0:T(512)S(1)}, f32[512]{0:T(512)S(1)}, /*index=5*...) fusion(f32[512,512]{1,0:T(8,128)S(1)} %get-tuple-element.67, ...), kind=kLoop, calls=%fused_computation.53 | loop fusion | flops 6285312 | bytes 8417280 | tf_op jit(solution)/shard_map/reduce_sum | solution.py:134
  29.3 24.9 %all_to_all.54 = f32[64,1,96]{2,1,0:T(1,128)S(1)} all-to-all(f32[64,1,96]{2,1,0:T(1,128)S(1)} %all_to_all.36), channel_id=1, replica_groups=mesh['rows'=64,'cols'=8] {'rows'}, dimensions={0} | all-to-all | bytes 49152 | tf_op jit(solution)/shard_map/all_to_all | solution.py:36
  54.3 15.8 %all_to_all.55 = f32[64,1,96]{2,1,0:T(1,128)S(1)} all-to-all(f32[64,1,96]{2,1,0:T(1,128)S(1)} %broadcast_in_dim.8), channel_id=1, replica_groups=mesh['rows'=64,'cols'=8] {'rows'}, dimensions={0} | all-to-all | bytes 49152 | tf_op jit(solution)/shard_map/all_to_all | solution.py:42
  71.4 1.8 multiply_reduce_fusion.6
  73.2 12.7 %psum.15 = f32[512]{0:T(512)S(1)} all-reduce(f32[512]{0:T(512)S(1)} %add_add_fusion), channel_id=1, replica_groups=mesh['rows'=64,'cols'=8] {'cols'}, use_global_device_ids=true, to_apply=%region_28.0 | all-reduce | flops 512 | bytes 4096 | tf_op jit(solution)/shard_map/psum | solution.py:32
  86.0 1.7 multiply_reduce_fusion.3
  88.1 15.8 %all_to_all.56 = f32[64,1,32]{2,1,0:T(1,128)S(1)} all-to-all(f32[64,1,32]{2,1,0:T(1,128)S(1)} %bitcast.39), channel_id=1, replica_groups=mesh['rows'=64,'cols'=8] {'rows'}, dimensions={0} | all-to-all | bytes 16384 | tf_op jit(solution)/shard_map/all_to_all | solution.py:36
  103.9 15.8 %all_to_all.57 = f32[64,1,32]{2,1,0:T(1,128)S(1)} all-to-all(f32[64,1,32]{2,1,0:T(1,128)S(1)} %broadcast_in_dim.9), channel_id=1, replica_groups=mesh['rows'=64,'cols'=8] {'rows'}, dimensions={0} | all-to-all | bytes 16384 | tf_op jit(solution)/shard_map/all_to_all | solution.py:42
  120.6 3.4 %multiply_convert_fusion = (bf16[512,512]{1,0:T(8,128)(2,1)S(1)}, bf16[512,512]{1,0:T(8,128)(2,1)S(1)}, bf16[512,512]{1,0:T(8,128)(2,1)S(1)}, bf16[512,512]{1,0:T(8,128)(2,1)S(1)}) fusion(f32[512,512]{1,0:T(8,128)} %copy-done.4, f32[512,512]{1,0:T(8,128)S(1)} %get-tuple-element.67, f32[512]{0:T(512)S(1)} %get-tuple-element.45, ...), kind=kLoop, calls=%fused_computation.28 | loop fusion | flops 6291456 | bytes 10498048 | tf_op jit(solution)/shard_map/convert_element_type | solution.py:163
  128.0 1.0 pad_maximum_fusion
  129.1 4.8 %all-to-all-start.5 = ((f32[64,1,4096]{2,1,0:T(1,128)}), f32[64,1,4096]{2,1,0:T(1,128)S(1)}, u32[]{:S(2)}, u32[]{:S(2)}) async-start(f32[64,1,4096]{2,1,0:T(1,128)} %bitcast.13), calls=%async_computation.5 | async-start | bytes 2097152 | tf_op jit(solution)/shard_map/all_to_all | solution.py:36
  136.3 0.7 copy-done.11
  137.0 1.0 convolution_add_fusion.4
  138.0 24.3 %all-to-all-done.5 = f32[64,1,4096]{2,1,0:T(1,128)S(1)} async-done(((f32[64,1,4096]{2,1,0:T(1,128)}), f32[64,1,4096]{2,1,0:T(1,128)S(1)}, u32[]{:S(2)}, u32[]{:S(2)}) %all-to-all-start.5) | async-done | bytes 1048608 | tf_op jit(solution)/shard_map/all_to_all | solution.py:36
  162.3 6.4 %all-to-all-start.4 = ((f32[8,1,8192]{2,1,0:T(1,128)}), f32[8,1,8192]{2,1,0:T(1,128)S(1)}, u32[]{:S(2)}, u32[]{:S(2)}) async-start(f32[8,1,8192]{2,1,0:T(1,128)} %bitcast.11), calls=%async_computation.4 | async-start | bytes 524288 | tf_op jit(solution)/shard_map/all_to_all | solution.py:36
  168.7 0.9 reduce_sum.358
  169.8 4.4 %all-to-all-done.4 = f32[8,1,8192]{2,1,0:T(1,128)S(1)} async-done(((f32[8,1,8192]{2,1,0:T(1,128)}), f32[8,1,8192]{2,1,0:T(1,128)S(1)}, u32[]{:S(2)}, u32[]{:S(2)}) %all-to-all-start.4) | async-done | bytes 262176 | tf_op jit(solution)/shard_map/all_to_all | solution.py:36
  174.2 2.0 broadcast_in_dim.11
  176.1 6.5 %all-to-all-start.6 = ((f32[64,1,4096]{2,1,0:T(1,128)}), f32[64,1,4096]{2,1,0:T(1,128)S(1)}, u32[]{:S(2)}, u32[]{:S(2)}) async-start(f32[64,1,4096]{2,1,0:T(1,128)} %broadcast_in_dim.11), calls=%async_computation.6 | async-start | bytes 2097152 | tf_op jit(solution)/shard_map/all_to_all | solution.py:42
  183.7 28.2 %all-to-all-done.6 = f32[64,1,4096]{2,1,0:T(1,128)S(1)} async-done(((f32[64,1,4096]{2,1,0:T(1,128)}), f32[64,1,4096]{2,1,0:T(1,128)S(1)}, u32[]{:S(2)}, u32[]{:S(2)}) %all-to-all-start.6) | async-done | bytes 1048608 | tf_op jit(solution)/shard_map/all_to_all | solution.py:42
  212.0 1.0 copy.11
  (104 shorter events, 18.2 us)
Async XLA Ops:
  0.6 2.2 %copy-start.16 = (bf16[2048,128]{1,0:T(8,128)(2,1)S(1)}, bf16[2048,128]{1,0:T(8,128)(2,1)}, u32[]{:S(2)}) copy-start(bf16[2048,128]{1,0:T(8,128)(2,1)} %param.7) | copy-start | bytes 1572868
  2.8 0.9 copy-start.7
  3.7 6.2 %copy-start.5 = (bf16[2048,128]{1,0:T(8,128)(2,1)}, bf16[2048,128]{1,0:T(8,128)(2,1)S(1)}, u32[]{:S(2)}) copy-start(bf16[2048,128]{1,0:T(8,128)(2,1)S(1)} %fusion.13) | copy-start | bytes 1572868
  4.1 5.9 %copy-start.1 = (f32[512,512]{1,0:T(8,128)}, f32[512,512]{1,0:T(8,128)S(1)}, u32[]{:S(2)}) copy-start(f32[512,512]{1,0:T(8,128)S(1)} %fusion.34) | copy-start | bytes 3145732
  4.4 4.1 %copy-start.2 = (f32[512,512]{1,0:T(8,128)}, f32[512,512]{1,0:T(8,128)S(1)}, u32[]{:S(2)}) copy-start(f32[512,512]{1,0:T(8,128)S(1)} %fusion.29) | copy-start | bytes 3145732
  4.8 3.2 %copy-start.3 = (f32[512,512]{1,0:T(8,128)}, f32[512,512]{1,0:T(8,128)S(1)}, u32[]{:S(2)}) copy-start(f32[512,512]{1,0:T(8,128)S(1)} %fusion.25) | copy-start | bytes 3145732
  4.8 1.0 copy-start.17
  5.9 2.1 copy-start.4
  5.9 0.7 copy-start.19
  6.6 0.7 copy-start.20
  24.9 0.7 copy-start.18
  123.9 0.9 copy-start.10
  123.9 1.0 copy-start.14
  123.9 2.4 %copy-start.12 = (bf16[512,512]{1,0:T(8,128)(2,1)}, bf16[512,512]{1,0:T(8,128)(2,1)S(1)}, u32[]{:S(2)}) copy-start(bf16[512,512]{1,0:T(8,128)(2,1)S(1)} %get-tuple-element.63) | copy-start | bytes 1572868
  124.0 3.3 %copy-start.8 = (bf16[512,512]{1,0:T(8,128)(2,1)}, bf16[512,512]{1,0:T(8,128)(2,1)S(1)}, u32[]{:S(2)}) copy-start(bf16[512,512]{1,0:T(8,128)(2,1)S(1)} %get-tuple-element.64) | copy-start | bytes 1572868
  124.3 1.6 copy-start
  129.1 4.9 %copy-start.6 = (bf16[2048,128]{1,0:T(8,128)(2,1)S(1)}, bf16[2048,128]{1,0:T(8,128)(2,1)}, u32[]{:S(2)}) copy-start(bf16[2048,128]{1,0:T(8,128)(2,1)} %copy-done.5) | copy-start | bytes 1572868
  129.1 4.9 %copy-start.9 = (bf16[512,512]{1,0:T(8,128)(2,1)S(1)}, bf16[512,512]{1,0:T(8,128)(2,1)}, u32[]{:S(2)}) copy-start(bf16[512,512]{1,0:T(8,128)(2,1)} %copy-done.8) | copy-start | bytes 1572868
  129.1 33.2 %all-to-all-start.5 = ((f32[64,1,4096]{2,1,0:T(1,128)}), f32[64,1,4096]{2,1,0:T(1,128)S(1)}, u32[]{:S(2)}, u32[]{:S(2)}) async-start(f32[64,1,4096]{2,1,0:T(1,128)} %bitcast.13), calls=%async_computation.5 | async-start | bytes 2097152 | tf_op jit(solution)/shard_map/all_to_all | solution.py:36
  133.9 1.0 copy-start.15
  134.9 1.0 copy-start.13
  136.0 1.0 copy-start.11
  162.3 11.9 %all-to-all-start.4 = ((f32[8,1,8192]{2,1,0:T(1,128)}), f32[8,1,8192]{2,1,0:T(1,128)S(1)}, u32[]{:S(2)}, u32[]{:S(2)}) async-start(f32[8,1,8192]{2,1,0:T(1,128)} %bitcast.11), calls=%async_computation.4 | async-start | bytes 524288 | tf_op jit(solution)/shard_map/all_to_all | solution.py:36
  176.1 35.8 %all-to-all-start.6 = ((f32[64,1,4096]{2,1,0:T(1,128)}), f32[64,1,4096]{2,1,0:T(1,128)S(1)}, u32[]{:S(2)}, u32[]{:S(2)}) async-start(f32[64,1,4096]{2,1,0:T(1,128)} %broadcast_in_dim.11), calls=%async_computation.6 | async-start | bytes 2097152 | tf_op jit(solution)/shard_map/all_to_all | solution.py:42

commit v5 on v4

--- a/solution.py
+++ b/solution.py
@@ -176,7 +176,7 @@
     if local_rows % width_cols:
         query_part = lax.psum_scatter(dqhat, "cols", scatter_dimension=0, tiled=True)
     else:
-        query_part = exchange_sum(dqhat, "cols", width_cols).reshape(-1, dqhat.shape[1])
+        query_part = halving_scatter(dqhat, "cols", width_cols)
     piece = query_part.shape[0]
     begin = lax.axis_index("cols") * piece
     grad_queries = unit_back(

time: 216 us -> 205 us (0.949)
  waiting for transfers between devices: 56.9 us -> 46.7 us
    all_to_all x1, waiting for transfers between devices: 28.2 us -> 8.09 us  [exchange_gather(): return lax.all_to_all(copies, axis, 0, 0).reshape(shape)]
    ppermute x0 -> x3, waiting for transfers between devices: none -> 10.7 us  [halving_scatter(): block = keep + lax.ppermute(send, axis, pairs)]
    ppermute x0 -> x3, starting transfers between devices: none -> 6.79 us  [halving_scatter(): block = keep + lax.ppermute(send, axis, pairs)]
    all_to_all x2 -> x1, starting transfers between devices: 11.2 us -> 4.79 us  [exchange_sum(): pieces = lax.all_to_all(stack.reshape(count, -1), axis, 0, 0)]
    all_to_all x2 -> x1, waiting for transfers between devices: 28.7 us -> 28 us  [exchange_sum(): pieces = lax.all_to_all(stack.reshape(count, -1), axis, 0, 0)]
  transfers between devices with their start and end apart: 3 -> 5, of which waited for: 3 -> 5; matrix products, arithmetic and copies ran while one was open for 2% -> 1% of each run, Pallas kernels for 0% -> 0%
where the time goes in v5:
time: 205 us; the launch traced here: 202 us
  blocking collectives  99.3 us (48%)
  waiting for transfers between devices  46.7 us (23%)
  starting transfers between devices  18.4 us (9%)
  other arithmetic  17.9 us (9%)
  local copies, waits for them, and re-layouts  9.78 us (5%)
  matrix products  8.89 us (4%)
    all_to_all x2, blocking collectives, exchange_sum(): pieces = lax.all_to_all(stack.reshape(count, -1), axis, 0, 0)  40.7 us
    all_to_all x2, blocking collectives, exchange_gather(): return lax.all_to_all(copies, axis, 0, 0).reshape(shape)  31.5 us
    all_to_all x1, waiting for transfers between devices, exchange_sum(): pieces = lax.all_to_all(stack.reshape(count, -1), axis, 0, 0)  28 us
    psum x2, blocking collectives, across_slots(): return lax.psum(stack, 'cols')  27.1 us
    ppermute x3, waiting for transfers between devices, halving_scatter(): block = keep + lax.ppermute(send, axis, pairs)  10.7 us
    all_to_all x1, waiting for transfers between devices, exchange_gather(): return lax.all_to_all(copies, axis, 0, 0).reshape(shape)  8.09 us
    all_to_all x1, starting transfers between devices, exchange_gather(): return lax.all_to_all(copies, axis, 0, 0).reshape(shape)  6.83 us
    ppermute x3, starting transfers between devices, halving_scatter(): block = keep + lax.ppermute(send, axis, pairs)  6.79 us
  transfers between devices with their start and end apart: 5, of which 5 were waited for; matrix products, arithmetic and copies ran while one was open for 1% of the time, Pallas kernels for 0%

profile of v5, /device:TPU:6, one launch (start us, length us, event | category | flops | bytes accessed | tf_op | source)
XLA Modules:
  0.0 202.2 jit_solution(4456585136479199132)
XLA Ops:
  1.4 1.4 fusion.12
  8.5 1.4 fusion.44
  10.5 14.3 %psum.14 = f32[2,512]{1,0:T(2,128)S(1)} all-reduce(f32[2,512]{1,0:T(2,128)S(1)} %pad_maximum_fusion.6), channel_id=1, replica_groups=mesh['rows'=64,'cols'=8] {'cols'}, use_global_device_ids=true, to_apply=%region_10.0 | all-reduce | flops 1024 | bytes 8192 | tf_op jit(solution)/shard_map/psum | solution.py:32
  25.5 3.5 %multiply_reduce_fusion.20 = (f32[512]{0:T(512)S(1)}, f32[512]{0:T(512)S(1)}, f32[512]{0:T(512)S(1)}, f32[512]{0:T(512)S(1)}, f32[512]{0:T(512)S(1)}, /*index=5*...) fusion(f32[512,512]{1,0:T(8,128)S(1)} %get-tuple-element.67, ...), kind=kLoop, calls=%fused_computation.53 | loop fusion | flops 6285312 | bytes 8417280 | tf_op jit(solution)/shard_map/reduce_sum | solution.py:134
  29.3 24.9 %all_to_all.45 = f32[64,1,96]{2,1,0:T(1,128)S(1)} all-to-all(f32[64,1,96]{2,1,0:T(1,128)S(1)} %all_to_all.30), channel_id=1, replica_groups=mesh['rows'=64,'cols'=8] {'rows'}, dimensions={0} | all-to-all | bytes 49152 | tf_op jit(solution)/shard_map/all_to_all | solution.py:36
  54.3 15.8 %all_to_all.46 = f32[64,1,96]{2,1,0:T(1,128)S(1)} all-to-all(f32[64,1,96]{2,1,0:T(1,128)S(1)} %broadcast_in_dim.8), channel_id=1, replica_groups=mesh['rows'=64,'cols'=8] {'rows'}, dimensions={0} | all-to-all | bytes 49152 | tf_op jit(solution)/shard_map/all_to_all | solution.py:42
  71.4 1.8 multiply_reduce_fusion.6
  73.2 12.7 %psum.15 = f32[512]{0:T(512)S(1)} all-reduce(f32[512]{0:T(512)S(1)} %add_add_fusion), channel_id=1, replica_groups=mesh['rows'=64,'cols'=8] {'cols'}, use_global_device_ids=true, to_apply=%region_28.0 | all-reduce | flops 512 | bytes 4096 | tf_op jit(solution)/shard_map/psum | solution.py:32
  86.0 1.7 multiply_reduce_fusion.3
  88.0 15.8 %all_to_all.47 = f32[64,1,32]{2,1,0:T(1,128)S(1)} all-to-all(f32[64,1,32]{2,1,0:T(1,128)S(1)} %bitcast.35), channel_id=1, replica_groups=mesh['rows'=64,'cols'=8] {'rows'}, dimensions={0} | all-to-all | bytes 16384 | tf_op jit(solution)/shard_map/all_to_all | solution.py:36
  103.9 15.8 %all_to_all.48 = f32[64,1,32]{2,1,0:T(1,128)S(1)} all-to-all(f32[64,1,32]{2,1,0:T(1,128)S(1)} %broadcast_in_dim.9), channel_id=1, replica_groups=mesh['rows'=64,'cols'=8] {'rows'}, dimensions={0} | all-to-all | bytes 16384 | tf_op jit(solution)/shard_map/all_to_all | solution.py:42
  120.6 3.4 %multiply_convert_fusion = (bf16[512,512]{1,0:T(8,128)(2,1)S(1)}, bf16[512,512]{1,0:T(8,128)(2,1)S(1)}, bf16[512,512]{1,0:T(8,128)(2,1)S(1)}, bf16[512,512]{1,0:T(8,128)(2,1)S(1)}) fusion(f32[512,512]{1,0:T(8,128)} %copy-done.4, f32[512,512]{1,0:T(8,128)S(1)} %get-tuple-element.67, f32[512]{0:T(512)S(1)} %get-tuple-element.45, ...), kind=kLoop, calls=%fused_computation.28 | loop fusion | flops 6291456 | bytes 10498048 | tf_op jit(solution)/shard_map/convert_element_type | solution.py:163
  128.1 1.0 pad_maximum_fusion
  129.1 4.8 %all-to-all-start.4 = ((f32[64,1,4096]{2,1,0:T(1,128)}), f32[64,1,4096]{2,1,0:T(1,128)S(1)}, u32[]{:S(2)}, u32[]{:S(2)}) async-start(f32[64,1,4096]{2,1,0:T(1,128)} %bitcast.11), calls=%async_computation.4 | async-start | bytes 2097152 | tf_op jit(solution)/shard_map/all_to_all | solution.py:36
  134.3 28.0 %all-to-all-done.4 = f32[64,1,4096]{2,1,0:T(1,128)S(1)} async-done(((f32[64,1,4096]{2,1,0:T(1,128)}), f32[64,1,4096]{2,1,0:T(1,128)S(1)}, u32[]{:S(2)}, u32[]{:S(2)}) %all-to-all-start.4) | async-done | bytes 1048608 | tf_op jit(solution)/shard_map/all_to_all | solution.py:36
  163.3 2.0 broadcast_in_dim.11
  165.3 6.8 %all-to-all-start.5 = ((f32[64,1,4096]{2,1,0:T(1,128)}), f32[64,1,4096]{2,1,0:T(1,128)S(1)}, u32[]{:S(2)}, u32[]{:S(2)}) async-start(f32[64,1,4096]{2,1,0:T(1,128)} %broadcast_in_dim.11), calls=%async_computation.5 | async-start | bytes 2097152 | tf_op jit(solution)/shard_map/all_to_all | solution.py:42
  174.6 2.8 %collective-permute-start = (f32[256,128]{1,0:T(8,128)S(1)}, f32[256,128]{1,0:T(8,128)S(1)}, u32[]{:S(2)}, u32[]{:S(2)}) collective-permute-start(f32[256,128]{1,0:T(8,128)S(1)} %constant_dynamic-slice_fusion.2), channel_id=1, source_target_pairs={{0,4},{1,5},{2,6},{3,7},{4,0},{5,1},{6,2},{7,3},{8,12},{9,13},{10,... | collective-permute-start | bytes 393224 | tf_op jit(solution)/shard_map/ppermute | solution.py:67
  177.4 5.6 %collective-permute-done = f32[256,128]{1,0:T(8,128)S(1)} collective-permute-done((f32[256,128]{1,0:T(8,128)S(1)}, f32[256,128]{1,0:T(8,128)S(1)}, u32[]{:S(2)}, u32[]{:S(2)}) %collective-permute-start) | collective-permute-done | bytes 131104 | tf_op jit(solution)/shard_map/ppermute | solution.py:67
  183.0 2.1 %collective-permute-start.1 = (f32[128,128]{1,0:T(8,128)S(1)}, f32[128,128]{1,0:T(8,128)S(1)}, u32[]{:S(2)}, u32[]{:S(2)}) collective-permute-start(f32[128,128]{1,0:T(8,128)S(1)} %constant_dynamic-slice_fusion.1), channel_id=1, source_target_pairs={{0,2},{1,3},{2,0},{3,1},{4,6},{5,7},{6,4},{7,5},{8,10},{9,11},{10,... | collective-permute-start | bytes 196616 | tf_op jit(solution)/shard_map/ppermute | solution.py:67
  185.1 4.0 %collective-permute-done.1 = f32[128,128]{1,0:T(8,128)S(1)} collective-permute-done((f32[128,128]{1,0:T(8,128)S(1)}, f32[128,128]{1,0:T(8,128)S(1)}, u32[]{:S(2)}, u32[]{:S(2)}) %collective-permute-start.1) | collective-permute-done | bytes 65568 | tf_op jit(solution)/shard_map/ppermute | solution.py:67
  189.2 1.9 collective-permute-start.2
  191.2 1.1 collective-permute-done.2
  193.1 8.1 %all-to-all-done.5 = f32[64,1,4096]{2,1,0:T(1,128)S(1)} async-done(((f32[64,1,4096]{2,1,0:T(1,128)}), f32[64,1,4096]{2,1,0:T(1,128)S(1)}, u32[]{:S(2)}, u32[]{:S(2)}) %all-to-all-start.5) | async-done | bytes 1048608 | tf_op jit(solution)/shard_map/all_to_all | solution.py:42
  (112 shorter events, 20.3 us)
Async XLA Ops:
  0.6 2.2 %copy-start.16 = (bf16[2048,128]{1,0:T(8,128)(2,1)S(1)}, bf16[2048,128]{1,0:T(8,128)(2,1)}, u32[]{:S(2)}) copy-start(bf16[2048,128]{1,0:T(8,128)(2,1)} %param.7) | copy-start | bytes 1572868
  2.8 0.9 copy-start.7
  3.7 6.2 %copy-start.5 = (bf16[2048,128]{1,0:T(8,128)(2,1)}, bf16[2048,128]{1,0:T(8,128)(2,1)S(1)}, u32[]{:S(2)}) copy-start(bf16[2048,128]{1,0:T(8,128)(2,1)S(1)} %fusion.13) | copy-start | bytes 1572868
  4.1 5.9 %copy-start.1 = (f32[512,512]{1,0:T(8,128)}, f32[512,512]{1,0:T(8,128)S(1)}, u32[]{:S(2)}) copy-start(f32[512,512]{1,0:T(8,128)S(1)} %fusion.34) | copy-start | bytes 3145732
  4.4 4.1 %copy-start.2 = (f32[512,512]{1,0:T(8,128)}, f32[512,512]{1,0:T(8,128)S(1)}, u32[]{:S(2)}) copy-start(f32[512,512]{1,0:T(8,128)S(1)} %fusion.29) | copy-start | bytes 3145732
  4.8 3.2 %copy-start.3 = (f32[512,512]{1,0:T(8,128)}, f32[512,512]{1,0:T(8,128)S(1)}, u32[]{:S(2)}) copy-start(f32[512,512]{1,0:T(8,128)S(1)} %fusion.25) | copy-start | bytes 3145732
  4.8 1.0 copy-start.17
  5.9 2.1 %copy-start.4 = (f32[512,512]{1,0:T(8,128)}, f32[512,512]{1,0:T(8,128)S(1)}, u32[]{:S(2)}) copy-start(f32[512,512]{1,0:T(8,128)S(1)} %fusion.21) | copy-start | bytes 3145732
  5.9 0.7 copy-start.19
  123.9 0.9 copy-start.10
  123.9 1.0 copy-start.14
  123.9 2.4 %copy-start.12 = (bf16[512,512]{1,0:T(8,128)(2,1)}, bf16[512,512]{1,0:T(8,128)(2,1)S(1)}, u32[]{:S(2)}) copy-start(bf16[512,512]{1,0:T(8,128)(2,1)S(1)} %get-tuple-element.63) | copy-start | bytes 1572868
  124.0 3.3 %copy-start.8 = (bf16[512,512]{1,0:T(8,128)(2,1)}, bf16[512,512]{1,0:T(8,128)(2,1)S(1)}, u32[]{:S(2)}) copy-start(bf16[512,512]{1,0:T(8,128)(2,1)S(1)} %get-tuple-element.64) | copy-start | bytes 1572868
  124.3 1.6 copy-start
  129.1 4.9 %copy-start.6 = (bf16[2048,128]{1,0:T(8,128)(2,1)S(1)}, bf16[2048,128]{1,0:T(8,128)(2,1)}, u32[]{:S(2)}) copy-start(bf16[2048,128]{1,0:T(8,128)(2,1)} %copy-done.5) | copy-start | bytes 1572868
  129.1 4.9 %copy-start.9 = (bf16[512,512]{1,0:T(8,128)(2,1)S(1)}, bf16[512,512]{1,0:T(8,128)(2,1)}, u32[]{:S(2)}) copy-start(bf16[512,512]{1,0:T(8,128)(2,1)} %copy-done.8) | copy-start | bytes 1572868
  129.1 33.2 %all-to-all-start.4 = ((f32[64,1,4096]{2,1,0:T(1,128)}), f32[64,1,4096]{2,1,0:T(1,128)S(1)}, u32[]{:S(2)}, u32[]{:S(2)}) async-start(f32[64,1,4096]{2,1,0:T(1,128)} %bitcast.11), calls=%async_computation.4 | async-start | bytes 2097152 | tf_op jit(solution)/shard_map/all_to_all | solution.py:36
  165.3 6.8 %copy-start.15 = (bf16[512,512]{1,0:T(8,128)(2,1)S(1)}, bf16[512,512]{1,0:T(8,128)(2,1)}, u32[]{:S(2)}) copy-start(bf16[512,512]{1,0:T(8,128)(2,1)} %copy-done.14) | copy-start | bytes 1572868
  165.3 35.9 %all-to-all-start.5 = ((f32[64,1,4096]{2,1,0:T(1,128)}), f32[64,1,4096]{2,1,0:T(1,128)S(1)}, u32[]{:S(2)}, u32[]{:S(2)}) async-start(f32[64,1,4096]{2,1,0:T(1,128)} %broadcast_in_dim.11), calls=%async_computation.5 | async-start | bytes 2097152 | tf_op jit(solution)/shard_map/all_to_all | solution.py:42
  172.2 1.0 copy-start.13
  173.2 1.0 copy-start.11
  174.6 8.4 %collective-permute-start = (f32[256,128]{1,0:T(8,128)S(1)}, f32[256,128]{1,0:T(8,128)S(1)}, u32[]{:S(2)}, u32[]{:S(2)}) collective-permute-start(f32[256,128]{1,0:T(8,128)S(1)} %constant_dynamic-slice_fusion.2), channel_id=1, source_target_pairs={{0,4},{1,5},{2,6},{3,7},{4,0},{5,1},{6,2},{7,3},{8,12},{9,13},{10,... | collective-permute-start | bytes 393224 | tf_op jit(solution)/shard_map/ppermute | solution.py:67
  183.0 6.2 %collective-permute-start.1 = (f32[128,128]{1,0:T(8,128)S(1)}, f32[128,128]{1,0:T(8,128)S(1)}, u32[]{:S(2)}, u32[]{:S(2)}) collective-permute-start(f32[128,128]{1,0:T(8,128)S(1)} %constant_dynamic-slice_fusion.1), channel_id=1, source_target_pairs={{0,2},{1,3},{2,0},{3,1},{4,6},{5,7},{6,4},{7,5},{8,10},{9,11},{10,... | collective-permute-start | bytes 196616 | tf_op jit(solution)/shard_map/ppermute | solution.py:67
  189.2 3.1 %collective-permute-start.2 = (f32[64,128]{1,0:T(8,128)S(1)}, f32[64,128]{1,0:T(8,128)S(1)}, u32[]{:S(2)}, u32[]{:S(2)}) collective-permute-start(f32[64,128]{1,0:T(8,128)S(1)} %constant_dynamic-slice_fusion), channel_id=1, source_target_pairs={{0,1},{1,0},{2,3},{3,2},{4,5},{5,4},{6,7},{7,6},{8,9},{9,8},{10,11... | collective-permute-start | bytes 98312 | tf_op jit(solution)/shard_map/ppermute | solution.py:67
  (2 other events, 1.4 us)

commit v6 on v5

--- a/solution.py
+++ b/solution.py
@@ -5,7 +5,7 @@
 import jax
 import jax.numpy as jnp
 from jax import lax
-from jax.sharding import PartitionSpec as P
+from jax.sharding import Mesh, PartitionSpec as P
 
 TEMPER = 0.05
 
@@ -28,8 +28,11 @@
     )
 
 
+COLS = ("chips", "core")
+
+
 def across_slots(stack):
-    return lax.psum(stack, "cols")
+    return lax.psum(lax.psum(stack, "core"), "chips")
 
 
 def exchange_sum(stack, axis, count):
@@ -174,11 +177,11 @@
         dp_parts.append(part)
     dphat = jnp.concatenate(dp_parts, axis=0)
     if local_rows % width_cols:
-        query_part = lax.psum_scatter(dqhat, "cols", scatter_dimension=0, tiled=True)
+        query_part = lax.psum_scatter(dqhat, COLS, scatter_dimension=0, tiled=True)
     else:
-        query_part = halving_scatter(dqhat, "cols", width_cols)
+        query_part = halving_scatter(dqhat, COLS, width_cols)
     piece = query_part.shape[0]
-    begin = lax.axis_index("cols") * piece
+    begin = lax.axis_index(COLS) * piece
     grad_queries = unit_back(
         query_part,
         lax.dynamic_slice_in_dim(qhat, begin, piece, 0),
@@ -208,8 +211,22 @@
         return len(column)
 
 
+def cores_of(mesh):
+    row = list(mesh.devices[0, :])
+    try:
+        lead = row[0].coords
+        return sum(1 for _ in itertools.takewhile(lambda d: d.coords == lead, row))
+    except AttributeError:
+        return 1
+
+
 def solution(mesh):
-    in_specs = (P("rows", None), P("cols", None), P("cols"), P("rows"), P("cols"), P("rows", None))
-    out_specs = (P(("rows", "cols"), None), P("cols", None))
-    body = functools.partial(local, mesh.shape["rows"], inner_of(mesh), mesh.shape["cols"])
-    return jax.shard_map(body, mesh=mesh, in_specs=in_specs, out_specs=out_specs, check_vma=False)
+    rows, cols = mesh.shape["rows"], mesh.shape["cols"]
+    cores = cores_of(mesh)
+    if cols % cores:
+        cores = 1
+    grid = Mesh(mesh.devices.reshape(rows, cols // cores, cores), ("rows",) + COLS)
+    in_specs = (P("rows", None), P(COLS, None), P(COLS), P("rows"), P(COLS), P("rows", None))
+    out_specs = (P(("rows",) + COLS, None), P(COLS, None))
+    body = functools.partial(local, rows, inner_of(mesh), cols)
+    return jax.shard_map(body, mesh=grid, in_specs=in_specs, out_specs=out_specs, check_vma=False)

time: 205 us -> 201 us (0.980)
  waiting for transfers between devices: 46.7 us -> 42.8 us
    all_to_all x1, waiting for transfers between devices: 28 us -> 25.5 us  [exchange_sum(): pieces = lax.all_to_all(stack.reshape(count, -1), axis, 0, 0)]
    psum x2 -> x4, blocking collectives: 27.1 us -> 27.3 us  [across_slots(): return lax.psum(lax.psum(stack, 'core'), 'chips')]
where the time goes in v6:
time: 201 us; the launch traced here: 199 us
  blocking collectives  98.1 us (49%)
  waiting for transfers between devices  42.8 us (21%)
  starting transfers between devices  19.9 us (10%)
  other arithmetic  17.9 us (9%)
  local copies, waits for them, and re-layouts  9.79 us (5%)
  matrix products  8.89 us (4%)
    all_to_all x2, blocking collectives, exchange_sum(): pieces = lax.all_to_all(stack.reshape(count, -1), axis, 0, 0)  39.3 us
    all_to_all x2, blocking collectives, exchange_gather(): return lax.all_to_all(copies, axis, 0, 0).reshape(shape)  31.5 us
    psum x4, blocking collectives, across_slots(): return lax.psum(lax.psum(stack, 'core'), 'chips')  27.3 us
    all_to_all x1, waiting for transfers between devices, exchange_sum(): pieces = lax.all_to_all(stack.reshape(count, -1), axis, 0, 0)  25.5 us
    ppermute x3, waiting for transfers between devices, halving_scatter(): block = keep + lax.ppermute(send, axis, pairs)  9.02 us
    ppermute x3, starting transfers between devices, halving_scatter(): block = keep + lax.ppermute(send, axis, pairs)  8.42 us
    all_to_all x1, waiting for transfers between devices, exchange_gather(): return lax.all_to_all(copies, axis, 0, 0).reshape(shape)  8.2 us
    all_to_all x1, starting transfers between devices, exchange_gather(): return lax.all_to_all(copies, axis, 0, 0).reshape(shape)  6.71 us
  transfers between devices with their start and end apart: 5, of which 5 were waited for; matrix products, arithmetic and copies ran while one was open for 1% of the time, Pallas kernels for 0%

profile of v6, /device:TPU:6, one launch (start us, length us, event | category | flops | bytes accessed | tf_op | source)
XLA Modules:
  0.0 198.5 jit_solution(9697354213614816596)
XLA Ops:
  1.4 1.4 fusion.12
  8.5 1.4 fusion.44
  10.5 2.5 %psum.28 = f32[2,512]{1,0:T(2,128)S(1)} all-reduce(f32[2,512]{1,0:T(2,128)S(1)} %pad_maximum_fusion.6), channel_id=1, replica_groups=mesh['rows'=64,'chips'=4,'core'=2] {'core'}, use_global_device_ids=true, to_apply=%region_10.0 | all-reduce | flops 1024 | bytes 8192 | tf_op jit(solution)/shard_map/psum | solution.py:35
  13.0 12.3 %psum.29 = f32[2,512]{1,0:T(2,128)S(1)} all-reduce(f32[2,512]{1,0:T(2,128)S(1)} %psum.28), channel_id=1, replica_groups=mesh['rows'=64,'chips'=4,'core'=2] {'chips'}, use_global_device_ids=true, to_apply=%region_11.0 | all-reduce | flops 1024 | bytes 8192 | tf_op jit(solution)/shard_map/psum | solution.py:35
  26.0 3.5 %multiply_reduce_fusion.20 = (f32[512]{0:T(512)S(1)}, f32[512]{0:T(512)S(1)}, f32[512]{0:T(512)S(1)}, f32[512]{0:T(512)S(1)}, f32[512]{0:T(512)S(1)}, /*index=5*...) fusion(f32[512,512]{1,0:T(8,128)S(1)} %get-tuple-element.67, ...), kind=kLoop, calls=%fused_computation.53 | loop fusion | flops 6285312 | bytes 8417280 | tf_op jit(solution)/shard_map/reduce_sum | solution.py:137
  29.8 23.5 %all_to_all.45 = f32[64,1,96]{2,1,0:T(1,128)S(1)} all-to-all(f32[64,1,96]{2,1,0:T(1,128)S(1)} %all_to_all.30), channel_id=1, replica_groups=mesh['rows'=64,'chips'=4,'core'=2] {'rows'}, dimensions={0} | all-to-all | bytes 49152 | tf_op jit(solution)/shard_map/all_to_all | solution.py:39
  53.4 15.8 %all_to_all.46 = f32[64,1,96]{2,1,0:T(1,128)S(1)} all-to-all(f32[64,1,96]{2,1,0:T(1,128)S(1)} %broadcast_in_dim.8), channel_id=1, replica_groups=mesh['rows'=64,'chips'=4,'core'=2] {'rows'}, dimensions={0} | all-to-all | bytes 49152 | tf_op jit(solution)/shard_map/all_to_all | solution.py:45
  70.5 1.8 multiply_reduce_fusion.6
  72.4 2.5 %psum.30 = f32[1,512]{1,0:T(1,128)S(1)} all-reduce(f32[1,512]{1,0:T(1,128)S(1)} %bitcast.46), channel_id=1, replica_groups=mesh['rows'=64,'chips'=4,'core'=2] {'core'}, use_global_device_ids=true, to_apply=%region_29.0 | all-reduce | flops 512 | bytes 4096 | tf_op jit(solution)/shard_map/psum | solution.py:35
  74.8 10.0 %psum.31 = f32[512]{0:T(512)S(1)} all-reduce(f32[512]{0:T(512)S(1)} %bitcast.49), channel_id=1, replica_groups=mesh['rows'=64,'chips'=4,'core'=2] {'chips'}, use_global_device_ids=true, to_apply=%region_30.0 | all-reduce | flops 512 | bytes 4096 | tf_op jit(solution)/shard_map/psum | solution.py:35
  84.8 1.7 multiply_reduce_fusion.3
  86.9 15.8 %all_to_all.47 = f32[64,1,32]{2,1,0:T(1,128)S(1)} all-to-all(f32[64,1,32]{2,1,0:T(1,128)S(1)} %bitcast.37), channel_id=1, replica_groups=mesh['rows'=64,'chips'=4,'core'=2] {'rows'}, dimensions={0} | all-to-all | bytes 16384 | tf_op jit(solution)/shard_map/all_to_all | solution.py:39
  102.7 15.8 %all_to_all.48 = f32[64,1,32]{2,1,0:T(1,128)S(1)} all-to-all(f32[64,1,32]{2,1,0:T(1,128)S(1)} %broadcast_in_dim.9), channel_id=1, replica_groups=mesh['rows'=64,'chips'=4,'core'=2] {'rows'}, dimensions={0} | all-to-all | bytes 16384 | tf_op jit(solution)/shard_map/all_to_all | solution.py:45
  119.3 3.4 %multiply_convert_fusion = (bf16[512,512]{1,0:T(8,128)(2,1)S(1)}, bf16[512,512]{1,0:T(8,128)(2,1)S(1)}, bf16[512,512]{1,0:T(8,128)(2,1)S(1)}, bf16[512,512]{1,0:T(8,128)(2,1)S(1)}) fusion(f32[512,512]{1,0:T(8,128)} %copy-done.4, f32[512,512]{1,0:T(8,128)S(1)} %get-tuple-element.67, f32[512]{0:T(512)S(1)} %get-tuple-element.45, ...), kind=kLoop, calls=%fused_computation.28 | loop fusion | flops 6291456 | bytes 10498048 | tf_op jit(solution)/shard_map/convert_element_type | solution.py:166
  127.9 4.8 %all-to-all-start.4 = ((f32[64,1,4096]{2,1,0:T(1,128)}), f32[64,1,4096]{2,1,0:T(1,128)S(1)}, u32[]{:S(2)}, u32[]{:S(2)}) async-start(f32[64,1,4096]{2,1,0:T(1,128)} %bitcast.13), calls=%async_computation.4 | async-start | bytes 2097152 | tf_op jit(solution)/shard_map/all_to_all | solution.py:39
  133.1 25.5 %all-to-all-done.4 = f32[64,1,4096]{2,1,0:T(1,128)S(1)} async-done(((f32[64,1,4096]{2,1,0:T(1,128)}), f32[64,1,4096]{2,1,0:T(1,128)S(1)}, u32[]{:S(2)}, u32[]{:S(2)}) %all-to-all-start.4) | async-done | bytes 1048608 | tf_op jit(solution)/shard_map/all_to_all | solution.py:39
  159.7 2.0 %broadcast_in_dim.11 = f32[64,1,4096]{2,1,0:T(1,128)} broadcast(f32[4096]{0:T(1024)S(1)} %fusion.43), dimensions={2} | broadcast | bytes 1064960 | tf_op jit(solution)/shard_map/broadcast_in_dim | solution.py:44
  161.7 6.7 %all-to-all-start.5 = ((f32[64,1,4096]{2,1,0:T(1,128)}), f32[64,1,4096]{2,1,0:T(1,128)S(1)}, u32[]{:S(2)}, u32[]{:S(2)}) async-start(f32[64,1,4096]{2,1,0:T(1,128)} %broadcast_in_dim.11), calls=%async_computation.5 | async-start | bytes 2097152 | tf_op jit(solution)/shard_map/all_to_all | solution.py:45
  170.8 4.6 %collective-permute-start = (f32[256,128]{1,0:T(8,128)S(1)}, f32[256,128]{1,0:T(8,128)S(1)}, u32[]{:S(2)}, u32[]{:S(2)}) collective-permute-start(f32[256,128]{1,0:T(8,128)S(1)} %constant_dynamic-slice_fusion.2), channel_id=1, source_target_pairs={{0,4},{1,5},{2,6},{3,7},{4,0},{5,1},{6,2},{7,3},{8,12},{9,13},{10,... | collective-permute-start | bytes 393224 | tf_op jit(solution)/shard_map/ppermute | solution.py:70
  175.4 3.7 %collective-permute-done = f32[256,128]{1,0:T(8,128)S(1)} collective-permute-done((f32[256,128]{1,0:T(8,128)S(1)}, f32[256,128]{1,0:T(8,128)S(1)}, u32[]{:S(2)}, u32[]{:S(2)}) %collective-permute-start) | collective-permute-done | bytes 131104 | tf_op jit(solution)/shard_map/ppermute | solution.py:70
  179.2 1.9 collective-permute-start.1
  181.2 4.2 %collective-permute-done.1 = f32[128,128]{1,0:T(8,128)S(1)} collective-permute-done((f32[128,128]{1,0:T(8,128)S(1)}, f32[128,128]{1,0:T(8,128)S(1)}, u32[]{:S(2)}, u32[]{:S(2)}) %collective-permute-start.1) | collective-permute-done | bytes 65568 | tf_op jit(solution)/shard_map/ppermute | solution.py:70
  185.4 1.9 collective-permute-start.2
  189.3 8.2 %all-to-all-done.5 = f32[64,1,4096]{2,1,0:T(1,128)S(1)} async-done(((f32[64,1,4096]{2,1,0:T(1,128)}), f32[64,1,4096]{2,1,0:T(1,128)S(1)}, u32[]{:S(2)}, u32[]{:S(2)}) %all-to-all-start.5) | async-done | bytes 1048608 | tf_op jit(solution)/shard_map/all_to_all | solution.py:45
  (114 shorter events, 22.4 us)
Async XLA Ops:
  0.6 2.2 %copy-start.16 = (bf16[2048,128]{1,0:T(8,128)(2,1)S(1)}, bf16[2048,128]{1,0:T(8,128)(2,1)}, u32[]{:S(2)}) copy-start(bf16[2048,128]{1,0:T(8,128)(2,1)} %param.7) | copy-start | bytes 1572868
  2.8 0.9 copy-start.7
  3.7 6.2 %copy-start.5 = (bf16[2048,128]{1,0:T(8,128)(2,1)}, bf16[2048,128]{1,0:T(8,128)(2,1)S(1)}, u32[]{:S(2)}) copy-start(bf16[2048,128]{1,0:T(8,128)(2,1)S(1)} %fusion.13) | copy-start | bytes 1572868
  4.1 5.9 %copy-start.1 = (f32[512,512]{1,0:T(8,128)}, f32[512,512]{1,0:T(8,128)S(1)}, u32[]{:S(2)}) copy-start(f32[512,512]{1,0:T(8,128)S(1)} %fusion.34) | copy-start | bytes 3145732
  4.4 4.1 %copy-start.2 = (f32[512,512]{1,0:T(8,128)}, f32[512,512]{1,0:T(8,128)S(1)}, u32[]{:S(2)}) copy-start(f32[512,512]{1,0:T(8,128)S(1)} %fusion.29) | copy-start | bytes 3145732
  4.8 3.2 %copy-start.3 = (f32[512,512]{1,0:T(8,128)}, f32[512,512]{1,0:T(8,128)S(1)}, u32[]{:S(2)}) copy-start(f32[512,512]{1,0:T(8,128)S(1)} %fusion.25) | copy-start | bytes 3145732
  4.8 1.0 copy-start.17
  5.9 2.1 %copy-start.4 = (f32[512,512]{1,0:T(8,128)}, f32[512,512]{1,0:T(8,128)S(1)}, u32[]{:S(2)}) copy-start(f32[512,512]{1,0:T(8,128)S(1)} %fusion.21) | copy-start | bytes 3145732
  5.9 0.7 copy-start.19
  122.7 0.9 copy-start.10
  122.7 1.0 copy-start.14
  122.7 2.4 %copy-start.12 = (bf16[512,512]{1,0:T(8,128)(2,1)}, bf16[512,512]{1,0:T(8,128)(2,1)S(1)}, u32[]{:S(2)}) copy-start(bf16[512,512]{1,0:T(8,128)(2,1)S(1)} %get-tuple-element.63) | copy-start | bytes 1572868
  122.7 3.3 %copy-start.8 = (bf16[512,512]{1,0:T(8,128)(2,1)}, bf16[512,512]{1,0:T(8,128)(2,1)S(1)}, u32[]{:S(2)}) copy-start(bf16[512,512]{1,0:T(8,128)(2,1)S(1)} %get-tuple-element.64) | copy-start | bytes 1572868
  123.1 1.6 copy-start
  127.9 4.9 %copy-start.6 = (bf16[2048,128]{1,0:T(8,128)(2,1)S(1)}, bf16[2048,128]{1,0:T(8,128)(2,1)}, u32[]{:S(2)}) copy-start(bf16[2048,128]{1,0:T(8,128)(2,1)} %copy-done.5) | copy-start | bytes 1572868
  127.9 4.9 %copy-start.9 = (bf16[512,512]{1,0:T(8,128)(2,1)S(1)}, bf16[512,512]{1,0:T(8,128)(2,1)}, u32[]{:S(2)}) copy-start(bf16[512,512]{1,0:T(8,128)(2,1)} %copy-done.8) | copy-start | bytes 1572868
  127.9 30.7 %all-to-all-start.4 = ((f32[64,1,4096]{2,1,0:T(1,128)}), f32[64,1,4096]{2,1,0:T(1,128)S(1)}, u32[]{:S(2)}, u32[]{:S(2)}) async-start(f32[64,1,4096]{2,1,0:T(1,128)} %bitcast.13), calls=%async_computation.4 | async-start | bytes 2097152 | tf_op jit(solution)/shard_map/all_to_all | solution.py:39
  161.7 6.7 %copy-start.15 = (bf16[512,512]{1,0:T(8,128)(2,1)S(1)}, bf16[512,512]{1,0:T(8,128)(2,1)}, u32[]{:S(2)}) copy-start(bf16[512,512]{1,0:T(8,128)(2,1)} %copy-done.14) | copy-start | bytes 1572868
  161.7 35.9 %all-to-all-start.5 = ((f32[64,1,4096]{2,1,0:T(1,128)}), f32[64,1,4096]{2,1,0:T(1,128)S(1)}, u32[]{:S(2)}, u32[]{:S(2)}) async-start(f32[64,1,4096]{2,1,0:T(1,128)} %broadcast_in_dim.11), calls=%async_computation.5 | async-start | bytes 2097152 | tf_op jit(solution)/shard_map/all_to_all | solution.py:45
  168.4 1.0 copy-start.13
  169.4 1.0 copy-start.11
  170.8 8.4 %collective-permute-start = (f32[256,128]{1,0:T(8,128)S(1)}, f32[256,128]{1,0:T(8,128)S(1)}, u32[]{:S(2)}, u32[]{:S(2)}) collective-permute-start(f32[256,128]{1,0:T(8,128)S(1)} %constant_dynamic-slice_fusion.2), channel_id=1, source_target_pairs={{0,4},{1,5},{2,6},{3,7},{4,0},{5,1},{6,2},{7,3},{8,12},{9,13},{10,... | collective-permute-start | bytes 393224 | tf_op jit(solution)/shard_map/ppermute | solution.py:70
  179.2 6.2 %collective-permute-start.1 = (f32[128,128]{1,0:T(8,128)S(1)}, f32[128,128]{1,0:T(8,128)S(1)}, u32[]{:S(2)}, u32[]{:S(2)}) collective-permute-start(f32[128,128]{1,0:T(8,128)S(1)} %constant_dynamic-slice_fusion.1), channel_id=1, source_target_pairs={{0,2},{1,3},{2,0},{3,1},{4,6},{5,7},{6,4},{7,5},{8,10},{9,11},{10,... | collective-permute-start | bytes 196616 | tf_op jit(solution)/shard_map/ppermute | solution.py:70
  185.4 3.1 %collective-permute-start.2 = (f32[64,128]{1,0:T(8,128)S(1)}, f32[64,128]{1,0:T(8,128)S(1)}, u32[]{:S(2)}, u32[]{:S(2)}) collective-permute-start(f32[64,128]{1,0:T(8,128)S(1)} %constant_dynamic-slice_fusion), channel_id=1, source_target_pairs={{0,1},{1,0},{2,3},{3,2},{4,5},{5,4},{6,7},{7,6},{8,9},{9,8},{10,11... | collective-permute-start | bytes 98312 | tf_op jit(solution)/shard_map/ppermute | solution.py:70
  (2 other events, 1.4 us)

commit v7 on v6

--- a/solution.py
+++ b/solution.py
@@ -45,7 +45,14 @@
     return lax.all_to_all(copies, axis, 0, 0).reshape(shape)
 
 
-def across_queries(stack, count):
+def spread_sum(stack, axis, count):
+    copies = jnp.broadcast_to(stack.reshape(1, -1), (count, stack.size))
+    return jnp.sum(lax.all_to_all(copies, axis, 0, 0), axis=0).reshape(stack.shape)
+
+
+def across_queries(stack, count, spread=False):
+    if spread:
+        return spread_sum(stack, "rows", count)
     if stack.size % count == 0:
         return exchange_gather(exchange_sum(stack, "rows", count), "rows", count, stack.shape)
     if count & (count - 1):
@@ -155,7 +162,7 @@
     for start in starts:
         plan = share[:, None] * kernel_tile(start)
         t_parts.append(jnp.sum(alpha_two[:, None] * plan, axis=0))
-    t_two = across_queries(jnp.concatenate(t_parts)[None, :], count)[0]
+    t_two = across_queries(jnp.concatenate(t_parts)[None, :], count, spread=True)[0]
     beta_two = (qvec - t_two) / colsum
     dqhat = jnp.zeros(qhat.shape, jnp.float32)
     dp_parts = []

time: 201 us -> 196 us (0.975)
  blocking collectives: 98.1 us -> 89.2 us
  waiting for transfers between devices: 42.8 us -> 45.4 us
    all_to_all x0 -> x1, blocking collectives: none -> 22.7 us  [spread_sum(): lax.all_to_all(copies, axis, 0, 0)]
    all_to_all x2 -> x1, blocking collectives: 31.5 us -> 15.8 us  [exchange_gather(): return lax.all_to_all(copies, axis, 0, 0).reshape(shape)]
    all_to_all x2 -> x1, blocking collectives: 39.3 us -> 23.5 us  [exchange_sum(): pieces = lax.all_to_all(stack.reshape(count, -1), axis, 0, 0)]
    all_to_all x1, waiting for transfers between devices: 25.5 us -> 28.2 us  [exchange_sum(): pieces = lax.all_to_all(stack.reshape(count, -1), axis, 0, 0)]
where the time goes in v7:
time: 196 us; the launch traced here: 193 us
  blocking collectives  89.2 us (46%)
  waiting for transfers between devices  45.4 us (23%)
  starting transfers between devices  20.4 us (10%)
  other arithmetic  18.4 us (9%)
  local copies, waits for them, and re-layouts  9.66 us (5%)
  matrix products  8.89 us (5%)
    all_to_all x1, waiting for transfers between devices, exchange_sum(): pieces = lax.all_to_all(stack.reshape(count, -1), axis, 0, 0)  28.2 us
    psum x4, blocking collectives, across_slots(): return lax.psum(lax.psum(stack, 'core'), 'chips')  27.3 us
    all_to_all x1, blocking collectives, exchange_sum(): pieces = lax.all_to_all(stack.reshape(count, -1), axis, 0, 0)  23.5 us
    all_to_all x1, blocking collectives, spread_sum(): lax.all_to_all(copies, axis, 0, 0)  22.7 us
    all_to_all x1, blocking collectives, exchange_gather(): return lax.all_to_all(copies, axis, 0, 0).reshape(shape)  15.8 us
    ppermute x3, waiting for transfers between devices, halving_scatter(): block = keep + lax.ppermute(send, axis, pairs)  9 us
    ppermute x3, starting transfers between devices, halving_scatter(): block = keep + lax.ppermute(send, axis, pairs)  8.44 us
    all_to_all x1, waiting for transfers between devices, exchange_gather(): return lax.all_to_all(copies, axis, 0, 0).reshape(shape)  8.19 us
  transfers between devices with their start and end apart: 5, of which 5 were waited for; matrix products, arithmetic and copies ran while one was open for 1% of the time, Pallas kernels for 0%

profile of v7, /device:TPU:6, one launch (start us, length us, event | category | flops | bytes accessed | tf_op | source)
XLA Modules:
  0.0 193.2 jit_solution(17697586880396243899)
XLA Ops:
  1.4 1.4 fusion.12
  8.5 1.4 fusion.44
  10.5 2.5 %psum.28 = f32[2,512]{1,0:T(2,128)S(1)} all-reduce(f32[2,512]{1,0:T(2,128)S(1)} %pad_maximum_fusion.6), channel_id=1, replica_groups=mesh['rows'=64,'chips'=4,'core'=2] {'core'}, use_global_device_ids=true, to_apply=%region_10.0 | all-reduce | flops 1024 | bytes 8192 | tf_op jit(solution)/shard_map/psum | solution.py:35
  13.0 12.3 %psum.29 = f32[2,512]{1,0:T(2,128)S(1)} all-reduce(f32[2,512]{1,0:T(2,128)S(1)} %psum.28), channel_id=1, replica_groups=mesh['rows'=64,'chips'=4,'core'=2] {'chips'}, use_global_device_ids=true, to_apply=%region_11.0 | all-reduce | flops 1024 | bytes 8192 | tf_op jit(solution)/shard_map/psum | solution.py:35
  26.0 3.5 %multiply_reduce_fusion.20 = (f32[512]{0:T(512)S(1)}, f32[512]{0:T(512)S(1)}, f32[512]{0:T(512)S(1)}, f32[512]{0:T(512)S(1)}, f32[512]{0:T(512)S(1)}, /*index=5*...) fusion(f32[512,512]{1,0:T(8,128)S(1)} %get-tuple-element.67, ...), kind=kLoop, calls=%fused_computation.53 | loop fusion | flops 6285312 | bytes 8417280 | tf_op jit(solution)/shard_map/reduce_sum | solution.py:144
  29.8 23.5 %all_to_all.36 = f32[64,1,96]{2,1,0:T(1,128)S(1)} all-to-all(f32[64,1,96]{2,1,0:T(1,128)S(1)} %all_to_all.24), channel_id=1, replica_groups=mesh['rows'=64,'chips'=4,'core'=2] {'rows'}, dimensions={0} | all-to-all | bytes 49152 | tf_op jit(solution)/shard_map/all_to_all | solution.py:39
  53.4 15.8 %all_to_all.37 = f32[64,1,96]{2,1,0:T(1,128)S(1)} all-to-all(f32[64,1,96]{2,1,0:T(1,128)S(1)} %broadcast_in_dim.8), channel_id=1, replica_groups=mesh['rows'=64,'chips'=4,'core'=2] {'rows'}, dimensions={0} | all-to-all | bytes 49152 | tf_op jit(solution)/shard_map/all_to_all | solution.py:45
  70.5 1.8 multiply_reduce_fusion.6
  72.4 2.5 %psum.30 = f32[1,512]{1,0:T(1,128)S(1)} all-reduce(f32[1,512]{1,0:T(1,128)S(1)} %bitcast.44), channel_id=1, replica_groups=mesh['rows'=64,'chips'=4,'core'=2] {'core'}, use_global_device_ids=true, to_apply=%region_29.0 | all-reduce | flops 512 | bytes 4096 | tf_op jit(solution)/shard_map/psum | solution.py:35
  74.8 10.0 %psum.31 = f32[512]{0:T(512)S(1)} all-reduce(f32[512]{0:T(512)S(1)} %bitcast.47), channel_id=1, replica_groups=mesh['rows'=64,'chips'=4,'core'=2] {'chips'}, use_global_device_ids=true, to_apply=%region_30.0 | all-reduce | flops 512 | bytes 4096 | tf_op jit(solution)/shard_map/psum | solution.py:35
  84.8 1.7 multiply_reduce_fusion.3
  86.8 22.7 %all_to_all.38 = f32[64,1,2048]{2,1,0:T(1,128)} all-to-all(f32[64,1,2048]{2,1,0:T(1,128)S(1)} %broadcast_in_dim.9), channel_id=1, replica_groups=mesh['rows'=64,'chips'=4,'core'=2] {'rows'}, dimensions={0} | all-to-all | bytes 1048576 | tf_op jit(solution)/shard_map/all_to_all | solution.py:50
  109.5 1.4 reduce_sum.346
  110.9 3.4 %multiply_convert_fusion = (bf16[512,512]{1,0:T(8,128)(2,1)S(1)}, bf16[512,512]{1,0:T(8,128)(2,1)S(1)}, bf16[512,512]{1,0:T(8,128)(2,1)S(1)}, bf16[512,512]{1,0:T(8,128)(2,1)S(1)}) fusion(f32[512,512]{1,0:T(8,128)} %copy-done.4, f32[512,512]{1,0:T(8,128)S(1)} %get-tuple-element.67, f32[512]{0:T(512)S(1)} %get-tuple-element.45, ...), kind=kLoop, calls=%fused_computation.28 | loop fusion | flops 6291456 | bytes 10498048 | tf_op jit(solution)/shard_map/convert_element_type | solution.py:173
  119.4 5.2 %all-to-all-start.3 = ((f32[64,1,4096]{2,1,0:T(1,128)}), f32[64,1,4096]{2,1,0:T(1,128)S(1)}, u32[]{:S(2)}, u32[]{:S(2)}) async-start(f32[64,1,4096]{2,1,0:T(1,128)} %bitcast.12), calls=%async_computation.3 | async-start | bytes 2097152 | tf_op jit(solution)/shard_map/all_to_all | solution.py:39
  125.1 28.2 %all-to-all-done.3 = f32[64,1,4096]{2,1,0:T(1,128)S(1)} async-done(((f32[64,1,4096]{2,1,0:T(1,128)}), f32[64,1,4096]{2,1,0:T(1,128)S(1)}, u32[]{:S(2)}, u32[]{:S(2)}) %all-to-all-start.3) | async-done | bytes 1048608 | tf_op jit(solution)/shard_map/all_to_all | solution.py:39
  154.3 2.0 %broadcast_in_dim.11 = f32[64,1,4096]{2,1,0:T(1,128)} broadcast(f32[4096]{0:T(1024)S(1)} %fusion.43), dimensions={2} | broadcast | bytes 1064960 | tf_op jit(solution)/shard_map/broadcast_in_dim | solution.py:44
  156.3 6.8 %all-to-all-start.4 = ((f32[64,1,4096]{2,1,0:T(1,128)}), f32[64,1,4096]{2,1,0:T(1,128)S(1)}, u32[]{:S(2)}, u32[]{:S(2)}) async-start(f32[64,1,4096]{2,1,0:T(1,128)} %broadcast_in_dim.11), calls=%async_computation.4 | async-start | bytes 2097152 | tf_op jit(solution)/shard_map/all_to_all | solution.py:45
  165.5 4.6 %collective-permute-start = (f32[256,128]{1,0:T(8,128)S(1)}, f32[256,128]{1,0:T(8,128)S(1)}, u32[]{:S(2)}, u32[]{:S(2)}) collective-permute-start(f32[256,128]{1,0:T(8,128)S(1)} %constant_dynamic-slice_fusion.2), channel_id=1, source_target_pairs={{0,4},{1,5},{2,6},{3,7},{4,0},{5,1},{6,2},{7,3},{8,12},{9,13},{10,... | collective-permute-start | bytes 393224 | tf_op jit(solution)/shard_map/ppermute | solution.py:77
  170.2 3.7 %collective-permute-done = f32[256,128]{1,0:T(8,128)S(1)} collective-permute-done((f32[256,128]{1,0:T(8,128)S(1)}, f32[256,128]{1,0:T(8,128)S(1)}, u32[]{:S(2)}, u32[]{:S(2)}) %collective-permute-start) | collective-permute-done | bytes 131104 | tf_op jit(solution)/shard_map/ppermute | solution.py:77
  174.0 1.9 %collective-permute-start.1 = (f32[128,128]{1,0:T(8,128)S(1)}, f32[128,128]{1,0:T(8,128)S(1)}, u32[]{:S(2)}, u32[]{:S(2)}) collective-permute-start(f32[128,128]{1,0:T(8,128)S(1)} %constant_dynamic-slice_fusion.1), channel_id=1, source_target_pairs={{0,2},{1,3},{2,0},{3,1},{4,6},{5,7},{6,4},{7,5},{8,10},{9,11},{10,... | collective-permute-start | bytes 196616 | tf_op jit(solution)/shard_map/ppermute | solution.py:77
  175.9 4.2 %collective-permute-done.1 = f32[128,128]{1,0:T(8,128)S(1)} collective-permute-done((f32[128,128]{1,0:T(8,128)S(1)}, f32[128,128]{1,0:T(8,128)S(1)}, u32[]{:S(2)}, u32[]{:S(2)}) %collective-permute-start.1) | collective-permute-done | bytes 65568 | tf_op jit(solution)/shard_map/ppermute | solution.py:77
  180.1 1.9 collective-permute-start.2
  184.1 8.2 %all-to-all-done.4 = f32[64,1,4096]{2,1,0:T(1,128)S(1)} async-done(((f32[64,1,4096]{2,1,0:T(1,128)}), f32[64,1,4096]{2,1,0:T(1,128)S(1)}, u32[]{:S(2)}, u32[]{:S(2)}) %all-to-all-start.4) | async-done | bytes 1048608 | tf_op jit(solution)/shard_map/all_to_all | solution.py:45
  (107 shorter events, 21.5 us)
Async XLA Ops:
  0.6 2.2 %copy-start.16 = (bf16[2048,128]{1,0:T(8,128)(2,1)S(1)}, bf16[2048,128]{1,0:T(8,128)(2,1)}, u32[]{:S(2)}) copy-start(bf16[2048,128]{1,0:T(8,128)(2,1)} %param.7) | copy-start | bytes 1572868
  2.8 0.9 copy-start.7
  3.7 6.2 %copy-start.5 = (bf16[2048,128]{1,0:T(8,128)(2,1)}, bf16[2048,128]{1,0:T(8,128)(2,1)S(1)}, u32[]{:S(2)}) copy-start(bf16[2048,128]{1,0:T(8,128)(2,1)S(1)} %fusion.13) | copy-start | bytes 1572868
  4.1 5.9 %copy-start.1 = (f32[512,512]{1,0:T(8,128)}, f32[512,512]{1,0:T(8,128)S(1)}, u32[]{:S(2)}) copy-start(f32[512,512]{1,0:T(8,128)S(1)} %fusion.34) | copy-start | bytes 3145732
  4.4 4.1 %copy-start.2 = (f32[512,512]{1,0:T(8,128)}, f32[512,512]{1,0:T(8,128)S(1)}, u32[]{:S(2)}) copy-start(f32[512,512]{1,0:T(8,128)S(1)} %fusion.29) | copy-start | bytes 3145732
  4.8 3.2 %copy-start.3 = (f32[512,512]{1,0:T(8,128)}, f32[512,512]{1,0:T(8,128)S(1)}, u32[]{:S(2)}) copy-start(f32[512,512]{1,0:T(8,128)S(1)} %fusion.25) | copy-start | bytes 3145732
  4.8 1.0 copy-start.17
  5.9 2.1 %copy-start.4 = (f32[512,512]{1,0:T(8,128)}, f32[512,512]{1,0:T(8,128)S(1)}, u32[]{:S(2)}) copy-start(f32[512,512]{1,0:T(8,128)S(1)} %fusion.21) | copy-start | bytes 3145732
  5.9 0.7 copy-start.19
  114.3 0.9 copy-start.10
  114.3 1.0 copy-start.14
  114.3 2.4 %copy-start.12 = (bf16[512,512]{1,0:T(8,128)(2,1)}, bf16[512,512]{1,0:T(8,128)(2,1)S(1)}, u32[]{:S(2)}) copy-start(bf16[512,512]{1,0:T(8,128)(2,1)S(1)} %get-tuple-element.63) | copy-start | bytes 1572868
  114.3 3.3 %copy-start.8 = (bf16[512,512]{1,0:T(8,128)(2,1)}, bf16[512,512]{1,0:T(8,128)(2,1)S(1)}, u32[]{:S(2)}) copy-start(bf16[512,512]{1,0:T(8,128)(2,1)S(1)} %get-tuple-element.64) | copy-start | bytes 1572868
  114.6 1.6 copy-start
  119.4 5.3 %copy-start.6 = (bf16[2048,128]{1,0:T(8,128)(2,1)S(1)}, bf16[2048,128]{1,0:T(8,128)(2,1)}, u32[]{:S(2)}) copy-start(bf16[2048,128]{1,0:T(8,128)(2,1)} %copy-done.5) | copy-start | bytes 1572868
  119.4 5.3 %copy-start.9 = (bf16[512,512]{1,0:T(8,128)(2,1)S(1)}, bf16[512,512]{1,0:T(8,128)(2,1)}, u32[]{:S(2)}) copy-start(bf16[512,512]{1,0:T(8,128)(2,1)} %copy-done.8) | copy-start | bytes 1572868
  119.4 33.9 %all-to-all-start.3 = ((f32[64,1,4096]{2,1,0:T(1,128)}), f32[64,1,4096]{2,1,0:T(1,128)S(1)}, u32[]{:S(2)}, u32[]{:S(2)}) async-start(f32[64,1,4096]{2,1,0:T(1,128)} %bitcast.12), calls=%async_computation.3 | async-start | bytes 2097152 | tf_op jit(solution)/shard_map/all_to_all | solution.py:39
  156.3 6.8 %copy-start.15 = (bf16[512,512]{1,0:T(8,128)(2,1)S(1)}, bf16[512,512]{1,0:T(8,128)(2,1)}, u32[]{:S(2)}) copy-start(bf16[512,512]{1,0:T(8,128)(2,1)} %copy-done.14) | copy-start | bytes 1572868
  156.3 35.9 %all-to-all-start.4 = ((f32[64,1,4096]{2,1,0:T(1,128)}), f32[64,1,4096]{2,1,0:T(1,128)S(1)}, u32[]{:S(2)}, u32[]{:S(2)}) async-start(f32[64,1,4096]{2,1,0:T(1,128)} %broadcast_in_dim.11), calls=%async_computation.4 | async-start | bytes 2097152 | tf_op jit(solution)/shard_map/all_to_all | solution.py:45
  163.1 1.0 copy-start.13
  164.2 1.0 copy-start.11
  165.5 8.4 %collective-permute-start = (f32[256,128]{1,0:T(8,128)S(1)}, f32[256,128]{1,0:T(8,128)S(1)}, u32[]{:S(2)}, u32[]{:S(2)}) collective-permute-start(f32[256,128]{1,0:T(8,128)S(1)} %constant_dynamic-slice_fusion.2), channel_id=1, source_target_pairs={{0,4},{1,5},{2,6},{3,7},{4,0},{5,1},{6,2},{7,3},{8,12},{9,13},{10,... | collective-permute-start | bytes 393224 | tf_op jit(solution)/shard_map/ppermute | solution.py:77
  174.0 6.2 %collective-permute-start.1 = (f32[128,128]{1,0:T(8,128)S(1)}, f32[128,128]{1,0:T(8,128)S(1)}, u32[]{:S(2)}, u32[]{:S(2)}) collective-permute-start(f32[128,128]{1,0:T(8,128)S(1)} %constant_dynamic-slice_fusion.1), channel_id=1, source_target_pairs={{0,2},{1,3},{2,0},{3,1},{4,6},{5,7},{6,4},{7,5},{8,10},{9,11},{10,... | collective-permute-start | bytes 196616 | tf_op jit(solution)/shard_map/ppermute | solution.py:77
  180.1 3.1 %collective-permute-start.2 = (f32[64,128]{1,0:T(8,128)S(1)}, f32[64,128]{1,0:T(8,128)S(1)}, u32[]{:S(2)}, u32[]{:S(2)}) collective-permute-start(f32[64,128]{1,0:T(8,128)S(1)} %constant_dynamic-slice_fusion), channel_id=1, source_target_pairs={{0,1},{1,0},{2,3},{3,2},{4,5},{5,4},{6,7},{7,6},{8,9},{9,8},{10,11... | collective-permute-start | bytes 98312 | tf_op jit(solution)/shard_map/ppermute | solution.py:77
  (2 other events, 1.4 us)

commit v8 on v7

--- a/solution.py
+++ b/solution.py
@@ -149,6 +149,7 @@
     summed = across_queries(
         jnp.stack([jnp.concatenate(col_parts), jnp.concatenate(q_parts), jnp.concatenate(t_parts)]),
         count,
+        spread=True,
     )
     colsum, qvec, t_one = (summed[0], summed[1], summed[2])
     beta_one = (qvec - t_one) / colsum

time: 196 us -> 211 us (1.077)
  blocking collectives: 89.2 us -> 103 us
  local copies, waits for them, and re-layouts: 9.66 us -> 5.9 us
  other arithmetic: 18.4 us -> 21 us
    all_to_all x1 -> x2, blocking collectives: 22.7 us -> 76.4 us  [spread_sum(): lax.all_to_all(copies, axis, 0, 0)]
    all_to_all x2 -> x0, blocking collectives: 39.3 us -> none  [the longest x1 23.5 us: exchange_sum(): pieces = lax.all_to_all(stack.reshape(count, -1), axis, 0, 0)]
    unnamed x43 -> x41, local copies, waits for them, and re-layouts: 6.39 us -> 2.59 us
    reduce_sum x1 -> x2, other arithmetic: 1.36 us -> 3.76 us  [spread_sum(): jnp.sum(lax.all_to_all(copies, axis, 0, 0), axis=0).reshape(stack.shape)]
where the time goes in v8:
time: 211 us; the launch traced here: 208 us
  blocking collectives  103 us (49%)
  waiting for transfers between devices  46.3 us (22%)
  other arithmetic  21 us (10%)
  starting transfers between devices  20.8 us (10%)
  matrix products  8.9 us (4%)
  local copies, waits for them, and re-layouts  5.9 us (3%)
    all_to_all x2, blocking collectives, spread_sum(): lax.all_to_all(copies, axis, 0, 0)  76.4 us
    all_to_all x1, waiting for transfers between devices, exchange_sum(): pieces = lax.all_to_all(stack.reshape(count, -1), axis, 0, 0)  28.4 us
    psum x4, blocking collectives, across_slots(): return lax.psum(lax.psum(stack, 'core'), 'chips')  26.9 us
    all_to_all x1, waiting for transfers between devices, exchange_gather(): return lax.all_to_all(copies, axis, 0, 0).reshape(shape)  9.44 us
    ppermute x3, starting transfers between devices, halving_scatter(): block = keep + lax.ppermute(send, axis, pairs)  8.93 us
    ppermute x3, waiting for transfers between devices, halving_scatter(): block = keep + lax.ppermute(send, axis, pairs)  8.52 us
    all_to_all x1, starting transfers between devices, exchange_gather(): return lax.all_to_all(copies, axis, 0, 0).reshape(shape)  6.64 us
    all_to_all x1, starting transfers between devices, exchange_sum(): pieces = lax.all_to_all(stack.reshape(count, -1), axis, 0, 0)  5.28 us
  transfers between devices with their start and end apart: 5, of which 5 were waited for; matrix products, arithmetic and copies ran while one was open for 1% of the time, Pallas kernels for 0%

profile of v8, /device:TPU:6, one launch (start us, length us, event | category | flops | bytes accessed | tf_op | source)
XLA Modules:
  0.0 207.6 jit_solution(1501409622491366579)
XLA Ops:
  1.4 1.4 fusion.12
  2.8 1.4 fusion.13
  7.5 1.4 fusion.45
  9.5 2.5 %psum.28 = f32[2,512]{1,0:T(2,128)S(1)} all-reduce(f32[2,512]{1,0:T(2,128)S(1)} %pad_maximum_fusion.6), channel_id=1, replica_groups=mesh['rows'=64,'chips'=4,'core'=2] {'core'}, use_global_device_ids=true, to_apply=%region_10.0 | all-reduce | flops 1024 | bytes 8192 | tf_op jit(solution)/shard_map/psum | solution.py:35
  11.9 12.3 %psum.29 = f32[2,512]{1,0:T(2,128)S(1)} all-reduce(f32[2,512]{1,0:T(2,128)S(1)} %psum.28), channel_id=1, replica_groups=mesh['rows'=64,'chips'=4,'core'=2] {'chips'}, use_global_device_ids=true, to_apply=%region_11.0 | all-reduce | flops 1024 | bytes 8192 | tf_op jit(solution)/shard_map/psum | solution.py:35
  24.3 3.5 %multiply_reduce_fusion.20 = (f32[512]{0:T(512)S(1)}, f32[512]{0:T(512)S(1)}, f32[512]{0:T(512)S(1)}, f32[512]{0:T(512)S(1)}, f32[512]{0:T(512)S(1)}, /*index=5*...) fusion(f32[512,512]{1,0:T(8,128)S(1)} %get-tuple-element.64, ...), kind=kLoop, calls=%fused_computation.53 | loop fusion | flops 6285312 | bytes 8417280 | tf_op jit(solution)/shard_map/reduce_sum | solution.py:144
  28.8 50.8 %all_to_all.27 = f32[64,1,6144]{2,1,0:T(1,128)} all-to-all(f32[64,1,6144]{2,1,0:T(1,128)S(1)} %broadcast_in_dim.11), channel_id=1, replica_groups=mesh['rows'=64,'chips'=4,'core'=2] {'rows'}, dimensions={0} | all-to-all | bytes 3145728 | tf_op jit(solution)/shard_map/all_to_all | solution.py:50
  79.6 2.4 %reduce_sum.337 = f32[6144]{0:T(1024)S(1)} reduce(f32[64,1,6144]{2,1,0:T(1,128)} %all_to_all.27, f32[]{:T(128)} %constant.75.clone.1), dimensions={0,1}, to_apply=%region_24.0 | reduce | flops 387072 | bytes 1597444 | tf_op jit(solution)/shard_map/reduce_sum | solution.py:50
  82.0 1.8 multiply_reduce_fusion.6
  83.8 2.5 %psum.30 = f32[1,512]{1,0:T(1,128)S(1)} all-reduce(f32[1,512]{1,0:T(1,128)S(1)} %bitcast.36), channel_id=1, replica_groups=mesh['rows'=64,'chips'=4,'core'=2] {'core'}, use_global_device_ids=true, to_apply=%region_29.0 | all-reduce | flops 512 | bytes 4096 | tf_op jit(solution)/shard_map/psum | solution.py:35
  86.3 9.6 %psum.31 = f32[512]{0:T(512)S(1)} all-reduce(f32[512]{0:T(512)S(1)} %bitcast.39), channel_id=1, replica_groups=mesh['rows'=64,'chips'=4,'core'=2] {'chips'}, use_global_device_ids=true, to_apply=%region_30.0 | all-reduce | flops 512 | bytes 4096 | tf_op jit(solution)/shard_map/psum | solution.py:35
  95.9 1.7 multiply_reduce_fusion.3
  97.9 25.7 %all_to_all.28 = f32[64,1,2048]{2,1,0:T(1,128)} all-to-all(f32[64,1,2048]{2,1,0:T(1,128)S(1)} %broadcast_in_dim.12), channel_id=1, replica_groups=mesh['rows'=64,'chips'=4,'core'=2] {'rows'}, dimensions={0} | all-to-all | bytes 1048576 | tf_op jit(solution)/shard_map/all_to_all | solution.py:50
  124.9 3.4 %multiply_convert_fusion = (bf16[512,512]{1,0:T(8,128)(2,1)S(1)}, bf16[512,512]{1,0:T(8,128)(2,1)S(1)}, bf16[512,512]{1,0:T(8,128)(2,1)S(1)}, bf16[512,512]{1,0:T(8,128)(2,1)S(1)}) fusion(f32[512,512]{1,0:T(8,128)} %copy-done.4, f32[512,512]{1,0:T(8,128)S(1)} %get-tuple-element.64, f32[512]{0:T(512)S(1)} %get-tuple-element.42, ...), kind=kLoop, calls=%fused_computation.28 | loop fusion | flops 6291456 | bytes 10498048 | tf_op jit(solution)/shard_map/convert_element_type | solution.py:174
  133.5 5.3 %all-to-all-start.2 = ((f32[64,1,4096]{2,1,0:T(1,128)}), f32[64,1,4096]{2,1,0:T(1,128)S(1)}, u32[]{:S(2)}, u32[]{:S(2)}) async-start(f32[64,1,4096]{2,1,0:T(1,128)} %bitcast.9), calls=%async_computation.2 | async-start | bytes 2097152 | tf_op jit(solution)/shard_map/all_to_all | solution.py:39
  139.2 28.4 %all-to-all-done.2 = f32[64,1,4096]{2,1,0:T(1,128)S(1)} async-done(((f32[64,1,4096]{2,1,0:T(1,128)}), f32[64,1,4096]{2,1,0:T(1,128)S(1)}, u32[]{:S(2)}, u32[]{:S(2)}) %all-to-all-start.2) | async-done | bytes 1048608 | tf_op jit(solution)/shard_map/all_to_all | solution.py:39
  168.7 2.0 broadcast_in_dim.14
  170.7 6.6 %all-to-all-start.3 = ((f32[64,1,4096]{2,1,0:T(1,128)}), f32[64,1,4096]{2,1,0:T(1,128)S(1)}, u32[]{:S(2)}, u32[]{:S(2)}) async-start(f32[64,1,4096]{2,1,0:T(1,128)} %broadcast_in_dim.14), calls=%async_computation.3 | async-start | bytes 2097152 | tf_op jit(solution)/shard_map/all_to_all | solution.py:45
  178.7 4.6 %collective-permute-start = (f32[256,128]{1,0:T(8,128)S(1)}, f32[256,128]{1,0:T(8,128)S(1)}, u32[]{:S(2)}, u32[]{:S(2)}) collective-permute-start(f32[256,128]{1,0:T(8,128)S(1)} %constant_dynamic-slice_fusion.2), channel_id=1, source_target_pairs={{0,4},{1,5},{2,6},{3,7},{4,0},{5,1},{6,2},{7,3},{8,12},{9,13},{10,... | collective-permute-start | bytes 393224 | tf_op jit(solution)/shard_map/ppermute | solution.py:77
  183.3 3.7 %collective-permute-done = f32[256,128]{1,0:T(8,128)S(1)} collective-permute-done((f32[256,128]{1,0:T(8,128)S(1)}, f32[256,128]{1,0:T(8,128)S(1)}, u32[]{:S(2)}, u32[]{:S(2)}) %collective-permute-start) | collective-permute-done | bytes 131104 | tf_op jit(solution)/shard_map/ppermute | solution.py:77
  187.1 2.4 %collective-permute-start.1 = (f32[128,128]{1,0:T(8,128)S(1)}, f32[128,128]{1,0:T(8,128)S(1)}, u32[]{:S(2)}, u32[]{:S(2)}) collective-permute-start(f32[128,128]{1,0:T(8,128)S(1)} %constant_dynamic-slice_fusion.1), channel_id=1, source_target_pairs={{0,2},{1,3},{2,0},{3,1},{4,6},{5,7},{6,4},{7,5},{8,10},{9,11},{10,... | collective-permute-start | bytes 196616 | tf_op jit(solution)/shard_map/ppermute | solution.py:77
  189.6 3.7 %collective-permute-done.1 = f32[128,128]{1,0:T(8,128)S(1)} collective-permute-done((f32[128,128]{1,0:T(8,128)S(1)}, f32[128,128]{1,0:T(8,128)S(1)}, u32[]{:S(2)}, u32[]{:S(2)}) %collective-permute-start.1) | collective-permute-done | bytes 65568 | tf_op jit(solution)/shard_map/ppermute | solution.py:77
  193.3 1.9 collective-permute-start.2
  197.2 9.4 %all-to-all-done.3 = f32[64,1,4096]{2,1,0:T(1,128)S(1)} async-done(((f32[64,1,4096]{2,1,0:T(1,128)}), f32[64,1,4096]{2,1,0:T(1,128)S(1)}, u32[]{:S(2)}, u32[]{:S(2)}) %all-to-all-start.3) | async-done | bytes 1048608 | tf_op jit(solution)/shard_map/all_to_all | solution.py:45
  (100 shorter events, 17.9 us)
Async XLA Ops:
  0.6 3.5 %copy-start.7 = (bf16[512,128]{1,0:T(8,128)(2,1)S(1)}, bf16[512,128]{1,0:T(8,128)(2,1)}, u32[]{:S(2)}) copy-start(bf16[512,128]{1,0:T(8,128)(2,1)} %param.11) | copy-start | bytes 393220
  4.2 4.7 %copy-start.5 = (bf16[2048,128]{1,0:T(8,128)(2,1)}, bf16[2048,128]{1,0:T(8,128)(2,1)S(1)}, u32[]{:S(2)}) copy-start(bf16[2048,128]{1,0:T(8,128)(2,1)S(1)} %fusion.13) | copy-start | bytes 1572868
  4.5 4.4 %copy-start.1 = (f32[512,512]{1,0:T(8,128)}, f32[512,512]{1,0:T(8,128)S(1)}, u32[]{:S(2)}) copy-start(f32[512,512]{1,0:T(8,128)S(1)} %fusion.34) | copy-start | bytes 3145732
  4.9 2.6 %copy-start.2 = (f32[512,512]{1,0:T(8,128)}, f32[512,512]{1,0:T(8,128)S(1)}, u32[]{:S(2)}) copy-start(f32[512,512]{1,0:T(8,128)S(1)} %fusion.29) | copy-start | bytes 3145732
  4.9 1.0 copy-start.16
  4.9 1.2 copy-start.18
  4.9 1.2 copy-start.19
  5.3 1.6 copy-start.3
  8.9 15.4 %copy-start.17 = (s32[512]{0:T(512)S(1)}, s32[512]{0:T(512)}, u32[]{:S(2)}) copy-start(s32[512]{0:T(512)} %param.9) | copy-start | bytes 6148
  128.3 1.2 copy-start.10
  128.3 1.2 copy-start.14
  128.3 2.5 %copy-start.12 = (bf16[512,512]{1,0:T(8,128)(2,1)}, bf16[512,512]{1,0:T(8,128)(2,1)S(1)}, u32[]{:S(2)}) copy-start(bf16[512,512]{1,0:T(8,128)(2,1)S(1)} %get-tuple-element.60) | copy-start | bytes 1572868
  128.3 3.3 %copy-start.8 = (bf16[512,512]{1,0:T(8,128)(2,1)}, bf16[512,512]{1,0:T(8,128)(2,1)S(1)}, u32[]{:S(2)}) copy-start(bf16[512,512]{1,0:T(8,128)(2,1)S(1)} %get-tuple-element.61) | copy-start | bytes 1572868
  128.3 2.0 copy-start
  133.5 5.4 %copy-start.6 = (bf16[2048,128]{1,0:T(8,128)(2,1)S(1)}, bf16[2048,128]{1,0:T(8,128)(2,1)}, u32[]{:S(2)}) copy-start(bf16[2048,128]{1,0:T(8,128)(2,1)} %copy-done.5) | copy-start | bytes 1572868
  133.5 5.4 %copy-start.9 = (bf16[512,512]{1,0:T(8,128)(2,1)S(1)}, bf16[512,512]{1,0:T(8,128)(2,1)}, u32[]{:S(2)}) copy-start(bf16[512,512]{1,0:T(8,128)(2,1)} %copy-done.8) | copy-start | bytes 1572868
  133.5 34.1 %all-to-all-start.2 = ((f32[64,1,4096]{2,1,0:T(1,128)}), f32[64,1,4096]{2,1,0:T(1,128)S(1)}, u32[]{:S(2)}, u32[]{:S(2)}) async-start(f32[64,1,4096]{2,1,0:T(1,128)} %bitcast.9), calls=%async_computation.2 | async-start | bytes 2097152 | tf_op jit(solution)/shard_map/all_to_all | solution.py:39
  168.7 8.6 %copy-start.15 = (bf16[512,512]{1,0:T(8,128)(2,1)S(1)}, bf16[512,512]{1,0:T(8,128)(2,1)}, u32[]{:S(2)}) copy-start(bf16[512,512]{1,0:T(8,128)(2,1)} %copy-done.14) | copy-start | bytes 1572868
  170.7 7.0 %copy-start.13 = (bf16[512,512]{1,0:T(8,128)(2,1)S(1)}, bf16[512,512]{1,0:T(8,128)(2,1)}, u32[]{:S(2)}) copy-start(bf16[512,512]{1,0:T(8,128)(2,1)} %copy-done.12) | copy-start | bytes 1572868
  170.7 36.0 %all-to-all-start.3 = ((f32[64,1,4096]{2,1,0:T(1,128)}), f32[64,1,4096]{2,1,0:T(1,128)S(1)}, u32[]{:S(2)}, u32[]{:S(2)}) async-start(f32[64,1,4096]{2,1,0:T(1,128)} %broadcast_in_dim.14), calls=%async_computation.3 | async-start | bytes 2097152 | tf_op jit(solution)/shard_map/all_to_all | solution.py:45
  177.3 1.0 copy-start.11
  178.7 8.4 %collective-permute-start = (f32[256,128]{1,0:T(8,128)S(1)}, f32[256,128]{1,0:T(8,128)S(1)}, u32[]{:S(2)}, u32[]{:S(2)}) collective-permute-start(f32[256,128]{1,0:T(8,128)S(1)} %constant_dynamic-slice_fusion.2), channel_id=1, source_target_pairs={{0,4},{1,5},{2,6},{3,7},{4,0},{5,1},{6,2},{7,3},{8,12},{9,13},{10,... | collective-permute-start | bytes 393224 | tf_op jit(solution)/shard_map/ppermute | solution.py:77
  187.1 6.2 %collective-permute-start.1 = (f32[128,128]{1,0:T(8,128)S(1)}, f32[128,128]{1,0:T(8,128)S(1)}, u32[]{:S(2)}, u32[]{:S(2)}) collective-permute-start(f32[128,128]{1,0:T(8,128)S(1)} %constant_dynamic-slice_fusion.1), channel_id=1, source_target_pairs={{0,2},{1,3},{2,0},{3,1},{4,6},{5,7},{6,4},{7,5},{8,10},{9,11},{10,... | collective-permute-start | bytes 196616 | tf_op jit(solution)/shard_map/ppermute | solution.py:77
  193.3 3.1 %collective-permute-start.2 = (f32[64,128]{1,0:T(8,128)S(1)}, f32[64,128]{1,0:T(8,128)S(1)}, u32[]{:S(2)}, u32[]{:S(2)}) collective-permute-start(f32[64,128]{1,0:T(8,128)S(1)} %constant_dynamic-slice_fusion), channel_id=1, source_target_pairs={{0,1},{1,0},{2,3},{3,2},{4,5},{5,4},{6,7},{7,6},{8,9},{9,8},{10,11... | collective-permute-start | bytes 98312 | tf_op jit(solution)/shard_map/ppermute | solution.py:77
  (1 other events, 1.0 us)

commit v9 on v8

--- a/solution.py
+++ b/solution.py
@@ -29,6 +29,7 @@
 
 
 COLS = ("chips", "core")
+ROWS = ("slab", "lane")
 
 
 def across_slots(stack):
@@ -50,17 +51,17 @@
     return jnp.sum(lax.all_to_all(copies, axis, 0, 0), axis=0).reshape(stack.shape)
 
 
-def across_queries(stack, count, spread=False):
+def across_queries(stack, count, inner, spread=False):
     if spread:
-        return spread_sum(stack, "rows", count)
+        return spread_sum(spread_sum(stack, "lane", inner), "slab", count // inner)
     if stack.size % count == 0:
-        return exchange_gather(exchange_sum(stack, "rows", count), "rows", count, stack.shape)
+        return exchange_gather(exchange_sum(stack, ROWS, count), ROWS, count, stack.shape)
     if count & (count - 1):
-        return lax.psum(stack, "rows")
+        return lax.psum(stack, ROWS)
     step = 1
     while step < count:
         pairs = [(i, i ^ step) for i in range(count)]
-        stack = stack + lax.ppermute(stack, "rows", pairs)
+        stack = stack + lax.ppermute(stack, ROWS, pairs)
         step *= 2
     return stack
 
@@ -99,12 +100,12 @@
 def whole_sum(block, count, inner):
     bits = [1 << k for k in range(count.bit_length() - 1)]
     if count & (count - 1) or inner >= count or block.shape[0] % (2 * count):
-        return lax.psum(block, "rows")
+        return lax.psum(block, ROWS)
     low = [b for b in bits if b < inner]
     high = [b for b in bits if b >= inner]
     half = block.shape[0] // 2
-    first = butterfly(block[:half], "rows", count, low + high)
-    second = butterfly(block[half:], "rows", count, high + low)
+    first = butterfly(block[:half], ROWS, count, low + high)
+    second = butterfly(block[half:], ROWS, count, high + low)
     return jnp.concatenate([first, second])
 
 
@@ -149,6 +150,7 @@
     summed = across_queries(
         jnp.stack([jnp.concatenate(col_parts), jnp.concatenate(q_parts), jnp.concatenate(t_parts)]),
         count,
+        inner,
         spread=True,
     )
     colsum, qvec, t_one = (summed[0], summed[1], summed[2])
@@ -163,7 +165,7 @@
     for start in starts:
         plan = share[:, None] * kernel_tile(start)
         t_parts.append(jnp.sum(alpha_two[:, None] * plan, axis=0))
-    t_two = across_queries(jnp.concatenate(t_parts)[None, :], count, spread=True)[0]
+    t_two = across_queries(jnp.concatenate(t_parts)[None, :], count, inner, spread=True)[0]
     beta_two = (qvec - t_two) / colsum
     dqhat = jnp.zeros(qhat.shape, jnp.float32)
     dp_parts = []
@@ -199,14 +201,14 @@
         grad_protos = unit_back(whole_sum(dphat, count, inner), phat, plen)
     else:
         own = slots // count
-        first = lax.axis_index("rows") * own
-        summed = exchange_sum(dphat, "rows", count).reshape(own, dphat.shape[1])
+        first = lax.axis_index(ROWS) * own
+        summed = exchange_sum(dphat, ROWS, count).reshape(own, dphat.shape[1])
         piece = unit_back(
             summed,
             lax.dynamic_slice_in_dim(phat, first, own, 0),
             lax.dynamic_slice_in_dim(plen, first, own, 0),
         )
-        grad_protos = exchange_gather(piece, "rows", count, dphat.shape)
+        grad_protos = exchange_gather(piece, ROWS, count, dphat.shape)
     return (grad_queries, grad_protos)
 
 
@@ -233,8 +235,12 @@
     cores = cores_of(mesh)
     if cols % cores:
         cores = 1
-    grid = Mesh(mesh.devices.reshape(rows, cols // cores, cores), ("rows",) + COLS)
-    in_specs = (P("rows", None), P(COLS, None), P(COLS), P("rows"), P(COLS), P("rows", None))
-    out_specs = (P(("rows",) + COLS, None), P(COLS, None))
-    body = functools.partial(local, rows, inner_of(mesh), cols)
+    inner = inner_of(mesh)
+    if rows % inner:
+        inner = rows
+    shape = (rows // inner, inner, cols // cores, cores)
+    grid = Mesh(mesh.devices.reshape(shape), ROWS + COLS)
+    in_specs = (P(ROWS, None), P(COLS, None), P(COLS), P(ROWS), P(COLS), P(ROWS, None))
+    out_specs = (P(ROWS + COLS, None), P(COLS, None))
+    body = functools.partial(local, rows, inner, cols)
     return jax.shard_map(body, mesh=grid, in_specs=in_specs, out_specs=out_specs, check_vma=False)

time: 211 us -> 184 us (0.87)
  blocking collectives: 103 us -> 80.6 us
  waiting for transfers between devices: 46.3 us -> 42.8 us
  local copies, waits for them, and re-layouts: 5.9 us -> 8.9 us
  other arithmetic: 21 us -> 18.5 us
    all_to_all x2 -> x4, blocking collectives: 76.4 us -> 53.4 us  [spread_sum(): lax.all_to_all(copies, axis, 0, 0)]
    unnamed x41 -> x43, local copies, waits for them, and re-layouts: 2.59 us -> 6.39 us
    all_to_all x1, waiting for transfers between devices: 28.4 us -> 25.5 us  [exchange_sum(): pieces = lax.all_to_all(stack.reshape(count, -1), axis, 0, 0)]
where the time goes in v9:
time: 184 us; the launch traced here: 181 us
  blocking collectives  80.6 us (44%)
  waiting for transfers between devices  42.8 us (23%)
  starting transfers between devices  20.1 us (11%)
  other arithmetic  18.5 us (10%)
  matrix products  8.91 us (5%)
  local copies, waits for them, and re-layouts  8.9 us (5%)
    all_to_all x4, blocking collectives, spread_sum(): lax.all_to_all(copies, axis, 0, 0)  53.4 us
    psum x4, blocking collectives, across_slots(): return lax.psum(lax.psum(stack, 'core'), 'chips')  27.3 us
    all_to_all x1, waiting for transfers between devices, exchange_sum(): pieces = lax.all_to_all(stack.reshape(count, -1), axis, 0, 0)  25.5 us
    ppermute x3, waiting for transfers between devices, halving_scatter(): block = keep + lax.ppermute(send, axis, pairs)  9.02 us
    ppermute x3, starting transfers between devices, halving_scatter(): block = keep + lax.ppermute(send, axis, pairs)  8.42 us
    all_to_all x1, waiting for transfers between devices, exchange_gather(): return lax.all_to_all(copies, axis, 0, 0).reshape(shape)  8.21 us
    all_to_all x1, starting transfers between devices, exchange_gather(): return lax.all_to_all(copies, axis, 0, 0).reshape(shape)  6.71 us
    unnamed x43, local copies, waits for them, and re-layouts  6.39 us
  transfers between devices with their start and end apart: 5, of which 5 were waited for; matrix products, arithmetic and copies ran while one was open for 1% of the time, Pallas kernels for 0%

profile of v9, /device:TPU:6, one launch (start us, length us, event | category | flops | bytes accessed | tf_op | source)
XLA Modules:
  0.0 181.1 jit_solution(11427858850871300821)
XLA Ops:
  1.4 1.4 fusion.12
  8.5 1.4 fusion.45
  10.5 2.5 %psum.28 = f32[2,512]{1,0:T(2,128)S(1)} all-reduce(f32[2,512]{1,0:T(2,128)S(1)} %pad_maximum_fusion.6), channel_id=1, replica_groups=mesh['slab'=8,'lane'=8,'chips'=4,'core'=2] {'core'}, use_global_device_ids=true, to_apply=%region_10.0 | all-reduce | flops 1024 | bytes 8192 | tf_op jit(solution)/shard_map/psum | solution.py:36
  13.0 12.3 %psum.29 = f32[2,512]{1,0:T(2,128)S(1)} all-reduce(f32[2,512]{1,0:T(2,128)S(1)} %psum.28), channel_id=1, replica_groups=mesh['slab'=8,'lane'=8,'chips'=4,'core'=2] {'chips'}, use_global_device_ids=true, to_apply=%region_11.0 | all-reduce | flops 1024 | bytes 8192 | tf_op jit(solution)/shard_map/psum | solution.py:36
  26.0 3.5 %multiply_reduce_fusion.20 = (f32[512]{0:T(512)S(1)}, f32[512]{0:T(512)S(1)}, f32[512]{0:T(512)S(1)}, f32[512]{0:T(512)S(1)}, f32[512]{0:T(512)S(1)}, /*index=5*...) fusion(f32[512,512]{1,0:T(8,128)S(1)} %get-tuple-element.64, ...), kind=kLoop, calls=%fused_computation.53 | loop fusion | flops 6285312 | bytes 8417280 | tf_op jit(solution)/shard_map/reduce_sum | solution.py:145
  29.8 15.1 %all_to_all.39 = f32[8,1,6144]{2,1,0:T(1,128)} all-to-all(f32[8,1,6144]{2,1,0:T(1,128)S(1)} %broadcast_in_dim.15), channel_id=1, replica_groups=mesh['slab'=8,'lane'=8,'chips'=4,'core'=2] {'lane'}, dimensions={0} | all-to-all | bytes 393216 | tf_op jit(solution)/shard_map/all_to_all | solution.py:51
  46.1 16.8 %all_to_all.40 = f32[8,1,6144]{2,1,0:T(1,128)} all-to-all(f32[8,1,6144]{2,1,0:T(1,128)S(1)} %broadcast_in_dim.16), channel_id=1, replica_groups=mesh['slab'=8,'lane'=8,'chips'=4,'core'=2] {'slab'}, dimensions={0} | all-to-all | bytes 393216 | tf_op jit(solution)/shard_map/all_to_all | solution.py:51
  64.0 1.8 multiply_reduce_fusion.6
  65.8 2.5 %psum.30 = f32[1,512]{1,0:T(1,128)S(1)} all-reduce(f32[1,512]{1,0:T(1,128)S(1)} %bitcast.36), channel_id=1, replica_groups=mesh['slab'=8,'lane'=8,'chips'=4,'core'=2] {'core'}, use_global_device_ids=true, to_apply=%region_30.0 | all-reduce | flops 512 | bytes 4096 | tf_op jit(solution)/shard_map/psum | solution.py:36
  68.2 10.0 %psum.31 = f32[512]{0:T(512)S(1)} all-reduce(f32[512]{0:T(512)S(1)} %bitcast.39), channel_id=1, replica_groups=mesh['slab'=8,'lane'=8,'chips'=4,'core'=2] {'chips'}, use_global_device_ids=true, to_apply=%region_31.0 | all-reduce | flops 512 | bytes 4096 | tf_op jit(solution)/shard_map/psum | solution.py:36
  78.2 1.7 multiply_reduce_fusion.3
  80.0 10.8 %all_to_all.41 = f32[8,1,2048]{2,1,0:T(1,128)S(1)} all-to-all(f32[8,1,2048]{2,1,0:T(1,128)S(1)} %broadcast_in_dim.17), channel_id=1, replica_groups=mesh['slab'=8,'lane'=8,'chips'=4,'core'=2] {'lane'}, dimensions={0} | all-to-all | bytes 131072 | tf_op jit(solution)/shard_map/all_to_all | solution.py:51
  90.9 10.8 %all_to_all.42 = f32[8,1,2048]{2,1,0:T(1,128)S(1)} all-to-all(f32[8,1,2048]{2,1,0:T(1,128)S(1)} %broadcast_in_dim.18), channel_id=1, replica_groups=mesh['slab'=8,'lane'=8,'chips'=4,'core'=2] {'slab'}, dimensions={0} | all-to-all | bytes 131072 | tf_op jit(solution)/shard_map/all_to_all | solution.py:51
  101.7 3.4 %multiply_convert_fusion = (bf16[512,512]{1,0:T(8,128)(2,1)S(1)}, bf16[512,512]{1,0:T(8,128)(2,1)S(1)}, bf16[512,512]{1,0:T(8,128)(2,1)S(1)}, bf16[512,512]{1,0:T(8,128)(2,1)S(1)}) fusion(f32[512,512]{1,0:T(8,128)} %copy-done.4, f32[512,512]{1,0:T(8,128)S(1)} %get-tuple-element.64, f32[512]{0:T(512)S(1)} %get-tuple-element.42, ...), kind=kLoop, calls=%fused_computation.28 | loop fusion | flops 6291456 | bytes 10498048 | tf_op jit(solution)/shard_map/convert_element_type | solution.py:176
  110.3 5.0 %all-to-all-start.4 = ((f32[64,1,4096]{2,1,0:T(1,128)}), f32[64,1,4096]{2,1,0:T(1,128)S(1)}, u32[]{:S(2)}, u32[]{:S(2)}) async-start(f32[64,1,4096]{2,1,0:T(1,128)} %bitcast.9), calls=%async_computation.4 | async-start | bytes 2097152 | tf_op jit(solution)/shard_map/all_to_all | solution.py:40
  115.7 25.5 %all-to-all-done.4 = f32[64,1,4096]{2,1,0:T(1,128)S(1)} async-done(((f32[64,1,4096]{2,1,0:T(1,128)}), f32[64,1,4096]{2,1,0:T(1,128)S(1)}, u32[]{:S(2)}, u32[]{:S(2)}) %all-to-all-start.4) | async-done | bytes 1048608 | tf_op jit(solution)/shard_map/all_to_all | solution.py:40
  142.3 2.0 %broadcast_in_dim.20 = f32[64,1,4096]{2,1,0:T(1,128)} broadcast(f32[4096]{0:T(1024)S(1)} %fusion.43), dimensions={2} | broadcast | bytes 1064960 | tf_op jit(solution)/shard_map/broadcast_in_dim | solution.py:45
  144.2 6.7 %all-to-all-start.5 = ((f32[64,1,4096]{2,1,0:T(1,128)}), f32[64,1,4096]{2,1,0:T(1,128)S(1)}, u32[]{:S(2)}, u32[]{:S(2)}) async-start(f32[64,1,4096]{2,1,0:T(1,128)} %broadcast_in_dim.20), calls=%async_computation.5 | async-start | bytes 2097152 | tf_op jit(solution)/shard_map/all_to_all | solution.py:46
  153.4 4.6 %collective-permute-start = (f32[256,128]{1,0:T(8,128)S(1)}, f32[256,128]{1,0:T(8,128)S(1)}, u32[]{:S(2)}, u32[]{:S(2)}) collective-permute-start(f32[256,128]{1,0:T(8,128)S(1)} %constant_dynamic-slice_fusion.2), channel_id=1, source_target_pairs={{0,4},{1,5},{2,6},{3,7},{4,0},{5,1},{6,2},{7,3},{8,12},{9,13},{10,... | collective-permute-start | bytes 393224 | tf_op jit(solution)/shard_map/ppermute | solution.py:78
  158.0 3.7 %collective-permute-done = f32[256,128]{1,0:T(8,128)S(1)} collective-permute-done((f32[256,128]{1,0:T(8,128)S(1)}, f32[256,128]{1,0:T(8,128)S(1)}, u32[]{:S(2)}, u32[]{:S(2)}) %collective-permute-start) | collective-permute-done | bytes 131104 | tf_op jit(solution)/shard_map/ppermute | solution.py:78
  161.8 1.9 %collective-permute-start.1 = (f32[128,128]{1,0:T(8,128)S(1)}, f32[128,128]{1,0:T(8,128)S(1)}, u32[]{:S(2)}, u32[]{:S(2)}) collective-permute-start(f32[128,128]{1,0:T(8,128)S(1)} %constant_dynamic-slice_fusion.1), channel_id=1, source_target_pairs={{0,2},{1,3},{2,0},{3,1},{4,6},{5,7},{6,4},{7,5},{8,10},{9,11},{10,... | collective-permute-start | bytes 196616 | tf_op jit(solution)/shard_map/ppermute | solution.py:78
  163.7 4.2 %collective-permute-done.1 = f32[128,128]{1,0:T(8,128)S(1)} collective-permute-done((f32[128,128]{1,0:T(8,128)S(1)}, f32[128,128]{1,0:T(8,128)S(1)}, u32[]{:S(2)}, u32[]{:S(2)}) %collective-permute-start.1) | collective-permute-done | bytes 65568 | tf_op jit(solution)/shard_map/ppermute | solution.py:78
  168.0 1.9 %collective-permute-start.2 = (f32[64,128]{1,0:T(8,128)S(1)}, f32[64,128]{1,0:T(8,128)S(1)}, u32[]{:S(2)}, u32[]{:S(2)}) collective-permute-start(f32[64,128]{1,0:T(8,128)S(1)} %constant_dynamic-slice_fusion), channel_id=1, source_target_pairs={{0,1},{1,0},{2,3},{3,2},{4,5},{5,4},{6,7},{7,6},{8,9},{9,8},{10,11... | collective-permute-start | bytes 98312 | tf_op jit(solution)/shard_map/ppermute | solution.py:78
  171.9 8.2 %all-to-all-done.5 = f32[64,1,4096]{2,1,0:T(1,128)S(1)} async-done(((f32[64,1,4096]{2,1,0:T(1,128)}), f32[64,1,4096]{2,1,0:T(1,128)S(1)}, u32[]{:S(2)}, u32[]{:S(2)}) %all-to-all-start.5) | async-done | bytes 1048608 | tf_op jit(solution)/shard_map/all_to_all | solution.py:46
  (108 shorter events, 22.2 us)
Async XLA Ops:
  0.6 2.2 %copy-start.16 = (bf16[2048,128]{1,0:T(8,128)(2,1)S(1)}, bf16[2048,128]{1,0:T(8,128)(2,1)}, u32[]{:S(2)}) copy-start(bf16[2048,128]{1,0:T(8,128)(2,1)} %param.7) | copy-start | bytes 1572868
  2.8 0.9 copy-start.7
  3.7 6.2 %copy-start.5 = (bf16[2048,128]{1,0:T(8,128)(2,1)}, bf16[2048,128]{1,0:T(8,128)(2,1)S(1)}, u32[]{:S(2)}) copy-start(bf16[2048,128]{1,0:T(8,128)(2,1)S(1)} %fusion.13) | copy-start | bytes 1572868
  4.1 5.9 %copy-start.1 = (f32[512,512]{1,0:T(8,128)}, f32[512,512]{1,0:T(8,128)S(1)}, u32[]{:S(2)}) copy-start(f32[512,512]{1,0:T(8,128)S(1)} %fusion.34) | copy-start | bytes 3145732
  4.4 4.1 %copy-start.2 = (f32[512,512]{1,0:T(8,128)}, f32[512,512]{1,0:T(8,128)S(1)}, u32[]{:S(2)}) copy-start(f32[512,512]{1,0:T(8,128)S(1)} %fusion.29) | copy-start | bytes 3145732
  4.8 3.2 %copy-start.3 = (f32[512,512]{1,0:T(8,128)}, f32[512,512]{1,0:T(8,128)S(1)}, u32[]{:S(2)}) copy-start(f32[512,512]{1,0:T(8,128)S(1)} %fusion.25) | copy-start | bytes 3145732
  4.8 1.0 copy-start.17
  5.9 2.1 %copy-start.4 = (f32[512,512]{1,0:T(8,128)}, f32[512,512]{1,0:T(8,128)S(1)}, u32[]{:S(2)}) copy-start(f32[512,512]{1,0:T(8,128)S(1)} %fusion.21) | copy-start | bytes 3145732
  5.9 0.7 copy-start.19
  105.1 0.9 copy-start.10
  105.1 1.0 copy-start.14
  105.1 2.4 %copy-start.12 = (bf16[512,512]{1,0:T(8,128)(2,1)}, bf16[512,512]{1,0:T(8,128)(2,1)S(1)}, u32[]{:S(2)}) copy-start(bf16[512,512]{1,0:T(8,128)(2,1)S(1)} %get-tuple-element.60) | copy-start | bytes 1572868
  105.1 3.3 %copy-start.8 = (bf16[512,512]{1,0:T(8,128)(2,1)}, bf16[512,512]{1,0:T(8,128)(2,1)S(1)}, u32[]{:S(2)}) copy-start(bf16[512,512]{1,0:T(8,128)(2,1)S(1)} %get-tuple-element.61) | copy-start | bytes 1572868
  105.5 1.6 copy-start
  110.3 5.1 %copy-start.6 = (bf16[2048,128]{1,0:T(8,128)(2,1)S(1)}, bf16[2048,128]{1,0:T(8,128)(2,1)}, u32[]{:S(2)}) copy-start(bf16[2048,128]{1,0:T(8,128)(2,1)} %copy-done.5) | copy-start | bytes 1572868
  110.3 5.1 %copy-start.9 = (bf16[512,512]{1,0:T(8,128)(2,1)S(1)}, bf16[512,512]{1,0:T(8,128)(2,1)}, u32[]{:S(2)}) copy-start(bf16[512,512]{1,0:T(8,128)(2,1)} %copy-done.8) | copy-start | bytes 1572868
  110.3 30.9 %all-to-all-start.4 = ((f32[64,1,4096]{2,1,0:T(1,128)}), f32[64,1,4096]{2,1,0:T(1,128)S(1)}, u32[]{:S(2)}, u32[]{:S(2)}) async-start(f32[64,1,4096]{2,1,0:T(1,128)} %bitcast.9), calls=%async_computation.4 | async-start | bytes 2097152 | tf_op jit(solution)/shard_map/all_to_all | solution.py:40
  144.2 6.7 %copy-start.15 = (bf16[512,512]{1,0:T(8,128)(2,1)S(1)}, bf16[512,512]{1,0:T(8,128)(2,1)}, u32[]{:S(2)}) copy-start(bf16[512,512]{1,0:T(8,128)(2,1)} %copy-done.14) | copy-start | bytes 1572868
  144.2 35.9 %all-to-all-start.5 = ((f32[64,1,4096]{2,1,0:T(1,128)}), f32[64,1,4096]{2,1,0:T(1,128)S(1)}, u32[]{:S(2)}, u32[]{:S(2)}) async-start(f32[64,1,4096]{2,1,0:T(1,128)} %broadcast_in_dim.20), calls=%async_computation.5 | async-start | bytes 2097152 | tf_op jit(solution)/shard_map/all_to_all | solution.py:46
  151.0 1.0 copy-start.13
  152.0 1.0 copy-start.11
  153.4 8.4 %collective-permute-start = (f32[256,128]{1,0:T(8,128)S(1)}, f32[256,128]{1,0:T(8,128)S(1)}, u32[]{:S(2)}, u32[]{:S(2)}) collective-permute-start(f32[256,128]{1,0:T(8,128)S(1)} %constant_dynamic-slice_fusion.2), channel_id=1, source_target_pairs={{0,4},{1,5},{2,6},{3,7},{4,0},{5,1},{6,2},{7,3},{8,12},{9,13},{10,... | collective-permute-start | bytes 393224 | tf_op jit(solution)/shard_map/ppermute | solution.py:78
  161.8 6.2 %collective-permute-start.1 = (f32[128,128]{1,0:T(8,128)S(1)}, f32[128,128]{1,0:T(8,128)S(1)}, u32[]{:S(2)}, u32[]{:S(2)}) collective-permute-start(f32[128,128]{1,0:T(8,128)S(1)} %constant_dynamic-slice_fusion.1), channel_id=1, source_target_pairs={{0,2},{1,3},{2,0},{3,1},{4,6},{5,7},{6,4},{7,5},{8,10},{9,11},{10,... | collective-permute-start | bytes 196616 | tf_op jit(solution)/shard_map/ppermute | solution.py:78
  168.0 3.1 %collective-permute-start.2 = (f32[64,128]{1,0:T(8,128)S(1)}, f32[64,128]{1,0:T(8,128)S(1)}, u32[]{:S(2)}, u32[]{:S(2)}) collective-permute-start(f32[64,128]{1,0:T(8,128)S(1)} %constant_dynamic-slice_fusion), channel_id=1, source_target_pairs={{0,1},{1,0},{2,3},{3,2},{4,5},{5,4},{6,7},{7,6},{8,9},{9,8},{10,11... | collective-permute-start | bytes 98312 | tf_op jit(solution)/shard_map/ppermute | solution.py:78
  (2 other events, 1.4 us)

commit v10 on v9

--- a/solution.py
+++ b/solution.py
@@ -51,7 +51,10 @@
     return jnp.sum(lax.all_to_all(copies, axis, 0, 0), axis=0).reshape(stack.shape)
 
 
-def across_queries(stack, count, inner, spread=False):
+def across_queries(stack, count, inner, spread=False, mixed=False):
+    if mixed and stack.size % inner == 0:
+        piece = spread_sum(exchange_sum(stack, "lane", inner), "slab", count // inner)
+        return exchange_gather(piece, "lane", inner, stack.shape)
     if spread:
         return spread_sum(spread_sum(stack, "lane", inner), "slab", count // inner)
     if stack.size % count == 0:
@@ -152,6 +155,7 @@
         count,
         inner,
         spread=True,
+        mixed=True,
     )
     colsum, qvec, t_one = (summed[0], summed[1], summed[2])
     beta_one = (qvec - t_one) / colsum

time: 184 us -> 188 us (1.022)
  blocking collectives: 80.6 us -> 86.9 us
  other arithmetic: 18.5 us -> 16.5 us
    all_to_all x0 -> x2, blocking collectives: none -> 23.3 us  [the longest x1 13 us: exchange_sum(): pieces = lax.all_to_all(stack.reshape(count, -1), axis, 0, 0)]
    all_to_all x4 -> x3, blocking collectives: 53.4 us -> 36.2 us  [spread_sum(): lax.all_to_all(copies, axis, 0, 0)]
    reduce_sum x4 -> x3, other arithmetic: 2.26 us -> 0.14 us  [spread_sum(): jnp.sum(lax.all_to_all(copies, axis, 0, 0), axis=0).reshape(stack.shape)]
where the time goes in v10:
time: 188 us; the launch traced here: 185 us
  blocking collectives  86.9 us (46%)
  waiting for transfers between devices  42.8 us (23%)
  starting transfers between devices  20.1 us (11%)
  other arithmetic  16.5 us (9%)
  matrix products  8.89 us (5%)
  local copies, waits for them, and re-layouts  8.79 us (5%)
    all_to_all x3, blocking collectives, spread_sum(): lax.all_to_all(copies, axis, 0, 0)  36.2 us
    psum x4, blocking collectives, across_slots(): return lax.psum(lax.psum(stack, 'core'), 'chips')  27.4 us
    all_to_all x1, waiting for transfers between devices, exchange_sum(): pieces = lax.all_to_all(stack.reshape(count, -1), axis, 0, 0)  25.5 us
    all_to_all x1, blocking collectives, exchange_sum(): pieces = lax.all_to_all(stack.reshape(count, -1), axis, 0, 0)  13 us
    all_to_all x1, blocking collectives, exchange_gather(): return lax.all_to_all(copies, axis, 0, 0).reshape(shape)  10.3 us
    ppermute x3, waiting for transfers between devices, halving_scatter(): block = keep + lax.ppermute(send, axis, pairs)  9 us
    ppermute x3, starting transfers between devices, halving_scatter(): block = keep + lax.ppermute(send, axis, pairs)  8.44 us
    all_to_all x1, waiting for transfers between devices, exchange_gather(): return lax.all_to_all(copies, axis, 0, 0).reshape(shape)  8.22 us
  transfers between devices with their start and end apart: 5, of which 5 were waited for; matrix products, arithmetic and copies ran while one was open for 1% of the time, Pallas kernels for 0%

profile of v10, /device:TPU:6, one launch (start us, length us, event | category | flops | bytes accessed | tf_op | source)
XLA Modules:
  0.0 185.2 jit_solution(3085207820427326806)
XLA Ops:
  8.5 1.4 fusion.44
  10.5 2.5 %psum.28 = f32[2,512]{1,0:T(2,128)S(1)} all-reduce(f32[2,512]{1,0:T(2,128)S(1)} %pad_maximum_fusion.6), channel_id=1, replica_groups=mesh['slab'=8,'lane'=8,'chips'=4,'core'=2] {'core'}, use_global_device_ids=true, to_apply=%region_10.0 | all-reduce | flops 1024 | bytes 8192 | tf_op jit(solution)/shard_map/psum | solution.py:36
  13.0 12.3 %psum.29 = f32[2,512]{1,0:T(2,128)S(1)} all-reduce(f32[2,512]{1,0:T(2,128)S(1)} %psum.28), channel_id=1, replica_groups=mesh['slab'=8,'lane'=8,'chips'=4,'core'=2] {'chips'}, use_global_device_ids=true, to_apply=%region_11.0 | all-reduce | flops 1024 | bytes 8192 | tf_op jit(solution)/shard_map/psum | solution.py:36
  26.0 3.5 %multiply_reduce_fusion.20 = (f32[512]{0:T(512)S(1)}, f32[512]{0:T(512)S(1)}, f32[512]{0:T(512)S(1)}, f32[512]{0:T(512)S(1)}, f32[512]{0:T(512)S(1)}, /*index=5*...) fusion(f32[512,512]{1,0:T(8,128)S(1)} %get-tuple-element.67, ...), kind=kLoop, calls=%fused_computation.53 | loop fusion | flops 6285312 | bytes 8417280 | tf_op jit(solution)/shard_map/reduce_sum | solution.py:148
  29.7 13.0 %all_to_all.48 = f32[8,1,768]{2,1,0:T(1,128)S(1)} all-to-all(f32[8,1,768]{2,1,0:T(1,128)S(1)} %all_to_all.32), channel_id=1, replica_groups=mesh['slab'=8,'lane'=8,'chips'=4,'core'=2] {'lane'}, dimensions={0} | all-to-all | bytes 49152 | tf_op jit(solution)/shard_map/all_to_all | solution.py:40
  42.8 14.7 %all_to_all.49 = f32[8,1,768]{2,1,0:T(1,128)S(1)} all-to-all(f32[8,1,768]{2,1,0:T(1,128)S(1)} %broadcast_in_dim.12), channel_id=1, replica_groups=mesh['slab'=8,'lane'=8,'chips'=4,'core'=2] {'slab'}, dimensions={0} | all-to-all | bytes 49152 | tf_op jit(solution)/shard_map/all_to_all | solution.py:51
  57.6 10.3 %all_to_all.50 = f32[8,1,768]{2,1,0:T(1,128)S(1)} all-to-all(f32[8,1,768]{2,1,0:T(1,128)S(1)} %broadcast_in_dim.13), channel_id=1, replica_groups=mesh['slab'=8,'lane'=8,'chips'=4,'core'=2] {'lane'}, dimensions={0} | all-to-all | bytes 49152 | tf_op jit(solution)/shard_map/all_to_all | solution.py:46
  68.0 1.8 multiply_reduce_fusion.6
  69.8 2.5 %psum.30 = f32[1,512]{1,0:T(1,128)S(1)} all-reduce(f32[1,512]{1,0:T(1,128)S(1)} %bitcast.44), channel_id=1, replica_groups=mesh['slab'=8,'lane'=8,'chips'=4,'core'=2] {'core'}, use_global_device_ids=true, to_apply=%region_30.0 | all-reduce | flops 512 | bytes 4096 | tf_op jit(solution)/shard_map/psum | solution.py:36
  72.3 10.1 %psum.31 = f32[512]{0:T(512)S(1)} all-reduce(f32[512]{0:T(512)S(1)} %bitcast.47), channel_id=1, replica_groups=mesh['slab'=8,'lane'=8,'chips'=4,'core'=2] {'chips'}, use_global_device_ids=true, to_apply=%region_31.0 | all-reduce | flops 512 | bytes 4096 | tf_op jit(solution)/shard_map/psum | solution.py:36
  82.4 1.7 multiply_reduce_fusion.3
  84.2 10.8 %all_to_all.51 = f32[8,1,2048]{2,1,0:T(1,128)S(1)} all-to-all(f32[8,1,2048]{2,1,0:T(1,128)S(1)} %broadcast_in_dim.14), channel_id=1, replica_groups=mesh['slab'=8,'lane'=8,'chips'=4,'core'=2] {'lane'}, dimensions={0} | all-to-all | bytes 131072 | tf_op jit(solution)/shard_map/all_to_all | solution.py:51
  95.0 10.8 %all_to_all.52 = f32[8,1,2048]{2,1,0:T(1,128)S(1)} all-to-all(f32[8,1,2048]{2,1,0:T(1,128)S(1)} %broadcast_in_dim.15), channel_id=1, replica_groups=mesh['slab'=8,'lane'=8,'chips'=4,'core'=2] {'slab'}, dimensions={0} | all-to-all | bytes 131072 | tf_op jit(solution)/shard_map/all_to_all | solution.py:51
  105.9 3.4 %multiply_convert_fusion = (bf16[512,512]{1,0:T(8,128)(2,1)S(1)}, bf16[512,512]{1,0:T(8,128)(2,1)S(1)}, bf16[512,512]{1,0:T(8,128)(2,1)S(1)}, bf16[512,512]{1,0:T(8,128)(2,1)S(1)}) fusion(f32[512,512]{1,0:T(8,128)} %copy-done.4, f32[512,512]{1,0:T(8,128)S(1)} %get-tuple-element.67, f32[512]{0:T(512)S(1)} %get-tuple-element.45, ...), kind=kLoop, calls=%fused_computation.28 | loop fusion | flops 6291456 | bytes 10498048 | tf_op jit(solution)/shard_map/convert_element_type | solution.py:180
  114.4 5.0 %all-to-all-start.5 = ((f32[64,1,4096]{2,1,0:T(1,128)}), f32[64,1,4096]{2,1,0:T(1,128)S(1)}, u32[]{:S(2)}, u32[]{:S(2)}) async-start(f32[64,1,4096]{2,1,0:T(1,128)} %bitcast.12), calls=%async_computation.5 | async-start | bytes 2097152 | tf_op jit(solution)/shard_map/all_to_all | solution.py:40
  119.8 25.5 %all-to-all-done.5 = f32[64,1,4096]{2,1,0:T(1,128)S(1)} async-done(((f32[64,1,4096]{2,1,0:T(1,128)}), f32[64,1,4096]{2,1,0:T(1,128)S(1)}, u32[]{:S(2)}, u32[]{:S(2)}) %all-to-all-start.5) | async-done | bytes 1048608 | tf_op jit(solution)/shard_map/all_to_all | solution.py:40
  146.4 2.0 %broadcast_in_dim.17 = f32[64,1,4096]{2,1,0:T(1,128)} broadcast(f32[4096]{0:T(1024)S(1)} %fusion.43), dimensions={2} | broadcast | bytes 1064960 | tf_op jit(solution)/shard_map/broadcast_in_dim | solution.py:45
  148.4 6.7 %all-to-all-start.6 = ((f32[64,1,4096]{2,1,0:T(1,128)}), f32[64,1,4096]{2,1,0:T(1,128)S(1)}, u32[]{:S(2)}, u32[]{:S(2)}) async-start(f32[64,1,4096]{2,1,0:T(1,128)} %broadcast_in_dim.17), calls=%async_computation.6 | async-start | bytes 2097152 | tf_op jit(solution)/shard_map/all_to_all | solution.py:46
  157.5 4.6 %collective-permute-start = (f32[256,128]{1,0:T(8,128)S(1)}, f32[256,128]{1,0:T(8,128)S(1)}, u32[]{:S(2)}, u32[]{:S(2)}) collective-permute-start(f32[256,128]{1,0:T(8,128)S(1)} %constant_dynamic-slice_fusion.2), channel_id=1, source_target_pairs={{0,4},{1,5},{2,6},{3,7},{4,0},{5,1},{6,2},{7,3},{8,12},{9,13},{10,... | collective-permute-start | bytes 393224 | tf_op jit(solution)/shard_map/ppermute | solution.py:81
  162.2 3.7 %collective-permute-done = f32[256,128]{1,0:T(8,128)S(1)} collective-permute-done((f32[256,128]{1,0:T(8,128)S(1)}, f32[256,128]{1,0:T(8,128)S(1)}, u32[]{:S(2)}, u32[]{:S(2)}) %collective-permute-start) | collective-permute-done | bytes 131104 | tf_op jit(solution)/shard_map/ppermute | solution.py:81
  165.9 1.9 %collective-permute-start.1 = (f32[128,128]{1,0:T(8,128)S(1)}, f32[128,128]{1,0:T(8,128)S(1)}, u32[]{:S(2)}, u32[]{:S(2)}) collective-permute-start(f32[128,128]{1,0:T(8,128)S(1)} %constant_dynamic-slice_fusion.1), channel_id=1, source_target_pairs={{0,2},{1,3},{2,0},{3,1},{4,6},{5,7},{6,4},{7,5},{8,10},{9,11},{10,... | collective-permute-start | bytes 196616 | tf_op jit(solution)/shard_map/ppermute | solution.py:81
  167.9 4.2 %collective-permute-done.1 = f32[128,128]{1,0:T(8,128)S(1)} collective-permute-done((f32[128,128]{1,0:T(8,128)S(1)}, f32[128,128]{1,0:T(8,128)S(1)}, u32[]{:S(2)}, u32[]{:S(2)}) %collective-permute-start.1) | collective-permute-done | bytes 65568 | tf_op jit(solution)/shard_map/ppermute | solution.py:81
  172.1 1.9 %collective-permute-start.2 = (f32[64,128]{1,0:T(8,128)S(1)}, f32[64,128]{1,0:T(8,128)S(1)}, u32[]{:S(2)}, u32[]{:S(2)}) collective-permute-start(f32[64,128]{1,0:T(8,128)S(1)} %constant_dynamic-slice_fusion), channel_id=1, source_target_pairs={{0,1},{1,0},{2,3},{3,2},{4,5},{5,4},{6,7},{7,6},{8,9},{9,8},{10,11... | collective-permute-start | bytes 98312 | tf_op jit(solution)/shard_map/ppermute | solution.py:81
  176.0 8.2 %all-to-all-done.6 = f32[64,1,4096]{2,1,0:T(1,128)S(1)} async-done(((f32[64,1,4096]{2,1,0:T(1,128)}), f32[64,1,4096]{2,1,0:T(1,128)S(1)}, u32[]{:S(2)}, u32[]{:S(2)}) %all-to-all-start.6) | async-done | bytes 1048608 | tf_op jit(solution)/shard_map/all_to_all | solution.py:46
  (112 shorter events, 21.4 us)
Async XLA Ops:
  0.6 2.2 %copy-start.16 = (bf16[2048,128]{1,0:T(8,128)(2,1)S(1)}, bf16[2048,128]{1,0:T(8,128)(2,1)}, u32[]{:S(2)}) copy-start(bf16[2048,128]{1,0:T(8,128)(2,1)} %param.7) | copy-start | bytes 1572868
  2.8 0.9 copy-start.7
  3.7 6.2 %copy-start.5 = (bf16[2048,128]{1,0:T(8,128)(2,1)}, bf16[2048,128]{1,0:T(8,128)(2,1)S(1)}, u32[]{:S(2)}) copy-start(bf16[2048,128]{1,0:T(8,128)(2,1)S(1)} %fusion.13) | copy-start | bytes 1572868
  4.1 5.9 %copy-start.1 = (f32[512,512]{1,0:T(8,128)}, f32[512,512]{1,0:T(8,128)S(1)}, u32[]{:S(2)}) copy-start(f32[512,512]{1,0:T(8,128)S(1)} %fusion.34) | copy-start | bytes 3145732
  4.4 4.1 %copy-start.2 = (f32[512,512]{1,0:T(8,128)}, f32[512,512]{1,0:T(8,128)S(1)}, u32[]{:S(2)}) copy-start(f32[512,512]{1,0:T(8,128)S(1)} %fusion.29) | copy-start | bytes 3145732
  4.8 3.2 %copy-start.3 = (f32[512,512]{1,0:T(8,128)}, f32[512,512]{1,0:T(8,128)S(1)}, u32[]{:S(2)}) copy-start(f32[512,512]{1,0:T(8,128)S(1)} %fusion.25) | copy-start | bytes 3145732
  4.8 1.0 copy-start.17
  5.9 2.1 %copy-start.4 = (f32[512,512]{1,0:T(8,128)}, f32[512,512]{1,0:T(8,128)S(1)}, u32[]{:S(2)}) copy-start(f32[512,512]{1,0:T(8,128)S(1)} %fusion.21) | copy-start | bytes 3145732
  5.9 0.7 copy-start.19
  109.2 0.9 copy-start.10
  109.2 1.0 copy-start.14
  109.3 2.4 %copy-start.12 = (bf16[512,512]{1,0:T(8,128)(2,1)}, bf16[512,512]{1,0:T(8,128)(2,1)S(1)}, u32[]{:S(2)}) copy-start(bf16[512,512]{1,0:T(8,128)(2,1)S(1)} %get-tuple-element.63) | copy-start | bytes 1572868
  109.3 3.3 %copy-start.8 = (bf16[512,512]{1,0:T(8,128)(2,1)}, bf16[512,512]{1,0:T(8,128)(2,1)S(1)}, u32[]{:S(2)}) copy-start(bf16[512,512]{1,0:T(8,128)(2,1)S(1)} %get-tuple-element.64) | copy-start | bytes 1572868
  109.6 1.6 copy-start
  114.4 5.1 %copy-start.6 = (bf16[2048,128]{1,0:T(8,128)(2,1)S(1)}, bf16[2048,128]{1,0:T(8,128)(2,1)}, u32[]{:S(2)}) copy-start(bf16[2048,128]{1,0:T(8,128)(2,1)} %copy-done.5) | copy-start | bytes 1572868
  114.4 5.1 %copy-start.9 = (bf16[512,512]{1,0:T(8,128)(2,1)S(1)}, bf16[512,512]{1,0:T(8,128)(2,1)}, u32[]{:S(2)}) copy-start(bf16[512,512]{1,0:T(8,128)(2,1)} %copy-done.8) | copy-start | bytes 1572868
  114.4 30.9 %all-to-all-start.5 = ((f32[64,1,4096]{2,1,0:T(1,128)}), f32[64,1,4096]{2,1,0:T(1,128)S(1)}, u32[]{:S(2)}, u32[]{:S(2)}) async-start(f32[64,1,4096]{2,1,0:T(1,128)} %bitcast.12), calls=%async_computation.5 | async-start | bytes 2097152 | tf_op jit(solution)/shard_map/all_to_all | solution.py:40
  148.4 6.7 %copy-start.15 = (bf16[512,512]{1,0:T(8,128)(2,1)S(1)}, bf16[512,512]{1,0:T(8,128)(2,1)}, u32[]{:S(2)}) copy-start(bf16[512,512]{1,0:T(8,128)(2,1)} %copy-done.14) | copy-start | bytes 1572868
  148.4 35.9 %all-to-all-start.6 = ((f32[64,1,4096]{2,1,0:T(1,128)}), f32[64,1,4096]{2,1,0:T(1,128)S(1)}, u32[]{:S(2)}, u32[]{:S(2)}) async-start(f32[64,1,4096]{2,1,0:T(1,128)} %broadcast_in_dim.17), calls=%async_computation.6 | async-start | bytes 2097152 | tf_op jit(solution)/shard_map/all_to_all | solution.py:46
  155.1 1.0 copy-start.13
  156.1 1.0 copy-start.11
  157.5 8.4 %collective-permute-start = (f32[256,128]{1,0:T(8,128)S(1)}, f32[256,128]{1,0:T(8,128)S(1)}, u32[]{:S(2)}, u32[]{:S(2)}) collective-permute-start(f32[256,128]{1,0:T(8,128)S(1)} %constant_dynamic-slice_fusion.2), channel_id=1, source_target_pairs={{0,4},{1,5},{2,6},{3,7},{4,0},{5,1},{6,2},{7,3},{8,12},{9,13},{10,... | collective-permute-start | bytes 393224 | tf_op jit(solution)/shard_map/ppermute | solution.py:81
  165.9 6.2 %collective-permute-start.1 = (f32[128,128]{1,0:T(8,128)S(1)}, f32[128,128]{1,0:T(8,128)S(1)}, u32[]{:S(2)}, u32[]{:S(2)}) collective-permute-start(f32[128,128]{1,0:T(8,128)S(1)} %constant_dynamic-slice_fusion.1), channel_id=1, source_target_pairs={{0,2},{1,3},{2,0},{3,1},{4,6},{5,7},{6,4},{7,5},{8,10},{9,11},{10,... | collective-permute-start | bytes 196616 | tf_op jit(solution)/shard_map/ppermute | solution.py:81
  172.1 3.1 %collective-permute-start.2 = (f32[64,128]{1,0:T(8,128)S(1)}, f32[64,128]{1,0:T(8,128)S(1)}, u32[]{:S(2)}, u32[]{:S(2)}) collective-permute-start(f32[64,128]{1,0:T(8,128)S(1)} %constant_dynamic-slice_fusion), channel_id=1, source_target_pairs={{0,1},{1,0},{2,3},{3,2},{4,5},{5,4},{6,7},{7,6},{8,9},{9,8},{10,11... | collective-permute-start | bytes 98312 | tf_op jit(solution)/shard_map/ppermute | solution.py:81
  (2 other events, 1.4 us)

commit v11 on v9

--- a/solution.py
+++ b/solution.py
@@ -32,8 +32,8 @@
 ROWS = ("slab", "lane")
 
 
-def across_slots(stack):
-    return lax.psum(lax.psum(stack, "core"), "chips")
+def across_slots(stack, chips):
+    return spread_sum(lax.psum(stack, "core"), "chips", chips)
 
 
 def exchange_sum(stack, axis, count):
@@ -109,7 +109,7 @@
     return jnp.concatenate([first, second])
 
 
-def local(count, inner, width_cols, queries, prototypes, potential, weights, capacity, cotangent):
+def local(count, inner, width_cols, chips, queries, prototypes, potential, weights, capacity, cotangent):
     qhat, qlen = unit_rows(queries)
     phat, plen = unit_rows(prototypes)
     wgt = weights.astype(jnp.float32)
@@ -135,7 +135,7 @@
         kern = kernel_tile(start)
         ztot = ztot + jnp.sum(kern, axis=1)
         kgsum = kgsum + jnp.sum(kern * coupling_tile(start), axis=1)
-    totals = across_slots(jnp.stack([ztot, kgsum]))
+    totals = across_slots(jnp.stack([ztot, kgsum]), chips)
     share = wgt / totals[0]
     pvec = share * totals[1]
     alpha_one = pvec / wgt
@@ -159,7 +159,7 @@
     for start in starts:
         plan = share[:, None] * kernel_tile(start)
         rowprod = rowprod + jnp.sum(plan * beta_one[start : start + width][None, :], axis=1)
-    rowprod = across_slots(rowprod[None, :])[0]
+    rowprod = across_slots(rowprod[None, :], chips)[0]
     alpha_two = (pvec - rowprod) / wgt
     t_parts = []
     for start in starts:
@@ -242,5 +242,5 @@
     grid = Mesh(mesh.devices.reshape(shape), ROWS + COLS)
     in_specs = (P(ROWS, None), P(COLS, None), P(COLS), P(ROWS), P(COLS), P(ROWS, None))
     out_specs = (P(ROWS + COLS, None), P(COLS, None))
-    body = functools.partial(local, rows, inner, cols)
+    body = functools.partial(local, rows, inner, cols, cols // cores)
     return jax.shard_map(body, mesh=grid, in_specs=in_specs, out_specs=out_specs, check_vma=False)

time: 184 us -> 182 us (0.989)
  blocking collectives: 80.6 us -> 78.7 us
    psum x4 -> x2, blocking collectives: 27.3 us -> 4.94 us  [across_slots(): return spread_sum(lax.psum(stack, 'core'), 'chips', chips)]
    all_to_all x4 -> x6, blocking collectives: 53.4 us -> 73.8 us  [spread_sum(): lax.all_to_all(copies, axis, 0, 0)]
    unnamed x43 -> x44, local copies, waits for them, and re-layouts: 6.39 us -> 6.37 us
where the time goes in v11:
time: 182 us; the launch traced here: 179 us
  blocking collectives  78.7 us (43%)
  waiting for transfers between devices  42.4 us (23%)
  starting transfers between devices  20 us (11%)
  other arithmetic  18.6 us (10%)
  matrix products  8.92 us (5%)
  local copies, waits for them, and re-layouts  8.9 us (5%)
    all_to_all x6, blocking collectives, spread_sum(): lax.all_to_all(copies, axis, 0, 0)  73.8 us
    all_to_all x1, waiting for transfers between devices, exchange_sum(): pieces = lax.all_to_all(stack.reshape(count, -1), axis, 0, 0)  26.3 us
    ppermute x3, waiting for transfers between devices, halving_scatter(): block = keep + lax.ppermute(send, axis, pairs)  9.09 us
    ppermute x3, starting transfers between devices, halving_scatter(): block = keep + lax.ppermute(send, axis, pairs)  8.36 us
    all_to_all x1, waiting for transfers between devices, exchange_gather(): return lax.all_to_all(copies, axis, 0, 0).reshape(shape)  6.95 us
    all_to_all x1, starting transfers between devices, exchange_gather(): return lax.all_to_all(copies, axis, 0, 0).reshape(shape)  6.64 us
    unnamed x44, local copies, waits for them, and re-layouts  6.37 us
    all_to_all x1, starting transfers between devices, exchange_sum(): pieces = lax.all_to_all(stack.reshape(count, -1), axis, 0, 0)  4.97 us
  transfers between devices with their start and end apart: 5, of which 5 were waited for; matrix products, arithmetic and copies ran while one was open for 1% of the time, Pallas kernels for 0%

profile of v11, /device:TPU:6, one launch (start us, length us, event | category | flops | bytes accessed | tf_op | source)
XLA Modules:
  0.0 178.7 jit_solution(18170068556114603163)
XLA Ops:
  1.4 1.4 fusion.12
  8.5 1.4 fusion.46
  10.5 2.5 %psum.16 = f32[1024]{0:T(1024)S(1)} all-reduce(f32[1024]{0:T(1024)S(1)} %bitcast.35), channel_id=1, replica_groups=mesh['slab'=8,'lane'=8,'chips'=4,'core'=2] {'core'}, use_global_device_ids=true, to_apply=%region_10.0 | all-reduce | flops 1024 | bytes 8192 | tf_op jit(solution)/shard_map/psum | solution.py:36
  13.0 11.5 %all_to_all.51 = f32[4,1,1024]{2,1,0:T(1,128)S(1)} all-to-all(f32[4,1,1024]{2,1,0:T(1,128)S(1)} %broadcast_in_dim.21), channel_id=1, replica_groups=mesh['slab'=8,'lane'=8,'chips'=4,'core'=2] {'chips'}, dimensions={0} | all-to-all | bytes 32768 | tf_op jit(solution)/shard_map/all_to_all | solution.py:51
  25.2 3.5 %multiply_reduce_fusion.20 = (f32[512]{0:T(512)S(1)}, f32[512]{0:T(512)S(1)}, f32[512]{0:T(512)S(1)}, f32[512]{0:T(512)S(1)}, f32[512]{0:T(512)S(1)}, /*index=5*...) fusion(f32[512,512]{1,0:T(8,128)S(1)} %get-tuple-element.61, ...), kind=kLoop, calls=%fused_computation.53 | loop fusion | flops 6285312 | bytes 8417280 | tf_op jit(solution)/shard_map/reduce_sum | solution.py:145
  29.0 16.4 %all_to_all.52 = f32[8,1,6144]{2,1,0:T(1,128)} all-to-all(f32[8,1,6144]{2,1,0:T(1,128)S(1)} %broadcast_in_dim.23), channel_id=1, replica_groups=mesh['slab'=8,'lane'=8,'chips'=4,'core'=2] {'lane'}, dimensions={0} | all-to-all | bytes 393216 | tf_op jit(solution)/shard_map/all_to_all | solution.py:51
  46.5 16.8 %all_to_all.53 = f32[8,1,6144]{2,1,0:T(1,128)} all-to-all(f32[8,1,6144]{2,1,0:T(1,128)S(1)} %broadcast_in_dim.24), channel_id=1, replica_groups=mesh['slab'=8,'lane'=8,'chips'=4,'core'=2] {'slab'}, dimensions={0} | all-to-all | bytes 393216 | tf_op jit(solution)/shard_map/all_to_all | solution.py:51
  64.4 1.8 %multiply_reduce_fusion.6 = (f32[512]{0:T(512)S(1)}, f32[512]{0:T(512)S(1)}, f32[512]{0:T(512)S(1)}, f32[512]{0:T(512)S(1)}) fusion(f32[512,512]{1,0:T(8,128)} %get-tuple-element.64, f32[512]{0:T(512)S(1)} %get-tuple-element.46, f32[512]{0:T(512)S(1)} %get-tuple-element.56, f32[512]{0:T(512)S(1)} %get-tuple-element.44, f32[512,512]{1,0:T(8,128)S(1)} %get-tuple-element.61, ...), kind=kLoop, calls=%fused_computation.38 | loop fusion | flops 3143680 | bytes 4212736 | tf_op jit(solution)/shard_map/reduce_sum | solution.py:161
  66.2 2.5 %psum.18 = f32[512]{0:T(512)S(1)} all-reduce(f32[512]{0:T(512)S(1)} %add_add_fusion), channel_id=1, replica_groups=mesh['slab'=8,'lane'=8,'chips'=4,'core'=2] {'core'}, use_global_device_ids=true, to_apply=%region_30.0 | all-reduce | flops 512 | bytes 4096 | tf_op jit(solution)/shard_map/psum | solution.py:36
  68.7 7.6 %all_to_all.54 = f32[4,1,512]{2,1,0:T(1,128)S(1)} all-to-all(f32[4,1,512]{2,1,0:T(1,128)S(1)} %broadcast_in_dim.25), channel_id=1, replica_groups=mesh['slab'=8,'lane'=8,'chips'=4,'core'=2] {'chips'}, dimensions={0} | all-to-all | bytes 16384 | tf_op jit(solution)/shard_map/all_to_all | solution.py:51
  76.4 1.7 multiply_reduce_fusion.3
  78.2 10.8 %all_to_all.55 = f32[8,1,2048]{2,1,0:T(1,128)S(1)} all-to-all(f32[8,1,2048]{2,1,0:T(1,128)S(1)} %broadcast_in_dim.26), channel_id=1, replica_groups=mesh['slab'=8,'lane'=8,'chips'=4,'core'=2] {'lane'}, dimensions={0} | all-to-all | bytes 131072 | tf_op jit(solution)/shard_map/all_to_all | solution.py:51
  89.0 10.8 %all_to_all.56 = f32[8,1,2048]{2,1,0:T(1,128)S(1)} all-to-all(f32[8,1,2048]{2,1,0:T(1,128)S(1)} %broadcast_in_dim.27), channel_id=1, replica_groups=mesh['slab'=8,'lane'=8,'chips'=4,'core'=2] {'slab'}, dimensions={0} | all-to-all | bytes 131072 | tf_op jit(solution)/shard_map/all_to_all | solution.py:51
  99.9 3.4 %multiply_convert_fusion = (bf16[512,512]{1,0:T(8,128)(2,1)S(1)}, bf16[512,512]{1,0:T(8,128)(2,1)S(1)}, bf16[512,512]{1,0:T(8,128)(2,1)S(1)}, bf16[512,512]{1,0:T(8,128)(2,1)S(1)}) fusion(f32[512,512]{1,0:T(8,128)} %copy-done.4, f32[512,512]{1,0:T(8,128)S(1)} %get-tuple-element.61, f32[512]{0:T(512)S(1)} %get-tuple-element.39, ...), kind=kLoop, calls=%fused_computation.28 | loop fusion | flops 6291456 | bytes 10498048 | tf_op jit(solution)/shard_map/convert_element_type | solution.py:176
  108.4 5.0 %all-to-all-start.6 = ((f32[64,1,4096]{2,1,0:T(1,128)}), f32[64,1,4096]{2,1,0:T(1,128)S(1)}, u32[]{:S(2)}, u32[]{:S(2)}) async-start(f32[64,1,4096]{2,1,0:T(1,128)} %bitcast.5), calls=%async_computation.6 | async-start | bytes 2097152 | tf_op jit(solution)/shard_map/all_to_all | solution.py:40
  113.8 26.3 %all-to-all-done.6 = f32[64,1,4096]{2,1,0:T(1,128)S(1)} async-done(((f32[64,1,4096]{2,1,0:T(1,128)}), f32[64,1,4096]{2,1,0:T(1,128)S(1)}, u32[]{:S(2)}, u32[]{:S(2)}) %all-to-all-start.6) | async-done | bytes 1048608 | tf_op jit(solution)/shard_map/all_to_all | solution.py:40
  141.2 2.0 %broadcast_in_dim.29 = f32[64,1,4096]{2,1,0:T(1,128)} broadcast(f32[4096]{0:T(1024)S(1)} %fusion.43), dimensions={2} | broadcast | bytes 1064960 | tf_op jit(solution)/shard_map/broadcast_in_dim | solution.py:45
  143.2 6.6 %all-to-all-start.7 = ((f32[64,1,4096]{2,1,0:T(1,128)}), f32[64,1,4096]{2,1,0:T(1,128)S(1)}, u32[]{:S(2)}, u32[]{:S(2)}) async-start(f32[64,1,4096]{2,1,0:T(1,128)} %broadcast_in_dim.29), calls=%async_computation.7 | async-start | bytes 2097152 | tf_op jit(solution)/shard_map/all_to_all | solution.py:46
  152.3 4.0 %collective-permute-start = (f32[256,128]{1,0:T(8,128)S(1)}, f32[256,128]{1,0:T(8,128)S(1)}, u32[]{:S(2)}, u32[]{:S(2)}) collective-permute-start(f32[256,128]{1,0:T(8,128)S(1)} %constant_dynamic-slice_fusion.2), channel_id=1, source_target_pairs={{0,4},{1,5},{2,6},{3,7},{4,0},{5,1},{6,2},{7,3},{8,12},{9,13},{10,... | collective-permute-start | bytes 393224 | tf_op jit(solution)/shard_map/ppermute | solution.py:78
  156.3 4.3 %collective-permute-done = f32[256,128]{1,0:T(8,128)S(1)} collective-permute-done((f32[256,128]{1,0:T(8,128)S(1)}, f32[256,128]{1,0:T(8,128)S(1)}, u32[]{:S(2)}, u32[]{:S(2)}) %collective-permute-start) | collective-permute-done | bytes 131104 | tf_op jit(solution)/shard_map/ppermute | solution.py:78
  160.7 2.5 %collective-permute-start.1 = (f32[128,128]{1,0:T(8,128)S(1)}, f32[128,128]{1,0:T(8,128)S(1)}, u32[]{:S(2)}, u32[]{:S(2)}) collective-permute-start(f32[128,128]{1,0:T(8,128)S(1)} %constant_dynamic-slice_fusion.1), channel_id=1, source_target_pairs={{0,2},{1,3},{2,0},{3,1},{4,6},{5,7},{6,4},{7,5},{8,10},{9,11},{10,... | collective-permute-start | bytes 196616 | tf_op jit(solution)/shard_map/ppermute | solution.py:78
  163.2 3.7 %collective-permute-done.1 = f32[128,128]{1,0:T(8,128)S(1)} collective-permute-done((f32[128,128]{1,0:T(8,128)S(1)}, f32[128,128]{1,0:T(8,128)S(1)}, u32[]{:S(2)}, u32[]{:S(2)}) %collective-permute-start.1) | collective-permute-done | bytes 65568 | tf_op jit(solution)/shard_map/ppermute | solution.py:78
  166.9 1.9 %collective-permute-start.2 = (f32[64,128]{1,0:T(8,128)S(1)}, f32[64,128]{1,0:T(8,128)S(1)}, u32[]{:S(2)}, u32[]{:S(2)}) collective-permute-start(f32[64,128]{1,0:T(8,128)S(1)} %constant_dynamic-slice_fusion), channel_id=1, source_target_pairs={{0,1},{1,0},{2,3},{3,2},{4,5},{5,4},{6,7},{7,6},{8,9},{9,8},{10,11... | collective-permute-start | bytes 98312 | tf_op jit(solution)/shard_map/ppermute | solution.py:78
  170.8 7.0 %all-to-all-done.7 = f32[64,1,4096]{2,1,0:T(1,128)S(1)} async-done(((f32[64,1,4096]{2,1,0:T(1,128)}), f32[64,1,4096]{2,1,0:T(1,128)S(1)}, u32[]{:S(2)}, u32[]{:S(2)}) %all-to-all-start.7) | async-done | bytes 1048608 | tf_op jit(solution)/shard_map/all_to_all | solution.py:46
  (112 shorter events, 22.2 us)
Async XLA Ops:
  0.6 2.2 %copy-start.16 = (bf16[2048,128]{1,0:T(8,128)(2,1)S(1)}, bf16[2048,128]{1,0:T(8,128)(2,1)}, u32[]{:S(2)}) copy-start(bf16[2048,128]{1,0:T(8,128)(2,1)} %param.7) | copy-start | bytes 1572868
  2.8 0.9 copy-start.7
  3.7 6.3 %copy-start.5 = (bf16[2048,128]{1,0:T(8,128)(2,1)}, bf16[2048,128]{1,0:T(8,128)(2,1)S(1)}, u32[]{:S(2)}) copy-start(bf16[2048,128]{1,0:T(8,128)(2,1)S(1)} %fusion.13) | copy-start | bytes 1572868
  4.1 5.9 %copy-start.1 = (f32[512,512]{1,0:T(8,128)}, f32[512,512]{1,0:T(8,128)S(1)}, u32[]{:S(2)}) copy-start(f32[512,512]{1,0:T(8,128)S(1)} %fusion.34) | copy-start | bytes 3145732
  4.4 4.1 %copy-start.2 = (f32[512,512]{1,0:T(8,128)}, f32[512,512]{1,0:T(8,128)S(1)}, u32[]{:S(2)}) copy-start(f32[512,512]{1,0:T(8,128)S(1)} %fusion.29) | copy-start | bytes 3145732
  4.8 3.2 %copy-start.3 = (f32[512,512]{1,0:T(8,128)}, f32[512,512]{1,0:T(8,128)S(1)}, u32[]{:S(2)}) copy-start(f32[512,512]{1,0:T(8,128)S(1)} %fusion.25) | copy-start | bytes 3145732
  4.8 1.0 copy-start.17
  5.9 2.1 %copy-start.4 = (f32[512,512]{1,0:T(8,128)}, f32[512,512]{1,0:T(8,128)S(1)}, u32[]{:S(2)}) copy-start(f32[512,512]{1,0:T(8,128)S(1)} %fusion.21) | copy-start | bytes 3145732
  5.9 0.7 copy-start.19
  103.3 0.9 copy-start.10
  103.3 1.0 copy-start.14
  103.3 2.4 %copy-start.12 = (bf16[512,512]{1,0:T(8,128)(2,1)}, bf16[512,512]{1,0:T(8,128)(2,1)S(1)}, u32[]{:S(2)}) copy-start(bf16[512,512]{1,0:T(8,128)(2,1)S(1)} %get-tuple-element.59) | copy-start | bytes 1572868
  103.3 3.3 %copy-start.8 = (bf16[512,512]{1,0:T(8,128)(2,1)}, bf16[512,512]{1,0:T(8,128)(2,1)S(1)}, u32[]{:S(2)}) copy-start(bf16[512,512]{1,0:T(8,128)(2,1)S(1)} %get-tuple-element.60) | copy-start | bytes 1572868
  103.6 1.6 copy-start
  108.4 5.1 %copy-start.6 = (bf16[2048,128]{1,0:T(8,128)(2,1)S(1)}, bf16[2048,128]{1,0:T(8,128)(2,1)}, u32[]{:S(2)}) copy-start(bf16[2048,128]{1,0:T(8,128)(2,1)} %copy-done.5) | copy-start | bytes 1572868
  108.4 5.1 %copy-start.9 = (bf16[512,512]{1,0:T(8,128)(2,1)S(1)}, bf16[512,512]{1,0:T(8,128)(2,1)}, u32[]{:S(2)}) copy-start(bf16[512,512]{1,0:T(8,128)(2,1)} %copy-done.8) | copy-start | bytes 1572868
  108.4 31.7 %all-to-all-start.6 = ((f32[64,1,4096]{2,1,0:T(1,128)}), f32[64,1,4096]{2,1,0:T(1,128)S(1)}, u32[]{:S(2)}, u32[]{:S(2)}) async-start(f32[64,1,4096]{2,1,0:T(1,128)} %bitcast.5), calls=%async_computation.6 | async-start | bytes 2097152 | tf_op jit(solution)/shard_map/all_to_all | solution.py:40
  143.2 6.7 %copy-start.15 = (bf16[512,512]{1,0:T(8,128)(2,1)S(1)}, bf16[512,512]{1,0:T(8,128)(2,1)}, u32[]{:S(2)}) copy-start(bf16[512,512]{1,0:T(8,128)(2,1)} %copy-done.14) | copy-start | bytes 1572868
  143.2 34.5 %all-to-all-start.7 = ((f32[64,1,4096]{2,1,0:T(1,128)}), f32[64,1,4096]{2,1,0:T(1,128)S(1)}, u32[]{:S(2)}, u32[]{:S(2)}) async-start(f32[64,1,4096]{2,1,0:T(1,128)} %broadcast_in_dim.29), calls=%async_computation.7 | async-start | bytes 2097152 | tf_op jit(solution)/shard_map/all_to_all | solution.py:46
  149.9 1.0 copy-start.13
  150.9 1.0 copy-start.11
  152.3 8.4 %collective-permute-start = (f32[256,128]{1,0:T(8,128)S(1)}, f32[256,128]{1,0:T(8,128)S(1)}, u32[]{:S(2)}, u32[]{:S(2)}) collective-permute-start(f32[256,128]{1,0:T(8,128)S(1)} %constant_dynamic-slice_fusion.2), channel_id=1, source_target_pairs={{0,4},{1,5},{2,6},{3,7},{4,0},{5,1},{6,2},{7,3},{8,12},{9,13},{10,... | collective-permute-start | bytes 393224 | tf_op jit(solution)/shard_map/ppermute | solution.py:78
  160.7 6.2 %collective-permute-start.1 = (f32[128,128]{1,0:T(8,128)S(1)}, f32[128,128]{1,0:T(8,128)S(1)}, u32[]{:S(2)}, u32[]{:S(2)}) collective-permute-start(f32[128,128]{1,0:T(8,128)S(1)} %constant_dynamic-slice_fusion.1), channel_id=1, source_target_pairs={{0,2},{1,3},{2,0},{3,1},{4,6},{5,7},{6,4},{7,5},{8,10},{9,11},{10,... | collective-permute-start | bytes 196616 | tf_op jit(solution)/shard_map/ppermute | solution.py:78
  166.9 3.1 %collective-permute-start.2 = (f32[64,128]{1,0:T(8,128)S(1)}, f32[64,128]{1,0:T(8,128)S(1)}, u32[]{:S(2)}, u32[]{:S(2)}) collective-permute-start(f32[64,128]{1,0:T(8,128)S(1)} %constant_dynamic-slice_fusion), channel_id=1, source_target_pairs={{0,1},{1,0},{2,3},{3,2},{4,5},{5,4},{6,7},{7,6},{8,9},{9,8},{10,11... | collective-permute-start | bytes 98312 | tf_op jit(solution)/shard_map/ppermute | solution.py:78
  (2 other events, 1.4 us)

commit v12 on v11

--- a/solution.py
+++ b/solution.py
@@ -143,18 +143,15 @@
     for start in starts:
         plan = share[:, None] * kernel_tile(start)
         col_parts.append(jnp.sum(plan, axis=0))
-        q_parts.append(jnp.sum(plan * coupling_tile(start), axis=0))
-    for start in starts:
-        plan = share[:, None] * kernel_tile(start)
-        t_parts.append(jnp.sum(alpha_one[:, None] * plan, axis=0))
+        q_parts.append(jnp.sum(plan * (coupling_tile(start) - alpha_one[:, None]), axis=0))
     summed = across_queries(
-        jnp.stack([jnp.concatenate(col_parts), jnp.concatenate(q_parts), jnp.concatenate(t_parts)]),
+        jnp.stack([jnp.concatenate(col_parts), jnp.concatenate(q_parts)]),
         count,
         inner,
         spread=True,
     )
-    colsum, qvec, t_one = (summed[0], summed[1], summed[2])
-    beta_one = (qvec - t_one) / colsum
+    colsum, first_gap = (summed[0], summed[1])
+    beta_one = first_gap / colsum
     rowprod = jnp.zeros((local_rows,), jnp.float32)
     for start in starts:
         plan = share[:, None] * kernel_tile(start)
@@ -164,9 +161,9 @@
     t_parts = []
     for start in starts:
         plan = share[:, None] * kernel_tile(start)
-        t_parts.append(jnp.sum(alpha_two[:, None] * plan, axis=0))
+        t_parts.append(jnp.sum((alpha_one - alpha_two)[:, None] * plan, axis=0))
     t_two = across_queries(jnp.concatenate(t_parts)[None, :], count, inner, spread=True)[0]
-    beta_two = (qvec - t_two) / colsum
+    beta_two = (first_gap + t_two) / colsum
     dqhat = jnp.zeros(qhat.shape, jnp.float32)
     dp_parts = []
     for start in starts:

time: 182 us -> 183 us (level)
  local copies, waits for them, and re-layouts: 8.9 us -> 12.6 us
    unnamed x44 -> x55, local copies, waits for them, and re-layouts: 6.37 us -> 8.07 us
  transfers between devices with their start and end apart: 5 -> 5, of which waited for: 5 -> 5; matrix products, arithmetic and copies ran while one was open for 1% -> 2% of each run, Pallas kernels for 0% -> 0%
where the time goes in v12:
time: 183 us; the launch traced here: 179 us
  blocking collectives  77.1 us (42%)
  waiting for transfers between devices  41.1 us (22%)
  starting transfers between devices  20 us (11%)
  other arithmetic  18.3 us (10%)
  local copies, waits for them, and re-layouts  12.6 us (7%)
  matrix products  8.9 us (5%)
    all_to_all x6, blocking collectives, spread_sum(): lax.all_to_all(copies, axis, 0, 0)  72.2 us
    all_to_all x1, waiting for transfers between devices, exchange_sum(): pieces = lax.all_to_all(stack.reshape(count, -1), axis, 0, 0)  25.7 us
    ppermute x3, waiting for transfers between devices, halving_scatter(): block = keep + lax.ppermute(send, axis, pairs)  8.42 us
    ppermute x3, starting transfers between devices, halving_scatter(): block = keep + lax.ppermute(send, axis, pairs)  8.36 us
    unnamed x55, local copies, waits for them, and re-layouts  8.07 us
    all_to_all x1, waiting for transfers between devices, exchange_gather(): return lax.all_to_all(copies, axis, 0, 0).reshape(shape)  6.97 us
    all_to_all x1, starting transfers between devices, exchange_gather(): return lax.all_to_all(copies, axis, 0, 0).reshape(shape)  6.64 us
    all_to_all x1, starting transfers between devices, exchange_sum(): pieces = lax.all_to_all(stack.reshape(count, -1), axis, 0, 0)  4.97 us
  transfers between devices with their start and end apart: 5, of which 5 were waited for; matrix products, arithmetic and copies ran while one was open for 2% of the time, Pallas kernels for 0%

profile of v12, /device:TPU:6, one launch (start us, length us, event | category | flops | bytes accessed | tf_op | source)
XLA Modules:
  0.0 179.2 jit_solution(9022213844548459288)
XLA Ops:
  1.4 1.4 fusion.12
  9.1 1.4 fusion.46
  10.5 2.5 %psum.16 = f32[1024]{0:T(1024)S(1)} all-reduce(f32[1024]{0:T(1024)S(1)} %bitcast.37), channel_id=1, replica_groups=mesh['slab'=8,'lane'=8,'chips'=4,'core'=2] {'core'}, use_global_device_ids=true, to_apply=%region_10.0 | all-reduce | flops 1024 | bytes 8192 | tf_op jit(solution)/shard_map/psum | solution.py:36
  13.0 11.5 %all_to_all.51 = f32[4,1,1024]{2,1,0:T(1,128)S(1)} all-to-all(f32[4,1,1024]{2,1,0:T(1,128)S(1)} %broadcast_in_dim.21), channel_id=1, replica_groups=mesh['slab'=8,'lane'=8,'chips'=4,'core'=2] {'chips'}, dimensions={0} | all-to-all | bytes 32768 | tf_op jit(solution)/shard_map/all_to_all | solution.py:51
  25.8 3.3 %multiply_reduce_fusion.16 = (f32[512]{0:T(512)S(1)}, f32[512]{0:T(512)S(1)}, f32[512]{0:T(512)S(1)}, f32[512]{0:T(512)S(1)}, f32[512]{0:T(512)S(1)}, /*index=5*/f32[512]{0:T(512)S(1)}, f32[512]{0:T(512)S(1)}, f32[512]{0:T(512)S(1)}) fusion(f32[512,512]{1,0:T(8,128)S(1)} %get-tuple-element.56, f32[512]{0:T(512)S(1)} %get-tuple-element.50, ...), kind=kLoop, calls=%fused_computation.49 | loop fusion | flops 5238784 | bytes 8409088 | tf_op jit(solution)/shard_map/reduce_sum | solution.py:145
  29.3 15.6 %all_to_all.52 = f32[8,1,4096]{2,1,0:T(1,128)S(1)} all-to-all(f32[8,1,4096]{2,1,0:T(1,128)S(1)} %broadcast_in_dim.23), channel_id=1, replica_groups=mesh['slab'=8,'lane'=8,'chips'=4,'core'=2] {'lane'}, dimensions={0} | all-to-all | bytes 262144 | tf_op jit(solution)/shard_map/all_to_all | solution.py:51
  46.4 16.0 %all_to_all.53 = f32[8,1,4096]{2,1,0:T(1,128)S(1)} all-to-all(f32[8,1,4096]{2,1,0:T(1,128)S(1)} %broadcast_in_dim.24), channel_id=1, replica_groups=mesh['slab'=8,'lane'=8,'chips'=4,'core'=2] {'slab'}, dimensions={0} | all-to-all | bytes 262144 | tf_op jit(solution)/shard_map/all_to_all | solution.py:51
  63.8 1.8 multiply_reduce_fusion.6
  65.6 2.5 %psum.18 = f32[512]{0:T(512)S(1)} all-reduce(f32[512]{0:T(512)S(1)} %add_add_fusion), channel_id=1, replica_groups=mesh['slab'=8,'lane'=8,'chips'=4,'core'=2] {'core'}, use_global_device_ids=true, to_apply=%region_26.0 | all-reduce | flops 512 | bytes 4096 | tf_op jit(solution)/shard_map/psum | solution.py:36
  68.1 7.6 %all_to_all.54 = f32[4,1,512]{2,1,0:T(1,128)S(1)} all-to-all(f32[4,1,512]{2,1,0:T(1,128)S(1)} %broadcast_in_dim.25), channel_id=1, replica_groups=mesh['slab'=8,'lane'=8,'chips'=4,'core'=2] {'chips'}, dimensions={0} | all-to-all | bytes 16384 | tf_op jit(solution)/shard_map/all_to_all | solution.py:51
  76.4 1.7 multiply_reduce_fusion.3
  78.2 10.8 %all_to_all.55 = f32[8,1,2048]{2,1,0:T(1,128)S(1)} all-to-all(f32[8,1,2048]{2,1,0:T(1,128)S(1)} %broadcast_in_dim.26), channel_id=1, replica_groups=mesh['slab'=8,'lane'=8,'chips'=4,'core'=2] {'lane'}, dimensions={0} | all-to-all | bytes 131072 | tf_op jit(solution)/shard_map/all_to_all | solution.py:51
  89.0 10.8 %all_to_all.56 = f32[8,1,2048]{2,1,0:T(1,128)S(1)} all-to-all(f32[8,1,2048]{2,1,0:T(1,128)S(1)} %broadcast_in_dim.27), channel_id=1, replica_groups=mesh['slab'=8,'lane'=8,'chips'=4,'core'=2] {'slab'}, dimensions={0} | all-to-all | bytes 131072 | tf_op jit(solution)/shard_map/all_to_all | solution.py:51
  100.5 3.4 %multiply_convert_fusion = (bf16[512,512]{1,0:T(8,128)(2,1)S(1)}, bf16[512,512]{1,0:T(8,128)(2,1)S(1)}, bf16[512,512]{1,0:T(8,128)(2,1)S(1)}, bf16[512,512]{1,0:T(8,128)(2,1)S(1)}) fusion(f32[512,512]{1,0:T(8,128)} %copy-done.4, f32[512,512]{1,0:T(8,128)S(1)} %get-tuple-element.56, f32[512]{0:T(512)S(1)} %get-tuple-element.34, f32[512]{0:T(512)S(1)} %get-tuple-element.33, ...), kind=kLoop, calls=%fused_computation.28 | loop fusion | flops 6291456 | bytes 10498048 | tf_op jit(solution)/shard_map/convert_element_type | solution.py:173
  108.9 5.0 %all-to-all-start.6 = ((f32[64,1,4096]{2,1,0:T(1,128)}), f32[64,1,4096]{2,1,0:T(1,128)S(1)}, u32[]{:S(2)}, u32[]{:S(2)}) async-start(f32[64,1,4096]{2,1,0:T(1,128)} %bitcast.4), calls=%async_computation.6 | async-start | bytes 2097152 | tf_op jit(solution)/shard_map/all_to_all | solution.py:40
  114.9 25.7 %all-to-all-done.6 = f32[64,1,4096]{2,1,0:T(1,128)S(1)} async-done(((f32[64,1,4096]{2,1,0:T(1,128)}), f32[64,1,4096]{2,1,0:T(1,128)S(1)}, u32[]{:S(2)}, u32[]{:S(2)}) %all-to-all-start.6) | async-done | bytes 1048608 | tf_op jit(solution)/shard_map/all_to_all | solution.py:40
  141.7 2.0 %broadcast_in_dim.29 = f32[64,1,4096]{2,1,0:T(1,128)} broadcast(f32[4096]{0:T(1024)S(1)} %fusion.43), dimensions={2} | broadcast | bytes 1064960 | tf_op jit(solution)/shard_map/broadcast_in_dim | solution.py:45
  143.7 6.6 %all-to-all-start.7 = ((f32[64,1,4096]{2,1,0:T(1,128)}), f32[64,1,4096]{2,1,0:T(1,128)S(1)}, u32[]{:S(2)}, u32[]{:S(2)}) async-start(f32[64,1,4096]{2,1,0:T(1,128)} %broadcast_in_dim.29), calls=%async_computation.7 | async-start | bytes 2097152 | tf_op jit(solution)/shard_map/all_to_all | solution.py:46
  152.7 4.0 %collective-permute-start = (f32[256,128]{1,0:T(8,128)S(1)}, f32[256,128]{1,0:T(8,128)S(1)}, u32[]{:S(2)}, u32[]{:S(2)}) collective-permute-start(f32[256,128]{1,0:T(8,128)S(1)} %constant_dynamic-slice_fusion.2), channel_id=1, source_target_pairs={{0,4},{1,5},{2,6},{3,7},{4,0},{5,1},{6,2},{7,3},{8,12},{9,13},{10,... | collective-permute-start | bytes 393224 | tf_op jit(solution)/shard_map/ppermute | solution.py:78
  156.8 4.3 %collective-permute-done = f32[256,128]{1,0:T(8,128)S(1)} collective-permute-done((f32[256,128]{1,0:T(8,128)S(1)}, f32[256,128]{1,0:T(8,128)S(1)}, u32[]{:S(2)}, u32[]{:S(2)}) %collective-permute-start) | collective-permute-done | bytes 131104 | tf_op jit(solution)/shard_map/ppermute | solution.py:78
  161.1 2.5 %collective-permute-start.1 = (f32[128,128]{1,0:T(8,128)S(1)}, f32[128,128]{1,0:T(8,128)S(1)}, u32[]{:S(2)}, u32[]{:S(2)}) collective-permute-start(f32[128,128]{1,0:T(8,128)S(1)} %constant_dynamic-slice_fusion.1), channel_id=1, source_target_pairs={{0,2},{1,3},{2,0},{3,1},{4,6},{5,7},{6,4},{7,5},{8,10},{9,11},{10,... | collective-permute-start | bytes 196616 | tf_op jit(solution)/shard_map/ppermute | solution.py:78
  163.6 3.7 %collective-permute-done.1 = f32[128,128]{1,0:T(8,128)S(1)} collective-permute-done((f32[128,128]{1,0:T(8,128)S(1)}, f32[128,128]{1,0:T(8,128)S(1)}, u32[]{:S(2)}, u32[]{:S(2)}) %collective-permute-start.1) | collective-permute-done | bytes 65568 | tf_op jit(solution)/shard_map/ppermute | solution.py:78
  167.3 1.9 %collective-permute-start.2 = (f32[64,128]{1,0:T(8,128)S(1)}, f32[64,128]{1,0:T(8,128)S(1)}, u32[]{:S(2)}, u32[]{:S(2)}) collective-permute-start(f32[64,128]{1,0:T(8,128)S(1)} %constant_dynamic-slice_fusion), channel_id=1, source_target_pairs={{0,1},{1,0},{2,3},{3,2},{4,5},{5,4},{6,7},{7,6},{8,9},{9,8},{10,11... | collective-permute-start | bytes 98312 | tf_op jit(solution)/shard_map/ppermute | solution.py:78
  171.2 7.0 %all-to-all-done.7 = f32[64,1,4096]{2,1,0:T(1,128)S(1)} async-done(((f32[64,1,4096]{2,1,0:T(1,128)}), f32[64,1,4096]{2,1,0:T(1,128)S(1)}, u32[]{:S(2)}, u32[]{:S(2)}) %all-to-all-start.7) | async-done | bytes 1048608 | tf_op jit(solution)/shard_map/all_to_all | solution.py:46
  (121 shorter events, 25.2 us)
Async XLA Ops:
  0.6 2.2 %copy-start.16 = (bf16[2048,128]{1,0:T(8,128)(2,1)S(1)}, bf16[2048,128]{1,0:T(8,128)(2,1)}, u32[]{:S(2)}) copy-start(bf16[2048,128]{1,0:T(8,128)(2,1)} %param.7) | copy-start | bytes 1572868
  2.8 0.9 copy-start.7
  3.7 5.4 %copy-start.5 = (bf16[2048,128]{1,0:T(8,128)(2,1)}, bf16[2048,128]{1,0:T(8,128)(2,1)S(1)}, u32[]{:S(2)}) copy-start(bf16[2048,128]{1,0:T(8,128)(2,1)S(1)} %fusion.13) | copy-start | bytes 1572868
  4.1 5.0 %copy-start.1 = (f32[512,512]{1,0:T(8,128)}, f32[512,512]{1,0:T(8,128)S(1)}, u32[]{:S(2)}) copy-start(f32[512,512]{1,0:T(8,128)S(1)} %fusion.34) | copy-start | bytes 3145732
  4.4 4.1 %copy-start.2 = (f32[512,512]{1,0:T(8,128)}, f32[512,512]{1,0:T(8,128)S(1)}, u32[]{:S(2)}) copy-start(f32[512,512]{1,0:T(8,128)S(1)} %fusion.29) | copy-start | bytes 3145732
  4.8 3.2 %copy-start.3 = (f32[512,512]{1,0:T(8,128)}, f32[512,512]{1,0:T(8,128)S(1)}, u32[]{:S(2)}) copy-start(f32[512,512]{1,0:T(8,128)S(1)} %fusion.25) | copy-start | bytes 3145732
  4.8 1.0 copy-start.17
  5.9 2.1 %copy-start.4 = (f32[512,512]{1,0:T(8,128)}, f32[512,512]{1,0:T(8,128)S(1)}, u32[]{:S(2)}) copy-start(f32[512,512]{1,0:T(8,128)S(1)} %fusion.21) | copy-start | bytes 3145732
  99.8 0.7 copy-start.18
  103.9 0.9 copy-start.10
  103.9 1.0 copy-start.12
  103.9 1.8 %copy-start.14 = (bf16[512,512]{1,0:T(8,128)(2,1)}, bf16[512,512]{1,0:T(8,128)(2,1)S(1)}, u32[]{:S(2)}) copy-start(bf16[512,512]{1,0:T(8,128)(2,1)S(1)} %get-tuple-element.54) | copy-start | bytes 1572868
  103.9 2.7 %copy-start.8 = (bf16[512,512]{1,0:T(8,128)(2,1)}, bf16[512,512]{1,0:T(8,128)(2,1)S(1)}, u32[]{:S(2)}) copy-start(bf16[512,512]{1,0:T(8,128)(2,1)S(1)} %get-tuple-element.55) | copy-start | bytes 1572868
  106.1 1.2 copy-start
  108.9 5.8 %copy-start.6 = (bf16[2048,128]{1,0:T(8,128)(2,1)S(1)}, bf16[2048,128]{1,0:T(8,128)(2,1)}, u32[]{:S(2)}) copy-start(bf16[2048,128]{1,0:T(8,128)(2,1)} %copy-done.5) | copy-start | bytes 1572868
  108.9 5.8 %copy-start.9 = (bf16[512,512]{1,0:T(8,128)(2,1)S(1)}, bf16[512,512]{1,0:T(8,128)(2,1)}, u32[]{:S(2)}) copy-start(bf16[512,512]{1,0:T(8,128)(2,1)} %copy-done.8) | copy-start | bytes 1572868
  108.9 31.7 %all-to-all-start.6 = ((f32[64,1,4096]{2,1,0:T(1,128)}), f32[64,1,4096]{2,1,0:T(1,128)S(1)}, u32[]{:S(2)}, u32[]{:S(2)}) async-start(f32[64,1,4096]{2,1,0:T(1,128)} %bitcast.4), calls=%async_computation.6 | async-start | bytes 2097152 | tf_op jit(solution)/shard_map/all_to_all | solution.py:40
  143.7 6.7 %copy-start.15 = (bf16[512,512]{1,0:T(8,128)(2,1)S(1)}, bf16[512,512]{1,0:T(8,128)(2,1)}, u32[]{:S(2)}) copy-start(bf16[512,512]{1,0:T(8,128)(2,1)} %copy-done.14) | copy-start | bytes 1572868
  143.7 34.6 %all-to-all-start.7 = ((f32[64,1,4096]{2,1,0:T(1,128)}), f32[64,1,4096]{2,1,0:T(1,128)S(1)}, u32[]{:S(2)}, u32[]{:S(2)}) async-start(f32[64,1,4096]{2,1,0:T(1,128)} %broadcast_in_dim.29), calls=%async_computation.7 | async-start | bytes 2097152 | tf_op jit(solution)/shard_map/all_to_all | solution.py:46
  150.3 1.0 copy-start.13
  151.4 1.0 copy-start.11
  152.7 8.4 %collective-permute-start = (f32[256,128]{1,0:T(8,128)S(1)}, f32[256,128]{1,0:T(8,128)S(1)}, u32[]{:S(2)}, u32[]{:S(2)}) collective-permute-start(f32[256,128]{1,0:T(8,128)S(1)} %constant_dynamic-slice_fusion.2), channel_id=1, source_target_pairs={{0,4},{1,5},{2,6},{3,7},{4,0},{5,1},{6,2},{7,3},{8,12},{9,13},{10,... | collective-permute-start | bytes 393224 | tf_op jit(solution)/shard_map/ppermute | solution.py:78
  161.1 6.2 %collective-permute-start.1 = (f32[128,128]{1,0:T(8,128)S(1)}, f32[128,128]{1,0:T(8,128)S(1)}, u32[]{:S(2)}, u32[]{:S(2)}) collective-permute-start(f32[128,128]{1,0:T(8,128)S(1)} %constant_dynamic-slice_fusion.1), channel_id=1, source_target_pairs={{0,2},{1,3},{2,0},{3,1},{4,6},{5,7},{6,4},{7,5},{8,10},{9,11},{10,... | collective-permute-start | bytes 196616 | tf_op jit(solution)/shard_map/ppermute | solution.py:78
  167.3 3.1 %collective-permute-start.2 = (f32[64,128]{1,0:T(8,128)S(1)}, f32[64,128]{1,0:T(8,128)S(1)}, u32[]{:S(2)}, u32[]{:S(2)}) collective-permute-start(f32[64,128]{1,0:T(8,128)S(1)} %constant_dynamic-slice_fusion), channel_id=1, source_target_pairs={{0,1},{1,0},{2,3},{3,2},{4,5},{5,4},{6,7},{7,6},{8,9},{9,8},{10,11... | collective-permute-start | bytes 98312 | tf_op jit(solution)/shard_map/ppermute | solution.py:78
  (7 other events, 4.6 us)

commit v13 on v11

--- a/solution.py
+++ b/solution.py
@@ -32,8 +32,8 @@
 ROWS = ("slab", "lane")
 
 
-def across_slots(stack, chips):
-    return spread_sum(lax.psum(stack, "core"), "chips", chips)
+def across_slots(stack, width):
+    return spread_sum(stack, COLS, width)
 
 
 def exchange_sum(stack, axis, count):
@@ -242,5 +242,5 @@
     grid = Mesh(mesh.devices.reshape(shape), ROWS + COLS)
     in_specs = (P(ROWS, None), P(COLS, None), P(COLS), P(ROWS), P(COLS), P(ROWS, None))
     out_specs = (P(ROWS + COLS, None), P(COLS, None))
-    body = functools.partial(local, rows, inner, cols, cols // cores)
+    body = functools.partial(local, rows, inner, cols, cols)
     return jax.shard_map(body, mesh=grid, in_specs=in_specs, out_specs=out_specs, check_vma=False)

time: 182 us -> 179 us (0.984)
  blocking collectives: 78.7 us -> 74.6 us
    psum x2 -> x0, blocking collectives: 4.94 us -> none  [across_slots(): return spread_sum(lax.psum(stack, 'core'), 'chips', chips)]
where the time goes in v13:
time: 179 us; the launch traced here: 176 us
  blocking collectives  74.6 us (42%)
  waiting for transfers between devices  43.5 us (24%)
  starting transfers between devices  19.9 us (11%)
  other arithmetic  18.6 us (10%)
  matrix products  8.91 us (5%)
  local copies, waits for them, and re-layouts  8.9 us (5%)
    all_to_all x6, blocking collectives, spread_sum(): lax.all_to_all(copies, axis, 0, 0)  74.6 us
    all_to_all x1, waiting for transfers between devices, exchange_sum(): pieces = lax.all_to_all(stack.reshape(count, -1), axis, 0, 0)  27.2 us
    ppermute x3, waiting for transfers between devices, halving_scatter(): block = keep + lax.ppermute(send, axis, pairs)  9.1 us
    ppermute x3, starting transfers between devices, halving_scatter(): block = keep + lax.ppermute(send, axis, pairs)  8.34 us
    all_to_all x1, waiting for transfers between devices, exchange_gather(): return lax.all_to_all(copies, axis, 0, 0).reshape(shape)  7.18 us
    all_to_all x1, starting transfers between devices, exchange_gather(): return lax.all_to_all(copies, axis, 0, 0).reshape(shape)  6.63 us
    unnamed x44, local copies, waits for them, and re-layouts  6.37 us
    all_to_all x1, starting transfers between devices, exchange_sum(): pieces = lax.all_to_all(stack.reshape(count, -1), axis, 0, 0)  4.97 us
  transfers between devices with their start and end apart: 5, of which 5 were waited for; matrix products, arithmetic and copies ran while one was open for 1% of the time, Pallas kernels for 0%

profile of v13, /device:TPU:6, one launch (start us, length us, event | category | flops | bytes accessed | tf_op | source)
XLA Modules:
  0.0 175.6 jit_solution(15194150900443017068)
XLA Ops:
  1.4 1.4 fusion.12
  8.5 1.4 fusion.46
  10.6 11.6 %all_to_all.51 = f32[8,1,1024]{2,1,0:T(1,128)S(1)} all-to-all(f32[8,1,1024]{2,1,0:T(1,128)S(1)} %broadcast_in_dim.21), channel_id=1, replica_groups=mesh['slab'=8,'lane'=8,'chips'=4,'core'=2] {'chips','core'}, dimensions={0} | all-to-all | bytes 65536 | tf_op jit(solution)/shard_map/all_to_all | solution.py:51
  22.8 3.5 %multiply_reduce_fusion.20 = (f32[512]{0:T(512)S(1)}, f32[512]{0:T(512)S(1)}, f32[512]{0:T(512)S(1)}, f32[512]{0:T(512)S(1)}, f32[512]{0:T(512)S(1)}, /*index=5*...) fusion(f32[512,512]{1,0:T(8,128)S(1)} %get-tuple-element.61, ...), kind=kLoop, calls=%fused_computation.53 | loop fusion | flops 6285312 | bytes 8417280 | tf_op jit(solution)/shard_map/reduce_sum | solution.py:145
  26.6 17.0 %all_to_all.52 = f32[8,1,6144]{2,1,0:T(1,128)} all-to-all(f32[8,1,6144]{2,1,0:T(1,128)S(1)} %broadcast_in_dim.23), channel_id=1, replica_groups=mesh['slab'=8,'lane'=8,'chips'=4,'core'=2] {'lane'}, dimensions={0} | all-to-all | bytes 393216 | tf_op jit(solution)/shard_map/all_to_all | solution.py:51
  43.6 1.1 reduce_sum.374
  44.8 16.8 %all_to_all.53 = f32[8,1,6144]{2,1,0:T(1,128)} all-to-all(f32[8,1,6144]{2,1,0:T(1,128)S(1)} %broadcast_in_dim.24), channel_id=1, replica_groups=mesh['slab'=8,'lane'=8,'chips'=4,'core'=2] {'slab'}, dimensions={0} | all-to-all | bytes 393216 | tf_op jit(solution)/shard_map/all_to_all | solution.py:51
  62.7 1.8 %multiply_reduce_fusion.6 = (f32[512]{0:T(512)S(1)}, f32[512]{0:T(512)S(1)}, f32[512]{0:T(512)S(1)}, f32[512]{0:T(512)S(1)}) fusion(f32[512,512]{1,0:T(8,128)} %get-tuple-element.64, f32[512]{0:T(512)S(1)} %get-tuple-element.46, f32[512]{0:T(512)S(1)} %get-tuple-element.56, f32[512]{0:T(512)S(1)} %get-tuple-element.44, f32[512,512]{1,0:T(8,128)S(1)} %get-tuple-element.61, ...), kind=kLoop, calls=%fused_computation.38 | loop fusion | flops 3143680 | bytes 4212736 | tf_op jit(solution)/shard_map/reduce_sum | solution.py:161
  64.5 7.7 %all_to_all.54 = f32[8,1,512]{2,1,0:T(1,128)S(1)} all-to-all(f32[8,1,512]{2,1,0:T(1,128)S(1)} %broadcast_in_dim.25), channel_id=1, replica_groups=mesh['slab'=8,'lane'=8,'chips'=4,'core'=2] {'chips','core'}, dimensions={0} | all-to-all | bytes 32768 | tf_op jit(solution)/shard_map/all_to_all | solution.py:51
  72.2 1.7 multiply_reduce_fusion.3
  74.0 10.8 %all_to_all.55 = f32[8,1,2048]{2,1,0:T(1,128)S(1)} all-to-all(f32[8,1,2048]{2,1,0:T(1,128)S(1)} %broadcast_in_dim.26), channel_id=1, replica_groups=mesh['slab'=8,'lane'=8,'chips'=4,'core'=2] {'lane'}, dimensions={0} | all-to-all | bytes 131072 | tf_op jit(solution)/shard_map/all_to_all | solution.py:51
  84.9 10.8 %all_to_all.56 = f32[8,1,2048]{2,1,0:T(1,128)S(1)} all-to-all(f32[8,1,2048]{2,1,0:T(1,128)S(1)} %broadcast_in_dim.27), channel_id=1, replica_groups=mesh['slab'=8,'lane'=8,'chips'=4,'core'=2] {'slab'}, dimensions={0} | all-to-all | bytes 131072 | tf_op jit(solution)/shard_map/all_to_all | solution.py:51
  95.7 3.4 %multiply_convert_fusion = (bf16[512,512]{1,0:T(8,128)(2,1)S(1)}, bf16[512,512]{1,0:T(8,128)(2,1)S(1)}, bf16[512,512]{1,0:T(8,128)(2,1)S(1)}, bf16[512,512]{1,0:T(8,128)(2,1)S(1)}) fusion(f32[512,512]{1,0:T(8,128)} %copy-done.4, f32[512,512]{1,0:T(8,128)S(1)} %get-tuple-element.61, f32[512]{0:T(512)S(1)} %get-tuple-element.39, ...), kind=kLoop, calls=%fused_computation.28 | loop fusion | flops 6291456 | bytes 10498048 | tf_op jit(solution)/shard_map/convert_element_type | solution.py:176
  104.3 5.0 %all-to-all-start.6 = ((f32[64,1,4096]{2,1,0:T(1,128)}), f32[64,1,4096]{2,1,0:T(1,128)S(1)}, u32[]{:S(2)}, u32[]{:S(2)}) async-start(f32[64,1,4096]{2,1,0:T(1,128)} %bitcast.5), calls=%async_computation.6 | async-start | bytes 2097152 | tf_op jit(solution)/shard_map/all_to_all | solution.py:40
  109.7 27.2 %all-to-all-done.6 = f32[64,1,4096]{2,1,0:T(1,128)S(1)} async-done(((f32[64,1,4096]{2,1,0:T(1,128)}), f32[64,1,4096]{2,1,0:T(1,128)S(1)}, u32[]{:S(2)}, u32[]{:S(2)}) %all-to-all-start.6) | async-done | bytes 1048608 | tf_op jit(solution)/shard_map/all_to_all | solution.py:40
  137.9 2.0 %broadcast_in_dim.29 = f32[64,1,4096]{2,1,0:T(1,128)} broadcast(f32[4096]{0:T(1024)S(1)} %fusion.43), dimensions={2} | broadcast | bytes 1064960 | tf_op jit(solution)/shard_map/broadcast_in_dim | solution.py:45
  139.9 6.6 %all-to-all-start.7 = ((f32[64,1,4096]{2,1,0:T(1,128)}), f32[64,1,4096]{2,1,0:T(1,128)S(1)}, u32[]{:S(2)}, u32[]{:S(2)}) async-start(f32[64,1,4096]{2,1,0:T(1,128)} %broadcast_in_dim.29), calls=%async_computation.7 | async-start | bytes 2097152 | tf_op jit(solution)/shard_map/all_to_all | solution.py:46
  148.9 4.0 %collective-permute-start = (f32[256,128]{1,0:T(8,128)S(1)}, f32[256,128]{1,0:T(8,128)S(1)}, u32[]{:S(2)}, u32[]{:S(2)}) collective-permute-start(f32[256,128]{1,0:T(8,128)S(1)} %constant_dynamic-slice_fusion.2), channel_id=1, source_target_pairs={{0,4},{1,5},{2,6},{3,7},{4,0},{5,1},{6,2},{7,3},{8,12},{9,13},{10,... | collective-permute-start | bytes 393224 | tf_op jit(solution)/shard_map/ppermute | solution.py:78
  153.0 4.3 %collective-permute-done = f32[256,128]{1,0:T(8,128)S(1)} collective-permute-done((f32[256,128]{1,0:T(8,128)S(1)}, f32[256,128]{1,0:T(8,128)S(1)}, u32[]{:S(2)}, u32[]{:S(2)}) %collective-permute-start) | collective-permute-done | bytes 131104 | tf_op jit(solution)/shard_map/ppermute | solution.py:78
  157.3 2.4 %collective-permute-start.1 = (f32[128,128]{1,0:T(8,128)S(1)}, f32[128,128]{1,0:T(8,128)S(1)}, u32[]{:S(2)}, u32[]{:S(2)}) collective-permute-start(f32[128,128]{1,0:T(8,128)S(1)} %constant_dynamic-slice_fusion.1), channel_id=1, source_target_pairs={{0,2},{1,3},{2,0},{3,1},{4,6},{5,7},{6,4},{7,5},{8,10},{9,11},{10,... | collective-permute-start | bytes 196616 | tf_op jit(solution)/shard_map/ppermute | solution.py:78
  159.8 3.7 %collective-permute-done.1 = f32[128,128]{1,0:T(8,128)S(1)} collective-permute-done((f32[128,128]{1,0:T(8,128)S(1)}, f32[128,128]{1,0:T(8,128)S(1)}, u32[]{:S(2)}, u32[]{:S(2)}) %collective-permute-start.1) | collective-permute-done | bytes 65568 | tf_op jit(solution)/shard_map/ppermute | solution.py:78
  163.5 1.9 %collective-permute-start.2 = (f32[64,128]{1,0:T(8,128)S(1)}, f32[64,128]{1,0:T(8,128)S(1)}, u32[]{:S(2)}, u32[]{:S(2)}) collective-permute-start(f32[64,128]{1,0:T(8,128)S(1)} %constant_dynamic-slice_fusion), channel_id=1, source_target_pairs={{0,1},{1,0},{2,3},{3,2},{4,5},{5,4},{6,7},{7,6},{8,9},{9,8},{10,11... | collective-permute-start | bytes 98312 | tf_op jit(solution)/shard_map/ppermute | solution.py:78
  165.6 1.1 collective-permute-done.2
  167.5 7.2 %all-to-all-done.7 = f32[64,1,4096]{2,1,0:T(1,128)S(1)} async-done(((f32[64,1,4096]{2,1,0:T(1,128)}), f32[64,1,4096]{2,1,0:T(1,128)S(1)}, u32[]{:S(2)}, u32[]{:S(2)}) %all-to-all-start.7) | async-done | bytes 1048608 | tf_op jit(solution)/shard_map/all_to_all | solution.py:46
  (110 shorter events, 20.1 us)
Async XLA Ops:
  0.6 2.2 %copy-start.16 = (bf16[2048,128]{1,0:T(8,128)(2,1)S(1)}, bf16[2048,128]{1,0:T(8,128)(2,1)}, u32[]{:S(2)}) copy-start(bf16[2048,128]{1,0:T(8,128)(2,1)} %param.7) | copy-start | bytes 1572868
  2.8 0.9 copy-start.7
  3.7 6.2 %copy-start.5 = (bf16[2048,128]{1,0:T(8,128)(2,1)}, bf16[2048,128]{1,0:T(8,128)(2,1)S(1)}, u32[]{:S(2)}) copy-start(bf16[2048,128]{1,0:T(8,128)(2,1)S(1)} %fusion.13) | copy-start | bytes 1572868
  4.1 5.9 %copy-start.1 = (f32[512,512]{1,0:T(8,128)}, f32[512,512]{1,0:T(8,128)S(1)}, u32[]{:S(2)}) copy-start(f32[512,512]{1,0:T(8,128)S(1)} %fusion.34) | copy-start | bytes 3145732
  4.4 4.1 %copy-start.2 = (f32[512,512]{1,0:T(8,128)}, f32[512,512]{1,0:T(8,128)S(1)}, u32[]{:S(2)}) copy-start(f32[512,512]{1,0:T(8,128)S(1)} %fusion.29) | copy-start | bytes 3145732
  4.8 3.2 %copy-start.3 = (f32[512,512]{1,0:T(8,128)}, f32[512,512]{1,0:T(8,128)S(1)}, u32[]{:S(2)}) copy-start(f32[512,512]{1,0:T(8,128)S(1)} %fusion.25) | copy-start | bytes 3145732
  4.8 1.0 copy-start.17
  5.9 2.1 %copy-start.4 = (f32[512,512]{1,0:T(8,128)}, f32[512,512]{1,0:T(8,128)S(1)}, u32[]{:S(2)}) copy-start(f32[512,512]{1,0:T(8,128)S(1)} %fusion.21) | copy-start | bytes 3145732
  5.9 0.7 copy-start.19
  99.1 0.9 copy-start.10
  99.1 1.0 copy-start.14
  99.1 2.4 %copy-start.12 = (bf16[512,512]{1,0:T(8,128)(2,1)}, bf16[512,512]{1,0:T(8,128)(2,1)S(1)}, u32[]{:S(2)}) copy-start(bf16[512,512]{1,0:T(8,128)(2,1)S(1)} %get-tuple-element.59) | copy-start | bytes 1572868
  99.1 3.3 %copy-start.8 = (bf16[512,512]{1,0:T(8,128)(2,1)}, bf16[512,512]{1,0:T(8,128)(2,1)S(1)}, u32[]{:S(2)}) copy-start(bf16[512,512]{1,0:T(8,128)(2,1)S(1)} %get-tuple-element.60) | copy-start | bytes 1572868
  99.5 1.6 copy-start
  104.3 5.1 %copy-start.6 = (bf16[2048,128]{1,0:T(8,128)(2,1)S(1)}, bf16[2048,128]{1,0:T(8,128)(2,1)}, u32[]{:S(2)}) copy-start(bf16[2048,128]{1,0:T(8,128)(2,1)} %copy-done.5) | copy-start | bytes 1572868
  104.3 5.1 %copy-start.9 = (bf16[512,512]{1,0:T(8,128)(2,1)S(1)}, bf16[512,512]{1,0:T(8,128)(2,1)}, u32[]{:S(2)}) copy-start(bf16[512,512]{1,0:T(8,128)(2,1)} %copy-done.8) | copy-start | bytes 1572868
  104.3 32.6 %all-to-all-start.6 = ((f32[64,1,4096]{2,1,0:T(1,128)}), f32[64,1,4096]{2,1,0:T(1,128)S(1)}, u32[]{:S(2)}, u32[]{:S(2)}) async-start(f32[64,1,4096]{2,1,0:T(1,128)} %bitcast.5), calls=%async_computation.6 | async-start | bytes 2097152 | tf_op jit(solution)/shard_map/all_to_all | solution.py:40
  139.9 6.6 %copy-start.15 = (bf16[512,512]{1,0:T(8,128)(2,1)S(1)}, bf16[512,512]{1,0:T(8,128)(2,1)}, u32[]{:S(2)}) copy-start(bf16[512,512]{1,0:T(8,128)(2,1)} %copy-done.14) | copy-start | bytes 1572868
  139.9 34.8 %all-to-all-start.7 = ((f32[64,1,4096]{2,1,0:T(1,128)}), f32[64,1,4096]{2,1,0:T(1,128)S(1)}, u32[]{:S(2)}, u32[]{:S(2)}) async-start(f32[64,1,4096]{2,1,0:T(1,128)} %broadcast_in_dim.29), calls=%async_computation.7 | async-start | bytes 2097152 | tf_op jit(solution)/shard_map/all_to_all | solution.py:46
  146.5 1.0 copy-start.13
  147.6 1.0 copy-start.11
  148.9 8.4 %collective-permute-start = (f32[256,128]{1,0:T(8,128)S(1)}, f32[256,128]{1,0:T(8,128)S(1)}, u32[]{:S(2)}, u32[]{:S(2)}) collective-permute-start(f32[256,128]{1,0:T(8,128)S(1)} %constant_dynamic-slice_fusion.2), channel_id=1, source_target_pairs={{0,4},{1,5},{2,6},{3,7},{4,0},{5,1},{6,2},{7,3},{8,12},{9,13},{10,... | collective-permute-start | bytes 393224 | tf_op jit(solution)/shard_map/ppermute | solution.py:78
  157.3 6.2 %collective-permute-start.1 = (f32[128,128]{1,0:T(8,128)S(1)}, f32[128,128]{1,0:T(8,128)S(1)}, u32[]{:S(2)}, u32[]{:S(2)}) collective-permute-start(f32[128,128]{1,0:T(8,128)S(1)} %constant_dynamic-slice_fusion.1), channel_id=1, source_target_pairs={{0,2},{1,3},{2,0},{3,1},{4,6},{5,7},{6,4},{7,5},{8,10},{9,11},{10,... | collective-permute-start | bytes 196616 | tf_op jit(solution)/shard_map/ppermute | solution.py:78
  163.5 3.1 %collective-permute-start.2 = (f32[64,128]{1,0:T(8,128)S(1)}, f32[64,128]{1,0:T(8,128)S(1)}, u32[]{:S(2)}, u32[]{:S(2)}) collective-permute-start(f32[64,128]{1,0:T(8,128)S(1)} %constant_dynamic-slice_fusion), channel_id=1, source_target_pairs={{0,1},{1,0},{2,3},{3,2},{4,5},{5,4},{6,7},{7,6},{8,9},{9,8},{10,11... | collective-permute-start | bytes 98312 | tf_op jit(solution)/shard_map/ppermute | solution.py:78
  (2 other events, 1.4 us)
